TPU v7x, 128 devices: a whole 4x4x4 slice. The times are simulated.
128 devices in a mesh: row: 8 (over z, core), col: 16 (over x, y).
Axes of the slice: x: 4, y: 4, z: 4, core: 2. Of those that a mesh axis runs over, the one named last changes fastest.
Arguments:
- logarithmic_conductivity: float32 [64, 512, 2048], P(None, 'row', 'col'), may hold values from -0.6 to 0.6
- starting_head: bfloat16 [64, 512, 2048], P(None, 'row', 'col'), may hold values from -4 to 4
- recharge: float32 [512, 2048], P('row', 'col'), may hold values from -4 to 4
- well_cells: int32 [4, 256], replicated, may hold values from 0 to 8191
- well_owner: int32 [4], replicated, may hold values from 0 to 127
- observed: float32 [1024], replicated, may hold values from -4 to 4
- obs_var: float32 [1024], replicated, may hold values from 0.25 to 4
- perturb: float32 [64, 1024], replicated, may hold values from -4 to 4
Outputs:
- pressure_out: bfloat16 [64, 512, 2048], P(None, 'row', 'col')
- predicted: float32 [64, 1024], replicated
- updated_perm: float32 [64, 512, 2048], P(None, 'row', 'col')
Inputs may be any that keep to these rules, and one draw needn't show every extreme that they name: Well k of group g is the cell well_cells[g, k] (row-major) of the tile of device well_owner[g]; wells may repeat. `well_owner`: devices are numbered row index * the size of col + col index; groups may share an owner.
All inputs are finite; a program needn't handle non-finite values.
Results may differ from a plain program's by a relative error of at most 0.001.
Values sent between devices are 32-bit elements; how exact they have to be, the bound alone decides.
No kernel may reach another device: no remote copies, remote signals or barrier semaphores. Data moves between devices by JAX's collectives and lax.ppermute only.
A program may use at most 128 MiB of HBM per device.

v0:
```python
import math

import jax
import jax.numpy as jnp
from jax import lax
from jax.sharding import PartitionSpec as P
from jax.experimental import pallas as pl
from jax.experimental.pallas import tpu as pltpu

STEPS = 3


time_step = 0.13


def send(piece, axis, forward):
    count = lax.axis_size(axis)
    pairs = [(i, i + 1) for i in range(count - 1)]
    if not forward:
        pairs = [(target, source) for source, target in pairs]
    return lax.ppermute(piece, axis, pairs)


def circular_inside(axis, local, width, size):
    index = jnp.arange(size)
    gap = (index >= local + width) & (index < size - width)
    local_index = jnp.where(index < local + width, index, index - size)
    global_index = lax.axis_index(axis) * local + local_index
    return (~gap) & (global_index >= 0) & (global_index < local * lax.axis_size(axis))


def stencil_kernel(mask_ref, source_ref, source_rows_ref, source_cols_ref, perm_ref, head_ref,
                   perm_rows_ref, head_rows_ref, perm_cols_ref, head_cols_ref, out16_ref, out32_ref):
    rows, cols = perm_ref.shape[1], perm_ref.shape[2]
    ext_rows, ext_cols = rows + 8, 2 * cols

    def extend(interior, halo_rows, halo_cols):
        return jnp.concatenate([jnp.concatenate([interior, halo_rows], axis=0), halo_cols], axis=1)

    inside = mask_ref[...] > 0.5
    source = extend(source_ref[...], source_rows_ref[0], source_cols_ref[0])

    def member(j, carry):
        perm = extend(perm_ref[j], perm_rows_ref[j], perm_cols_ref[j])
        head = extend(head_ref[j].astype(jnp.float32), head_rows_ref[j], head_cols_ref[j])
        vertical = jnp.exp(0.5 * (perm + pltpu.roll(perm, ext_rows - 1, 0)))
        horizontal = jnp.exp(0.5 * (perm + pltpu.roll(perm, ext_cols - 1, 1)))
        faces = (pltpu.roll(vertical, 1, 0), vertical, pltpu.roll(horizontal, 1, 1), horizontal)
        for _ in range(STEPS):
            near = (pltpu.roll(head, 1, 0), pltpu.roll(head, ext_rows - 1, 0),
                    pltpu.roll(head, 1, 1), pltpu.roll(head, ext_cols - 1, 1))
            flux_total = jnp.zeros_like(head)
            for weight_face, near_press in zip(faces, near):
                flux_total = flux_total + weight_face * (near_press - head)
            head = head + time_step * (flux_total + source)
            head = jnp.where(inside, head, 0.0)
        final = head[:rows, :cols]
        out32_ref[j] = final
        out16_ref[j] = final.astype(jnp.bfloat16)
        return carry

    lax.fori_loop(0, perm_ref.shape[0], member, 0)


def run_stencil(mask, source, halo_rows, halo_cols, perm, head, block):
    members, rows, cols = perm.shape
    blocks = members // block
    full2 = lambda shape: pl.BlockSpec(shape, lambda i: (0, 0))
    member_block = lambda shape, shift: pl.BlockSpec((block,) + shape, lambda i: (i + shift, 0, 0))
    last = lambda shape: pl.BlockSpec((1,) + shape, lambda i: (2 * members, 0, 0))
    ext_rows = rows + 8
    cells = members * ext_rows * 2 * cols
    return pl.pallas_call(
        stencil_kernel,
        grid=(blocks,),
        in_specs=[
            full2(mask.shape),
            full2(source.shape),
            last((8, cols)),
            last((ext_rows, cols)),
            member_block((rows, cols), 0),
            member_block((rows, cols), 0),
            member_block((8, cols), 0),
            member_block((8, cols), blocks),
            member_block((ext_rows, cols), 0),
            member_block((ext_rows, cols), blocks),
        ],
        out_specs=[member_block((rows, cols), 0), member_block((rows, cols), 0)],
        out_shape=[
            jax.ShapeDtypeStruct(perm.shape, jnp.bfloat16),
            jax.ShapeDtypeStruct(perm.shape, jnp.float32),
        ],
        cost_estimate=pl.CostEstimate(
            flops=cells * 80, transcendentals=cells * 2, bytes_accessed=members * rows * cols * 14
        ),
    )(mask, source, halo_rows, halo_cols, perm, head, halo_rows, halo_rows, halo_cols, halo_cols)


def butterfly(value, axis):
    count = lax.axis_size(axis)
    step = 1
    while step < count:
        value = value + lax.ppermute(value, axis, [(i, i ^ step) for i in range(count)])
        step *= 2
    return value


def neighbours(padded):
    return (padded[:, :-2, 1:-1], padded[:, 2:, 1:-1], padded[:, 1:-1, :-2], padded[:, 1:-1, 2:])


def face_terms(padded_perm):
    centre_perm = padded_perm[:, 1:-1, 1:-1]
    return [jnp.exp(0.5 * (centre_perm + near_perm)) for near_perm in neighbours(padded_perm)]


def advance(coefficients, bordered_head, source):
    centre_press = bordered_head[:, 1:-1, 1:-1]
    flux_total = jnp.zeros_like(centre_press)
    for weight_face, near_press in zip(coefficients, neighbours(bordered_head)):
        flux_total = flux_total + weight_face * (near_press - centre_press)
    return centre_press + time_step * (flux_total + source)


def blending_weights(predicted, observed, obs_var, perturb):
    member_count = predicted.shape[0]
    ensemble_spread = math.sqrt(member_count - 1)
    centred = (predicted - jnp.mean(predicted, axis=0, keepdims=True)) / ensemble_spread
    innovation = observed[None, :] + jnp.sqrt(obs_var)[None, :] * perturb - predicted
    weighted = centred / obs_var[None, :]
    system = jnp.eye(member_count, dtype=centred.dtype) + jnp.dot(
        weighted, centred.T, precision=lax.Precision.HIGHEST
    )
    right_side = jnp.dot(weighted, innovation.T, precision=lax.Precision.HIGHEST)
    factor = jnp.linalg.cholesky(system)
    half_solved = lax.linalg.triangular_solve(factor, right_side, left_side=True, lower=True)
    return lax.linalg.triangular_solve(
        factor, half_solved, left_side=True, lower=True, transpose_a=True
    )


def per_device(
    logarithmic_conductivity,
    starting_head,
    recharge,
    well_cells,
    well_owner,
    observed,
    obs_var,
    perturb,
):
    member_count, row_count, col_count = logarithmic_conductivity.shape
    width = STEPS
    ext_rows, ext_cols = row_count + 8, 2 * col_count
    f32 = jnp.float32

    def stack_rows(lo, hi):
        return jnp.concatenate(
            [logarithmic_conductivity[:, lo:hi], starting_head[:, lo:hi].astype(f32), recharge[None, lo:hi]], axis=0
        )

    top_rows = jnp.moveaxis(stack_rows(0, width), 1, 0)
    bottom_rows = jnp.moveaxis(stack_rows(row_count - width, row_count), 1, 0)
    from_above = jnp.moveaxis(send(bottom_rows, "row", True), 0, 1)
    from_below = jnp.moveaxis(send(top_rows, "row", False), 0, 1)
    stacked_total = from_above.shape[0]
    halo_rows = jnp.concatenate(
        [from_below, jnp.zeros((stacked_total, 8 - 2 * width, col_count), f32), from_above], axis=1
    )

    def stack_cols(lo, hi):
        interior = jnp.concatenate(
            [logarithmic_conductivity[:, :, lo:hi], starting_head[:, :, lo:hi].astype(f32), recharge[None, :, lo:hi]],
            axis=0,
        )
        return jnp.moveaxis(jnp.concatenate([interior, halo_rows[:, :, lo:hi]], axis=1), 2, 0)

    from_left = jnp.moveaxis(send(stack_cols(col_count - width, col_count), "col", True), 0, 2)
    from_right = jnp.moveaxis(send(stack_cols(0, width), "col", False), 0, 2)
    halo_cols = jnp.concatenate(
        [from_right, jnp.zeros((stacked_total, ext_rows, col_count - 2 * width), f32), from_left], axis=2
    )
    inside = circular_inside("row", row_count, width, ext_rows)[:, None] & circular_inside(
        "col", col_count, width, ext_cols
    )[None, :]
    pressure_low, hydraulic_head = run_stencil(
        inside.astype(f32), recharge, halo_rows, halo_cols, logarithmic_conductivity, starting_head, 8
    )
    flat_press = hydraulic_head.reshape(member_count, row_count * col_count)
    group_total, well_count = well_cells.shape
    local_data = jnp.take(flat_press, well_cells.reshape(-1), axis=1)
    me = lax.axis_index("row") * lax.axis_size("col") + lax.axis_index("col")
    mine = jnp.repeat(well_owner == me, well_count)
    local_data = jnp.where(mine[None, :], local_data, 0.0)
    packed = local_data.reshape(-1, 128)
    predicted = butterfly(butterfly(packed, "col"), "row").reshape(local_data.shape)
    mixing = blending_weights(predicted, observed, obs_var, perturb)
    ensemble_spread = math.sqrt(member_count - 1)
    anomalies = (
        logarithmic_conductivity - jnp.mean(logarithmic_conductivity, axis=0, keepdims=True)
    ) / ensemble_spread
    updated_perm = logarithmic_conductivity + jnp.einsum(
        "mrc,mn->nrc", anomalies, mixing, precision=lax.Precision.HIGHEST
    )
    return (pressure_low, predicted, updated_perm)


def solution(mesh):
    return jax.shard_map(
        per_device,
        mesh=mesh,
        in_specs=(
            P(None, "row", "col"),
            P(None, "row", "col"),
            P("row", "col"),
            P(),
            P(),
            P(),
            P(),
            P(),
        ),
        out_specs=(P(None, "row", "col"), P(), P(None, "row", "col")),
        check_vma=False,
    )
```

profile of v0, /device:TPU:1, one launch (start us, length us, event | category | flops | bytes accessed | tf_op | source)
XLA Modules:
  0.0 162.2 jit_solution(3333287576093301605)
XLA Ops:
  0.6 1.1 fusion.29
  1.7 1.0 slice_convert_fusion.1
  2.7 0.7 slice_bitcast_fusion.3
  3.4 0.8 maximum_bitcast_fusion
  4.2 3.3 %collective-permute-start = (f32[3,129,128]{2,0,1:T(4,128)}, f32[3,129,128]{2,0,1:T(4,128)}, u32[]{:S(2)}, u32[]{:S(2)}) collective-permute-start(f32[3,129,128]{2,0,1:T(4,128)} %maximum_bitcast_fusion), channel_id=1, source_target_pairs={{16,0},{32,16},{48,32},{64,48},{80,64},{96,80},{112,96},{17,1},{33... | collective-permute-start | bytes 594440 | tf_op jit(solution)/shard_map/ppermute | solution.py:21
  7.5 0.8 maximum_bitcast_fusion.1
  8.3 3.7 %collective-permute-start.1 = (f32[3,129,128]{2,0,1:T(4,128)}, f32[3,129,128]{2,0,1:T(4,128)}, u32[]{:S(2)}, u32[]{:S(2)}) collective-permute-start(f32[3,129,128]{2,0,1:T(4,128)} %maximum_bitcast_fusion.1), channel_id=1, source_target_pairs={{0,16},{16,32},{32,48},{48,64},{64,80},{80,96},{96,112},{1,17},{17... | collective-permute-start | bytes 594440 | tf_op jit(solution)/shard_map/ppermute | solution.py:21
  11.9 4.3 %fusion.28 = (f32[64,64,3]{2,1,0:T(8,128)S(1)}, f32[64,64,3]{2,1,0:T(8,128)}) fusion(f32[64,64,128]{2,1,0:T(8,128)} %perm_ref.1), kind=kLoop, calls=%fused_computation.63 | loop fusion | bytes 196608 | tf_op jit(solution)/shard_map/slice | solution.py:173
  16.2 1.5 fusion.30
  17.8 2.3 %copy.89 = f32[64,64,3]{1,0,2:T(8,128)S(1)} copy(f32[64,64,3]{2,1,0:T(8,128)} %get-tuple-element.25) | data formatting | bytes 98304
  20.1 1.7 %copy.90 = bf16[64,64,3]{1,0,2:T(8,128)(2,1)S(1)} copy(bf16[64,64,3]{2,1,0:T(8,128)(2,1)} %get-tuple-element.29) | data formatting | bytes 49152
  21.9 0.7 copy.87
  22.6 0.5 copy.88
  23.4 0.7 and_convert_fusion.mask_ref
  24.1 1.2 pad_maximum_fusion.1.source_rows_ref.perm_rows_ref.head_rows_ref
  25.5 0.9 copy.72
  26.5 3.2 %collective-permute-start.3 = (f32[3,129,72]{2,1,0:T(8,128)S(1)}, f32[3,129,72]{2,1,0:T(8,128)S(1)}, u32[]{:S(2)}, u32[]{:S(2)}) collective-permute-start(f32[3,129,72]{2,1,0:T(8,128)S(1)} %maximum_bitcast_fusion.3), channel_id=1, source_target_pairs={{0,1},{1,2},{2,3},{3,4},{4,5},{5,6},{6,7},{7,8},{8,9},{9,10},{10,1... | collective-permute-start | bytes 334376 | tf_op jit(solution)/shard_map/ppermute | solution.py:21
  29.8 0.9 copy.66
  30.8 1.3 collective-permute-start.2
  32.5 2.1 %collective-permute-done.3 = f32[3,129,72]{2,1,0:T(8,128)S(1)} collective-permute-done((f32[3,129,72]{2,1,0:T(8,128)S(1)}, f32[3,129,72]{2,1,0:T(8,128)S(1)}, u32[]{:S(2)}, u32[]{:S(2)}) %collective-permute-start.3) | collective-permute-done | bytes 111488 | tf_op jit(solution)/shard_map/ppermute | solution.py:21
  34.6 3.2 %copy.73 = f32[3,129,72]{0,2,1:T(8,128)} copy(f32[3,129,72]{2,1,0:T(8,128)S(1)} %collective-permute-done.3) | data formatting | bytes 222912 | tf_op jit(solution)/shard_map/ppermute | solution.py:21
  37.8 1.7 %collective-permute-done.2 = f32[3,129,72]{2,1,0:T(8,128)S(1)} collective-permute-done((f32[3,129,72]{2,1,0:T(8,128)S(1)}, f32[3,129,72]{2,1,0:T(8,128)S(1)}, u32[]{:S(2)}, u32[]{:S(2)}) %collective-permute-start.2) | collective-permute-done | bytes 111488 | tf_op jit(solution)/shard_map/ppermute | solution.py:21
  39.5 3.2 %copy.67 = f32[3,129,72]{0,2,1:T(8,128)} copy(f32[3,129,72]{2,1,0:T(8,128)S(1)} %collective-permute-done.2) | data formatting | bytes 222912 | tf_op jit(solution)/shard_map/ppermute | solution.py:21
  42.6 7.2 %pad_maximum_fusion.source_cols_ref.perm_cols_ref.head_cols_ref = f32[129,72,128]{2,1,0:T(8,128)} fusion(f32[129,72,3]{2,1,0:T(8,128)} %bitcast.59, f32[129,72,3]{2,1,0:T(8,128)} %bitcast.60, f32[128]{0:T(128)S(1)} %pad.1.clone), kind=kLoop, calls=%fused_computation.1 | loop fusion | flops 2377728 | bytes 4978880 | tf_op jit(solution)/shard_map/concatenate | solution.py:180
  49.9 28.0 %shard_map.103 = (bf16[64,64,128]{2,1,0:T(8,128)(2,1)}, f32[64,64,128]{2,1,0:T(8,128)}) custom-call(f32[72,256]{1,0:T(8,128)} %and_convert_fusion.mask_ref, f32[64,128]{1,0:T(8,128)} %source_ref.1, f32[129,8,128]{2,1,0:T(8,128)} %copy-done.1, f32[129,72,128]{2,1,0:T(8,128)} %pad_maximum_fusion.source_cols_ref.perm_cols_ref.head_cols_ref, ...), custom_call_target="tpu_custom_call" | custom-call | flops 94371840 | bytes 7340032 | tf_op jit(solution)/shard_map/pallas_call | solution.py:73
  77.9 3.8 %copy.86 = f32[64,64,128]{0,2,1:T(8,128)} copy(f32[64,64,128]{2,1,0:T(8,128)} %get-tuple-element.6) | data formatting | bytes 4194304 | tf_op jit(solution)/shard_map/reshape | solution.py:189
  81.7 5.0 %gather_fusion = f32[1024,64]{1,0:T(8,128)S(1)} fusion(f32[64,8192]{0,1:T(8,128)} %bitcast.61, s32[1024]{0:T(1024)S(1)} %broadcast_clamp_fusion), kind=kCustom, calls=%fused_computation | custom fusion | bytes 528384 | tf_op jit(solution)/shard_map/jit(_take)/gather | solution.py:191
  87.1 1.4 collective-permute-start.4
  88.5 5.8 %collective-permute-done.4 = f32[512,128]{1,0:T(8,128)S(1)} collective-permute-done((f32[512,128]{1,0:T(8,128)S(1)}, f32[512,128]{1,0:T(8,128)S(1)}, u32[]{:S(2)}, u32[]{:S(2)}) %collective-permute-start.4) | collective-permute-done | bytes 262176 | tf_op jit(solution)/shard_map/ppermute | solution.py:103
  94.3 4.5 %collective-permute-start.5 = (f32[512,128]{1,0:T(8,128)S(1)}, f32[512,128]{1,0:T(8,128)S(1)}, u32[]{:S(2)}, u32[]{:S(2)}) collective-permute-start(f32[512,128]{1,0:T(8,128)S(1)} %add.115), channel_id=1, source_target_pairs={{0,2},{1,3},{2,0},{3,1},{4,6},{5,7},{6,4},{7,5},{8,10},{9,11},{10,... | collective-permute-start | bytes 786440 | tf_op jit(solution)/shard_map/ppermute | solution.py:103
  98.8 5.3 %collective-permute-done.5 = f32[512,128]{1,0:T(8,128)S(1)} collective-permute-done((f32[512,128]{1,0:T(8,128)S(1)}, f32[512,128]{1,0:T(8,128)S(1)}, u32[]{:S(2)}, u32[]{:S(2)}) %collective-permute-start.5) | collective-permute-done | bytes 262176 | tf_op jit(solution)/shard_map/ppermute | solution.py:103
  104.1 1.2 collective-permute-start.6
  105.3 4.8 %collective-permute-done.6 = f32[512,128]{1,0:T(8,128)S(1)} collective-permute-done((f32[512,128]{1,0:T(8,128)S(1)}, f32[512,128]{1,0:T(8,128)S(1)}, u32[]{:S(2)}, u32[]{:S(2)}) %collective-permute-start.6) | collective-permute-done | bytes 262176 | tf_op jit(solution)/shard_map/ppermute | solution.py:103
  110.1 2.4 %collective-permute-start.7 = (f32[512,128]{1,0:T(8,128)S(1)}, f32[512,128]{1,0:T(8,128)S(1)}, u32[]{:S(2)}, u32[]{:S(2)}) collective-permute-start(f32[512,128]{1,0:T(8,128)S(1)} %add.117), channel_id=1, source_target_pairs={{0,8},{1,9},{2,10},{3,11},{4,12},{5,13},{6,14},{7,15},{8,0},{9,1},... | collective-permute-start | bytes 786440 | tf_op jit(solution)/shard_map/ppermute | solution.py:103
  112.6 4.6 %collective-permute-done.7 = f32[512,128]{1,0:T(8,128)S(1)} collective-permute-done((f32[512,128]{1,0:T(8,128)S(1)}, f32[512,128]{1,0:T(8,128)S(1)}, u32[]{:S(2)}, u32[]{:S(2)}) %collective-permute-start.7) | collective-permute-done | bytes 262176 | tf_op jit(solution)/shard_map/ppermute | solution.py:103
  117.2 3.9 %collective-permute-start.8 = (f32[512,128]{1,0:T(8,128)S(1)}, f32[512,128]{1,0:T(8,128)S(1)}, u32[]{:S(2)}, u32[]{:S(2)}) collective-permute-start(f32[512,128]{1,0:T(8,128)S(1)} %add.118), channel_id=1, source_target_pairs={{0,16},{16,0},{32,48},{48,32},{64,80},{80,64},{96,112},{112,96},{1... | collective-permute-start | bytes 786440 | tf_op jit(solution)/shard_map/ppermute | solution.py:103
  121.0 1.2 collective-permute-done.8
  122.2 2.4 %collective-permute-start.9 = (f32[512,128]{1,0:T(8,128)S(1)}, f32[512,128]{1,0:T(8,128)S(1)}, u32[]{:S(2)}, u32[]{:S(2)}) collective-permute-start(f32[512,128]{1,0:T(8,128)S(1)} %add.119), channel_id=1, source_target_pairs={{0,32},{16,48},{32,0},{48,16},{64,96},{80,112},{96,64},{112,80},{1... | collective-permute-start | bytes 786440 | tf_op jit(solution)/shard_map/ppermute | solution.py:103
  124.8 6.1 %collective-permute-done.9 = f32[512,128]{1,0:T(8,128)S(1)} collective-permute-done((f32[512,128]{1,0:T(8,128)S(1)}, f32[512,128]{1,0:T(8,128)S(1)}, u32[]{:S(2)}, u32[]{:S(2)}) %collective-permute-start.9) | collective-permute-done | bytes 262176 | tf_op jit(solution)/shard_map/ppermute | solution.py:103
  130.9 3.6 %collective-permute-start.10 = (f32[512,128]{1,0:T(8,128)S(1)}, f32[512,128]{1,0:T(8,128)S(1)}, u32[]{:S(2)}, u32[]{:S(2)}) collective-permute-start(f32[512,128]{1,0:T(8,128)S(1)} %add.120), channel_id=1, source_target_pairs={{0,64},{16,80},{32,96},{48,112},{64,0},{80,16},{96,32},{112,48},{1... | collective-permute-start | bytes 786440 | tf_op jit(solution)/shard_map/ppermute | solution.py:103
  134.6 1.6 subtract_multiply_fusion
  136.1 3.9 %collective-permute-done.10 = f32[512,128]{1,0:T(8,128)S(1)} collective-permute-done((f32[512,128]{1,0:T(8,128)S(1)}, f32[512,128]{1,0:T(8,128)S(1)}, u32[]{:S(2)}, u32[]{:S(2)}) %collective-permute-start.10) | collective-permute-done | bytes 262176 | tf_op jit(solution)/shard_map/ppermute | solution.py:103
  140.8 5.8 %cholesky.17 = f32[64,64]{1,0:T(8,128)S(1)} custom-call(f32[64,64]{1,0:T(8,128)S(1)} %fusion.22), custom_call_target="Cholesky" | custom-call | tf_op jit(solution)/shard_map/jit(cholesky)/cholesky | solution.py:135
  146.7 0.7 compare_reduce_fusion
  147.4 0.7 fusion.17
  148.1 4.9 %custom-call.8 = f32[1,64,64]{1,2,0:T(8,128)S(1)} custom-call(f32[1,64,64]{2,1,0:T(8,128)S(1)} %fusion.17), custom_call_target="InvertDiagBlocksLowerTriangular" | custom-call | tf_op jit(solution)/shard_map/triangular_solve | solution.py:137
  153.9 5.7 %copy_add_fusion = f32[64,64,128]{2,0,1:T(8,128)S(1)} fusion(f32[64,64,128]{2,1,0:T(8,128)S(1)} %copy-done, f32[64,64,1]{0,1,2:T(8,128)S(1)} %convolution_bitcast_fusion, f32[64,64,128]{2,1,0:T(8,128)} %subtract_multiply_fusion), kind=kOutput, calls=%fused_computation.2 | convolution fusion | flops 403177472 | bytes 6307840 | tf_op jit(solution)/shard_map/mrc,mn->nrc/dot_general | solution.py:202
  159.6 2.5 %copy.80 = f32[64,64,128]{2,1,0:T(8,128)} copy(f32[64,64,128]{2,0,1:T(8,128)S(1)} %copy_add_fusion) | data formatting | bytes 4194304
  (72 shorter events, 3.6 us)
Async XLA Ops:
  4.2 19.9 %collective-permute-start = (f32[3,129,128]{2,0,1:T(4,128)}, f32[3,129,128]{2,0,1:T(4,128)}, u32[]{:S(2)}, u32[]{:S(2)}) collective-permute-start(f32[3,129,128]{2,0,1:T(4,128)} %maximum_bitcast_fusion), channel_id=1, source_target_pairs={{16,0},{32,16},{48,32},{64,48},{80,64},{96,80},{112,96},{17,1},{33... | collective-permute-start | bytes 594440 | tf_op jit(solution)/shard_map/ppermute | solution.py:21
  8.3 8.0 %copy-start.2 = (bf16[64,64,128]{2,1,0:T(8,128)(2,1)S(1)}, bf16[64,64,128]{2,1,0:T(8,128)(2,1)}, u32[]{:S(2)}) copy-start(bf16[64,64,128]{2,1,0:T(8,128)(2,1)} %head_ref.1) | copy-start | bytes 3145732
  8.3 15.9 %collective-permute-start.1 = (f32[3,129,128]{2,0,1:T(4,128)}, f32[3,129,128]{2,0,1:T(4,128)}, u32[]{:S(2)}, u32[]{:S(2)}) collective-permute-start(f32[3,129,128]{2,0,1:T(4,128)} %maximum_bitcast_fusion.1), channel_id=1, source_target_pairs={{0,16},{16,32},{32,48},{48,64},{64,80},{80,96},{96,112},{1,17},{17... | collective-permute-start | bytes 594440 | tf_op jit(solution)/shard_map/ppermute | solution.py:21
  16.2 1.5 copy-start.4
  21.8 1.4 copy-start.6
  25.3 5.3 %copy-start.1 = (f32[129,8,128]{2,1,0:T(8,128)}, f32[129,8,128]{2,1,0:T(8,128)S(1)}, u32[]{:S(2)}) copy-start(f32[129,8,128]{2,1,0:T(8,128)S(1)} %pad_maximum_fusion.1.source_rows_ref.perm_rows_ref.head_rows_ref) | copy-start | bytes 1585156
  25.3 6.8 %copy-start.9 = (s32[4]{0:T(128)S(1)}, s32[4]{0:T(128)}, u32[]{:S(2)}) copy-start(s32[4]{0:T(128)} %param.12) | copy-start | bytes 52
  26.5 8.0 %collective-permute-start.3 = (f32[3,129,72]{2,1,0:T(8,128)S(1)}, f32[3,129,72]{2,1,0:T(8,128)S(1)}, u32[]{:S(2)}, u32[]{:S(2)}) collective-permute-start(f32[3,129,72]{2,1,0:T(8,128)S(1)} %maximum_bitcast_fusion.3), channel_id=1, source_target_pairs={{0,1},{1,2},{2,3},{3,4},{4,5},{5,6},{6,7},{7,8},{8,9},{9,10},{10,1... | collective-permute-start | bytes 334376 | tf_op jit(solution)/shard_map/ppermute | solution.py:21
  30.8 8.7 %collective-permute-start.2 = (f32[3,129,72]{2,1,0:T(8,128)S(1)}, f32[3,129,72]{2,1,0:T(8,128)S(1)}, u32[]{:S(2)}, u32[]{:S(2)}) collective-permute-start(f32[3,129,72]{2,1,0:T(8,128)S(1)} %maximum_bitcast_fusion.2), channel_id=1, source_target_pairs={{1,0},{2,1},{3,2},{4,3},{5,4},{6,5},{7,6},{8,7},{9,8},{10,9},{11,1... | collective-permute-start | bytes 334376 | tf_op jit(solution)/shard_map/ppermute | solution.py:21
  87.1 37.5 %copy-start = (f32[64,64,128]{2,1,0:T(8,128)S(1)}, f32[64,64,128]{2,1,0:T(8,128)}, u32[]{:S(2)}) copy-start(f32[64,64,128]{2,1,0:T(8,128)} %perm_ref.1) | copy-start | bytes 6291460
  87.1 7.1 %collective-permute-start.4 = (f32[512,128]{1,0:T(8,128)S(1)}, f32[512,128]{1,0:T(8,128)S(1)}, u32[]{:S(2)}, u32[]{:S(2)}) collective-permute-start(f32[512,128]{1,0:T(8,128)S(1)} %select_select_fusion), channel_id=1, source_target_pairs={{0,1},{1,0},{2,3},{3,2},{4,5},{5,4},{6,7},{7,6},{8,9},{9,8},{10,11... | collective-permute-start | bytes 786440 | tf_op jit(solution)/shard_map/ppermute | solution.py:103
  94.3 9.8 %collective-permute-start.5 = (f32[512,128]{1,0:T(8,128)S(1)}, f32[512,128]{1,0:T(8,128)S(1)}, u32[]{:S(2)}, u32[]{:S(2)}) collective-permute-start(f32[512,128]{1,0:T(8,128)S(1)} %add.115), channel_id=1, source_target_pairs={{0,2},{1,3},{2,0},{3,1},{4,6},{5,7},{6,4},{7,5},{8,10},{9,11},{10,... | collective-permute-start | bytes 786440 | tf_op jit(solution)/shard_map/ppermute | solution.py:103
  104.1 20.6 %copy-start.5 = (f32[1024]{0:T(1024)S(1)}, f32[1024]{0:T(1024)}, u32[]{:S(2)}) copy-start(f32[1024]{0:T(1024)} %param.14) | copy-start | bytes 12292
  104.1 6.0 %collective-permute-start.6 = (f32[512,128]{1,0:T(8,128)S(1)}, f32[512,128]{1,0:T(8,128)S(1)}, u32[]{:S(2)}, u32[]{:S(2)}) collective-permute-start(f32[512,128]{1,0:T(8,128)S(1)} %add.116), channel_id=1, source_target_pairs={{0,4},{1,5},{2,6},{3,7},{4,0},{5,1},{6,2},{7,3},{8,12},{9,13},{10,... | collective-permute-start | bytes 786440 | tf_op jit(solution)/shard_map/ppermute | solution.py:103
  110.1 7.0 %collective-permute-start.7 = (f32[512,128]{1,0:T(8,128)S(1)}, f32[512,128]{1,0:T(8,128)S(1)}, u32[]{:S(2)}, u32[]{:S(2)}) collective-permute-start(f32[512,128]{1,0:T(8,128)S(1)} %add.117), channel_id=1, source_target_pairs={{0,8},{1,9},{2,10},{3,11},{4,12},{5,13},{6,14},{7,15},{8,0},{9,1},... | collective-permute-start | bytes 786440 | tf_op jit(solution)/shard_map/ppermute | solution.py:103
  117.2 5.0 %collective-permute-start.8 = (f32[512,128]{1,0:T(8,128)S(1)}, f32[512,128]{1,0:T(8,128)S(1)}, u32[]{:S(2)}, u32[]{:S(2)}) collective-permute-start(f32[512,128]{1,0:T(8,128)S(1)} %add.118), channel_id=1, source_target_pairs={{0,16},{16,0},{32,48},{48,32},{64,80},{80,64},{96,112},{112,96},{1... | collective-permute-start | bytes 786440 | tf_op jit(solution)/shard_map/ppermute | solution.py:103
  122.2 8.7 %collective-permute-start.9 = (f32[512,128]{1,0:T(8,128)S(1)}, f32[512,128]{1,0:T(8,128)S(1)}, u32[]{:S(2)}, u32[]{:S(2)}) collective-permute-start(f32[512,128]{1,0:T(8,128)S(1)} %add.119), channel_id=1, source_target_pairs={{0,32},{16,48},{32,0},{48,16},{64,96},{80,112},{96,64},{112,80},{1... | collective-permute-start | bytes 786440 | tf_op jit(solution)/shard_map/ppermute | solution.py:103
  130.9 9.1 %collective-permute-start.10 = (f32[512,128]{1,0:T(8,128)S(1)}, f32[512,128]{1,0:T(8,128)S(1)}, u32[]{:S(2)}, u32[]{:S(2)}) collective-permute-start(f32[512,128]{1,0:T(8,128)S(1)} %add.120), channel_id=1, source_target_pairs={{0,64},{16,80},{32,96},{48,112},{64,0},{80,16},{96,32},{112,48},{1... | collective-permute-start | bytes 786440 | tf_op jit(solution)/shard_map/ppermute | solution.py:103
  136.1 16.9 %copy-start.7 = (f32[64,1024]{1,0:T(8,128)S(1)}, f32[64,1024]{1,0:T(8,128)}, u32[]{:S(2)}) copy-start(f32[64,1024]{1,0:T(8,128)} %param.15) | copy-start | bytes 786436
  136.1 16.9 %copy-start.8 = (f32[1024]{0:T(1024)S(1)}, f32[1024]{0:T(1024)}, u32[]{:S(2)}) copy-start(f32[1024]{0:T(1024)} %param.13) | copy-start | bytes 12292
  140.1 13.6 %copy-start.3 = (f32[64,1024]{1,0:T(8,128)}, f32[64,1024]{1,0:T(8,128)S(1)}, u32[]{:S(2)}) copy-start(f32[64,1024]{1,0:T(8,128)S(1)} %reshape.139) | copy-start | bytes 786436
where the time goes:
time: 163 us; the launch traced here: 162 us
  waiting for transfers between devices  35.4 us (22%)
  local copies, waits for them, and re-layouts  33.6 us (21%)
  starting transfers between devices  30.8 us (19%)
  Pallas kernels  28 us (17%)
  other arithmetic  26.4 us (16%)
  matrix products  6.91 us (4%)
    ppermute x7, waiting for transfers between devices, butterfly(): lax.ppermute(value, axis, [(i, i ^ step) for i in range(count)])  31.6 us
    pallas_call x1, Pallas kernels, run_stencil(): pl.pallas_call(stencil_kernel, grid=(blocks,), in_specs=[full2(mask.shape...  28 us
    ppermute x7, starting transfers between devices, butterfly(): lax.ppermute(value, axis, [(i, i ^ step) for i in range(count)])  19.4 us
    ppermute x4, starting transfers between devices, send(): return lax.ppermute(piece, axis, pairs)  11.5 us
    unnamed x26, local copies, waits for them, and re-layouts  7.81 us
    concatenate x1, other arithmetic, per_device(): jnp.concatenate([from_right, jnp.zeros((stacked_total, ext_rows, col_coun...  7.25 us
    another operation x3, other arithmetic, blending_weights(): factor = jnp.linalg.cholesky(system)  6.6 us
    ppermute x2, local copies, waits for them, and re-layouts, send(): return lax.ppermute(piece, axis, pairs)  6.37 us
  transfers between devices with their start and end apart: 11, of which 9 were waited for; matrix products, arithmetic and copies ran while one was open for 12% of the time, Pallas kernels for 0%

commit v1 on v0

--- a/solution.py
+++ b/solution.py
@@ -96,13 +96,14 @@
     )(mask, source, halo_rows, halo_cols, perm, head, halo_rows, halo_rows, halo_cols, halo_cols)
 
 
-def butterfly(value, axis):
-    count = lax.axis_size(axis)
-    step = 1
-    while step < count:
-        value = value + lax.ppermute(value, axis, [(i, i ^ step) for i in range(count)])
-        step *= 2
-    return value
+def broadcast_from_owners(value, axes):
+    count = 1
+    for axis in axes:
+        count *= lax.axis_size(axis)
+    chunks = value.reshape(count, -1)
+    own_chunk = lax.all_to_all(chunks, axes, 0, 0, tiled=True).sum(axis=0)
+    spread = jnp.broadcast_to(own_chunk[None], chunks.shape)
+    return lax.all_to_all(spread, axes, 0, 0, tiled=True).reshape(value.shape)
 
 
 def neighbours(padded):
@@ -186,14 +187,13 @@
     pressure_low, hydraulic_head = run_stencil(
         inside.astype(f32), recharge, halo_rows, halo_cols, logarithmic_conductivity, starting_head, 8
     )
-    flat_press = hydraulic_head.reshape(member_count, row_count * col_count)
     group_total, well_count = well_cells.shape
-    local_data = jnp.take(flat_press, well_cells.reshape(-1), axis=1)
+    wells = well_cells.reshape(-1)
+    local_data = hydraulic_head[:, wells // col_count, wells % col_count]
     me = lax.axis_index("row") * lax.axis_size("col") + lax.axis_index("col")
     mine = jnp.repeat(well_owner == me, well_count)
     local_data = jnp.where(mine[None, :], local_data, 0.0)
-    packed = local_data.reshape(-1, 128)
-    predicted = butterfly(butterfly(packed, "col"), "row").reshape(local_data.shape)
+    predicted = broadcast_from_owners(local_data, ("row", "col"))
     mixing = blending_weights(predicted, observed, obs_var, perturb)
     ensemble_spread = math.sqrt(member_count - 1)
     anomalies = (

time: 163 us -> 160 us (0.982)
  waiting for transfers between devices: 35.4 us -> 23.9 us
  local copies, waits for them, and re-layouts: 33.6 us -> 42.8 us
  starting transfers between devices: 30.8 us -> 27.3 us
  other arithmetic: 26.4 us -> 28.4 us
    ppermute x7 -> x0, waiting for transfers between devices: 31.6 us -> none  [butterfly(): lax.ppermute(value, axis, [(i, i ^ step) for i in range(count)])]
    all_to_all x0 -> x2, waiting for transfers between devices: none -> 20.1 us  [the longest x1 10.4 us: broadcast_from_owners(): own_chunk = lax.all_to_all(chunks, axes, 0, 0, tiled=True).sum(axis=0)]
    ppermute x7 -> x0, starting transfers between devices: 19.4 us -> none  [butterfly(): lax.ppermute(value, axis, [(i, i ^ step) for i in range(count)])]
    all_to_all x0 -> x2, starting transfers between devices: none -> 15.8 us  [the longest x1 11.5 us: broadcast_from_owners(): own_chunk = lax.all_to_all(chunks, axes, 0, 0, tiled=True).sum(axis=0)]
    gather x3, local copies, waits for them, and re-layouts: 5.22 us -> 10.8 us  [per_device(): local_data = hydraulic_head[:, wells // col_count, wells % col_count]]
    pallas_call x0 -> x1, local copies, waits for them, and re-layouts: none -> 3.82 us  [run_stencil(): pl.pallas_call(stencil_kernel, grid=(blocks,), in_specs=[full2(mask.shape...]
    reshape x3 -> x1, local copies, waits for them, and re-layouts: 3.89 us -> 0.09 us  [broadcast_from_owners(): return lax.all_to_all(spread, axes, 0, 0, tiled=True).reshape(value.shape)]
  transfers between devices with their start and end apart: 11 -> 6, of which waited for: 9 -> 4; matrix products, arithmetic and copies ran while one was open for 12% -> 12% of each run, Pallas kernels for 0% -> 0%
where the time goes in v1:
time: 160 us; the launch traced here: 159 us
  local copies, waits for them, and re-layouts  42.8 us (27%)
  other arithmetic  28.4 us (18%)
  Pallas kernels  28 us (18%)
  starting transfers between devices  27.3 us (17%)
  waiting for transfers between devices  23.9 us (15%)
  matrix products  8.04 us (5%)
    pallas_call x1, Pallas kernels, run_stencil(): pl.pallas_call(stencil_kernel, grid=(blocks,), in_specs=[full2(mask.shape...  28 us
    all_to_all x1, starting transfers between devices, broadcast_from_owners(): own_chunk = lax.all_to_all(chunks, axes, 0, 0, tiled=True).sum(axis=0)  11.5 us
    ppermute x4, starting transfers between devices, send(): return lax.ppermute(piece, axis, pairs)  11.5 us
    gather x3, local copies, waits for them, and re-layouts, per_device(): local_data = hydraulic_head[:, wells // col_count, wells % col_count]  10.8 us
    all_to_all x1, waiting for transfers between devices, broadcast_from_owners(): own_chunk = lax.all_to_all(chunks, axes, 0, 0, tiled=True).sum(axis=0)  10.4 us
    all_to_all x1, waiting for transfers between devices, broadcast_from_owners(): return lax.all_to_all(spread, axes, 0, 0, tiled=True).reshape(value.shape)  9.65 us
    unnamed x26, local copies, waits for them, and re-layouts  8.52 us
    concatenate x1, other arithmetic, per_device(): jnp.concatenate([from_right, jnp.zeros((stacked_total, ext_rows, col_coun...  7.22 us
  transfers between devices with their start and end apart: 6, of which 4 were waited for; matrix products, arithmetic and copies ran while one was open for 12% of the time, Pallas kernels for 0%

profile of v1, /device:TPU:1, one launch (start us, length us, event | category | flops | bytes accessed | tf_op | source)
XLA Modules:
  0.0 159.4 jit_solution(5717847728241065039)
XLA Ops:
  0.6 1.1 fusion.32
  1.7 1.0 slice_convert_fusion.1
  2.7 0.7 slice_bitcast_fusion.3
  3.4 0.8 maximum_bitcast_fusion
  4.2 3.3 %collective-permute-start = (f32[3,129,128]{2,0,1:T(4,128)}, f32[3,129,128]{2,0,1:T(4,128)}, u32[]{:S(2)}, u32[]{:S(2)}) collective-permute-start(f32[3,129,128]{2,0,1:T(4,128)} %maximum_bitcast_fusion), channel_id=1, source_target_pairs={{16,0},{32,16},{48,32},{64,48},{80,64},{96,80},{112,96},{17,1},{33... | collective-permute-start | bytes 594440 | tf_op jit(solution)/shard_map/ppermute | solution.py:21
  7.5 0.8 maximum_bitcast_fusion.1
  8.3 3.7 %collective-permute-start.1 = (f32[3,129,128]{2,0,1:T(4,128)}, f32[3,129,128]{2,0,1:T(4,128)}, u32[]{:S(2)}, u32[]{:S(2)}) collective-permute-start(f32[3,129,128]{2,0,1:T(4,128)} %maximum_bitcast_fusion.1), channel_id=1, source_target_pairs={{0,16},{16,32},{32,48},{48,64},{64,80},{80,96},{96,112},{1,17},{17... | collective-permute-start | bytes 594440 | tf_op jit(solution)/shard_map/ppermute | solution.py:21
  11.9 4.3 %fusion.31 = (f32[64,64,3]{2,1,0:T(8,128)S(1)}, f32[64,64,3]{2,1,0:T(8,128)}) fusion(f32[64,64,128]{2,1,0:T(8,128)} %perm_ref.1), kind=kLoop, calls=%fused_computation.71 | loop fusion | bytes 196608 | tf_op jit(solution)/shard_map/slice | solution.py:174
  16.2 1.5 fusion.33
  17.8 2.3 %copy.91 = f32[64,64,3]{1,0,2:T(8,128)S(1)} copy(f32[64,64,3]{2,1,0:T(8,128)} %get-tuple-element.25) | data formatting | bytes 98304
  20.1 1.7 %copy.92 = bf16[64,64,3]{1,0,2:T(8,128)(2,1)S(1)} copy(bf16[64,64,3]{2,1,0:T(8,128)(2,1)} %get-tuple-element.29) | data formatting | bytes 49152
  21.9 0.7 copy.89
  22.6 0.5 copy.90
  23.5 0.7 and_convert_fusion.mask_ref
  24.2 1.2 pad_maximum_fusion.1.source_rows_ref.perm_rows_ref.head_rows_ref
  25.6 0.9 copy.74
  26.7 3.2 %collective-permute-start.3 = (f32[3,129,72]{2,1,0:T(8,128)S(1)}, f32[3,129,72]{2,1,0:T(8,128)S(1)}, u32[]{:S(2)}, u32[]{:S(2)}) collective-permute-start(f32[3,129,72]{2,1,0:T(8,128)S(1)} %maximum_bitcast_fusion.3), channel_id=1, source_target_pairs={{0,1},{1,2},{2,3},{3,4},{4,5},{5,6},{6,7},{7,8},{8,9},{9,10},{10,1... | collective-permute-start | bytes 334376 | tf_op jit(solution)/shard_map/ppermute | solution.py:21
  29.9 0.9 copy.68
  30.9 1.3 collective-permute-start.2
  32.6 2.1 %collective-permute-done.3 = f32[3,129,72]{2,1,0:T(8,128)S(1)} collective-permute-done((f32[3,129,72]{2,1,0:T(8,128)S(1)}, f32[3,129,72]{2,1,0:T(8,128)S(1)}, u32[]{:S(2)}, u32[]{:S(2)}) %collective-permute-start.3) | collective-permute-done | bytes 111488 | tf_op jit(solution)/shard_map/ppermute | solution.py:21
  34.7 3.2 %copy.75 = f32[3,129,72]{0,2,1:T(8,128)} copy(f32[3,129,72]{2,1,0:T(8,128)S(1)} %collective-permute-done.3) | data formatting | bytes 222912 | tf_op jit(solution)/shard_map/ppermute | solution.py:21
  37.9 1.7 %collective-permute-done.2 = f32[3,129,72]{2,1,0:T(8,128)S(1)} collective-permute-done((f32[3,129,72]{2,1,0:T(8,128)S(1)}, f32[3,129,72]{2,1,0:T(8,128)S(1)}, u32[]{:S(2)}, u32[]{:S(2)}) %collective-permute-start.2) | collective-permute-done | bytes 111488 | tf_op jit(solution)/shard_map/ppermute | solution.py:21
  39.6 3.2 %copy.69 = f32[3,129,72]{0,2,1:T(8,128)} copy(f32[3,129,72]{2,1,0:T(8,128)S(1)} %collective-permute-done.2) | data formatting | bytes 222912 | tf_op jit(solution)/shard_map/ppermute | solution.py:21
  42.7 7.2 %pad_maximum_fusion.source_cols_ref.perm_cols_ref.head_cols_ref = f32[129,72,128]{2,1,0:T(8,128)} fusion(f32[129,72,3]{2,1,0:T(8,128)} %bitcast.50, f32[129,72,3]{2,1,0:T(8,128)} %bitcast.51, f32[128]{0:T(128)S(1)} %pad.1.clone), kind=kLoop, calls=%fused_computation.1 | loop fusion | flops 2377728 | bytes 4978880 | tf_op jit(solution)/shard_map/concatenate | solution.py:181
  50.0 28.0 %shard_map.103 = (bf16[64,64,128]{2,1,0:T(8,128)(2,1)}, f32[64,64,128]{2,1,0:T(8,128)}) custom-call(f32[72,256]{1,0:T(8,128)} %and_convert_fusion.mask_ref, f32[64,128]{1,0:T(8,128)} %source_ref.1, f32[129,8,128]{2,1,0:T(8,128)} %copy-done.1, f32[129,72,128]{2,1,0:T(8,128)} %pad_maximum_fusion.source_cols_ref.perm_cols_ref.head_cols_ref, ...), custom_call_target="tpu_custom_call" | custom-call | flops 94371840 | bytes 7340032 | tf_op jit(solution)/shard_map/pallas_call | solution.py:73
  77.9 3.8 %copy.76 = f32[64,64,128]{0,2,1:T(8,128)} copy(f32[64,64,128]{2,1,0:T(8,128)} %get-tuple-element.6) | data formatting | bytes 4194304 | tf_op jit(solution)/shard_map/pallas_call | solution.py:73
  81.8 10.6 %gather_fusion = f32[1024,64]{1,0:T(8,128)S(1)} fusion(f32[64,64,128]{0,2,1:T(8,128)} %copy.76, s32[1024]{0:T(1024)S(1)} %bitcast.49), kind=kCustom, calls=%fused_computation | custom fusion | bytes 532480 | tf_op jit(solution)/shard_map/gather | solution.py:192
  92.6 1.0 copy.78
  93.6 11.5 %all-to-all-start = ((f32[128,1,512]{2,1,0:T(1,128)}), f32[128,1,512]{2,1,0:T(1,128)S(1)}, u32[]{:S(2)}, u32[]{:S(2)}) async-start(f32[128,1,512]{2,1,0:T(1,128)} %copy.78), calls=%async_computation | async-start | bytes 524288 | tf_op jit(solution)/shard_map/all_to_all | solution.py:104
  105.4 0.4 div.86
  105.9 10.4 %all-to-all-done = f32[128,1,512]{2,1,0:T(1,128)S(1)} async-done(((f32[128,1,512]{2,1,0:T(1,128)}), f32[128,1,512]{2,1,0:T(1,128)S(1)}, u32[]{:S(2)}, u32[]{:S(2)}) %all-to-all-start) | async-done | bytes 262176 | tf_op jit(solution)/shard_map/all_to_all | solution.py:104
  116.5 0.8 broadcast_in_dim.68
  117.4 4.3 %all-to-all-start.1 = ((f32[128,1,512]{2,1,0:T(1,128)}), f32[128,1,512]{2,1,0:T(1,128)S(1)}, u32[]{:S(2)}, u32[]{:S(2)}) async-start(f32[128,1,512]{2,1,0:T(1,128)} %broadcast_in_dim.68), calls=%async_computation.1 | async-start | bytes 524288 | tf_op jit(solution)/shard_map/all_to_all | solution.py:106
  121.6 1.6 subtract_multiply_fusion
  123.2 9.6 %all-to-all-done.1 = f32[128,1,512]{2,1,0:T(1,128)S(1)} async-done(((f32[128,1,512]{2,1,0:T(1,128)}), f32[128,1,512]{2,1,0:T(1,128)S(1)}, u32[]{:S(2)}, u32[]{:S(2)}) %all-to-all-start.1) | async-done | bytes 262176 | tf_op jit(solution)/shard_map/all_to_all | solution.py:106
  132.8 0.6 reduce.7
  133.6 0.6 copy-done.3
  134.3 0.4 sub.51
  134.7 1.6 %fusion.30 = (f32[128,512]{1,0:T(8,128)S(1)}, f32[128,512]{1,0:T(8,128)S(1)}) fusion(f32[128,1,512]{2,1,0:T(1,128)S(1)} %all-to-all-done.1, f32[128,1,512]{2,1,0:T(1,128)S(1)} %sub.51, f32[128,1,512]{2,1,0:T(1,128)S(1)} %div.86), kind=kLoop, calls=%fused_computation.70 | loop fusion | flops 196608 | bytes 1310720 | tf_op jit(solution)/shard_map/div | solution.py:129
  136.6 0.4 fusion.35
  137.0 5.8 %cholesky.17 = f32[64,64]{1,0:T(8,128)S(1)} custom-call(f32[64,64]{1,0:T(8,128)S(1)} %fusion.21), custom_call_target="Cholesky" | custom-call | tf_op jit(solution)/shard_map/jit(cholesky)/cholesky | solution.py:136
  142.9 0.7 compare_reduce_fusion
  143.6 0.6 fusion.16
  144.3 4.9 %custom-call.8 = f32[1,64,64]{1,2,0:T(8,128)S(1)} custom-call(f32[1,64,64]{2,1,0:T(8,128)S(1)} %fusion.16), custom_call_target="InvertDiagBlocksLowerTriangular" | custom-call | tf_op jit(solution)/shard_map/triangular_solve | solution.py:138
  149.2 1.5 fusion.4
  151.0 0.2 convolution_bitcast_fusion
  151.2 5.7 %copy_add_fusion = f32[64,64,128]{2,0,1:T(8,128)S(1)} fusion(f32[64,64,128]{2,1,0:T(8,128)S(1)} %copy-done, f32[64,64,1]{0,1,2:T(8,128)S(1)} %convolution_bitcast_fusion, f32[64,64,128]{2,1,0:T(8,128)} %subtract_multiply_fusion), kind=kOutput, calls=%fused_computation.2 | convolution fusion | flops 403177472 | bytes 6307840 | tf_op jit(solution)/shard_map/mrc,mn->nrc/dot_general | solution.py:202
  156.9 2.5 %copy.83 = f32[64,64,128]{2,1,0:T(8,128)} copy(f32[64,64,128]{2,0,1:T(8,128)S(1)} %copy_add_fusion) | data formatting | bytes 4194304
  (61 shorter events, 2.8 us)
Async XLA Ops:
  4.2 20.0 %collective-permute-start = (f32[3,129,128]{2,0,1:T(4,128)}, f32[3,129,128]{2,0,1:T(4,128)}, u32[]{:S(2)}, u32[]{:S(2)}) collective-permute-start(f32[3,129,128]{2,0,1:T(4,128)} %maximum_bitcast_fusion), channel_id=1, source_target_pairs={{16,0},{32,16},{48,32},{64,48},{80,64},{96,80},{112,96},{17,1},{33... | collective-permute-start | bytes 594440 | tf_op jit(solution)/shard_map/ppermute | solution.py:21
  8.2 8.0 %copy-start.2 = (bf16[64,64,128]{2,1,0:T(8,128)(2,1)S(1)}, bf16[64,64,128]{2,1,0:T(8,128)(2,1)}, u32[]{:S(2)}) copy-start(bf16[64,64,128]{2,1,0:T(8,128)(2,1)} %head_ref.1) | copy-start | bytes 3145732
  8.3 16.0 %collective-permute-start.1 = (f32[3,129,128]{2,0,1:T(4,128)}, f32[3,129,128]{2,0,1:T(4,128)}, u32[]{:S(2)}, u32[]{:S(2)}) collective-permute-start(f32[3,129,128]{2,0,1:T(4,128)} %maximum_bitcast_fusion.1), channel_id=1, source_target_pairs={{0,16},{16,32},{32,48},{48,64},{64,80},{80,96},{96,112},{1,17},{17... | collective-permute-start | bytes 594440 | tf_op jit(solution)/shard_map/ppermute | solution.py:21
  16.2 1.5 copy-start.4
  21.8 1.4 copy-start.6
  21.8 1.5 copy-start.8
  25.4 5.3 %copy-start.1 = (f32[129,8,128]{2,1,0:T(8,128)}, f32[129,8,128]{2,1,0:T(8,128)S(1)}, u32[]{:S(2)}) copy-start(f32[129,8,128]{2,1,0:T(8,128)S(1)} %pad_maximum_fusion.1.source_rows_ref.perm_rows_ref.head_rows_ref) | copy-start | bytes 1585156
  26.7 8.0 %collective-permute-start.3 = (f32[3,129,72]{2,1,0:T(8,128)S(1)}, f32[3,129,72]{2,1,0:T(8,128)S(1)}, u32[]{:S(2)}, u32[]{:S(2)}) collective-permute-start(f32[3,129,72]{2,1,0:T(8,128)S(1)} %maximum_bitcast_fusion.3), channel_id=1, source_target_pairs={{0,1},{1,2},{2,3},{3,4},{4,5},{5,6},{6,7},{7,8},{8,9},{9,10},{10,1... | collective-permute-start | bytes 334376 | tf_op jit(solution)/shard_map/ppermute | solution.py:21
  30.9 8.7 %collective-permute-start.2 = (f32[3,129,72]{2,1,0:T(8,128)S(1)}, f32[3,129,72]{2,1,0:T(8,128)S(1)}, u32[]{:S(2)}, u32[]{:S(2)}) collective-permute-start(f32[3,129,72]{2,1,0:T(8,128)S(1)} %maximum_bitcast_fusion.2), channel_id=1, source_target_pairs={{1,0},{2,1},{3,2},{4,3},{5,4},{6,5},{7,6},{8,7},{9,8},{10,9},{11,1... | collective-permute-start | bytes 334376 | tf_op jit(solution)/shard_map/ppermute | solution.py:21
  92.3 12.8 %copy-start.5 = (f32[1024]{0:T(1024)S(1)}, f32[1024]{0:T(1024)}, u32[]{:S(2)}) copy-start(f32[1024]{0:T(1024)} %param.14) | copy-start | bytes 12292
  92.4 12.8 %copy-start = (f32[64,64,128]{2,1,0:T(8,128)S(1)}, f32[64,64,128]{2,1,0:T(8,128)}, u32[]{:S(2)}) copy-start(f32[64,64,128]{2,1,0:T(8,128)} %perm_ref.1) | copy-start | bytes 6291460
  93.6 22.7 %all-to-all-start = ((f32[128,1,512]{2,1,0:T(1,128)}), f32[128,1,512]{2,1,0:T(1,128)S(1)}, u32[]{:S(2)}, u32[]{:S(2)}) async-start(f32[128,1,512]{2,1,0:T(1,128)} %copy.78), calls=%async_computation | async-start | bytes 524288 | tf_op jit(solution)/shard_map/all_to_all | solution.py:104
  117.4 15.5 %all-to-all-start.1 = ((f32[128,1,512]{2,1,0:T(1,128)}), f32[128,1,512]{2,1,0:T(1,128)S(1)}, u32[]{:S(2)}, u32[]{:S(2)}) async-start(f32[128,1,512]{2,1,0:T(1,128)} %broadcast_in_dim.68), calls=%async_computation.1 | async-start | bytes 524288 | tf_op jit(solution)/shard_map/all_to_all | solution.py:106
  133.5 0.7 copy-start.3
  133.6 15.6 %copy-start.7 = (f32[1024]{0:T(1024)S(1)}, f32[1024]{0:T(1024)}, u32[]{:S(2)}) copy-start(f32[1024]{0:T(1024)} %param.13) | copy-start | bytes 12292

commit v2 on v1

--- a/solution.py
+++ b/solution.py
@@ -13,12 +13,18 @@
 time_step = 0.13
 
 
-def send(piece, axis, forward):
-    count = lax.axis_size(axis)
-    pairs = [(i, i + 1) for i in range(count - 1)]
-    if not forward:
-        pairs = [(target, source) for source, target in pairs]
-    return lax.ppermute(piece, axis, pairs)
+def send(piece, rows_by, cols_by, carried):
+    row_count, col_count = lax.axis_size("row"), lax.axis_size("col")
+    pairs = []
+    for r in range(row_count):
+        for c in range(col_count):
+            if 0 <= r + rows_by < row_count and 0 <= c + cols_by < col_count:
+                pairs.append((r * col_count + c, (r + rows_by) * col_count + c + cols_by))
+    if carried:
+        moved = jnp.moveaxis(piece, carried, 0)
+        return jnp.moveaxis(lax.ppermute(moved, ("row", "col"), pairs), 0, carried)
+    moved = jnp.moveaxis(piece, 0, -1)
+    return jnp.moveaxis(lax.ppermute(moved, ("row", "col"), pairs), -1, 0)
 
 
 def circular_inside(axis, local, width, size):
@@ -155,31 +161,35 @@
     ext_rows, ext_cols = row_count + 8, 2 * col_count
     f32 = jnp.float32
 
-    def stack_rows(lo, hi):
+    def piece(rows, cols):
         return jnp.concatenate(
-            [logarithmic_conductivity[:, lo:hi], starting_head[:, lo:hi].astype(f32), recharge[None, lo:hi]], axis=0
-        )
-
-    top_rows = jnp.moveaxis(stack_rows(0, width), 1, 0)
-    bottom_rows = jnp.moveaxis(stack_rows(row_count - width, row_count), 1, 0)
-    from_above = jnp.moveaxis(send(bottom_rows, "row", True), 0, 1)
-    from_below = jnp.moveaxis(send(top_rows, "row", False), 0, 1)
-    stacked_total = from_above.shape[0]
-    halo_rows = jnp.concatenate(
-        [from_below, jnp.zeros((stacked_total, 8 - 2 * width, col_count), f32), from_above], axis=1
-    )
-
-    def stack_cols(lo, hi):
-        interior = jnp.concatenate(
-            [logarithmic_conductivity[:, :, lo:hi], starting_head[:, :, lo:hi].astype(f32), recharge[None, :, lo:hi]],
+            [
+                logarithmic_conductivity[:, rows, cols],
+                starting_head[:, rows, cols].astype(f32),
+                recharge[None, rows, cols],
+            ],
             axis=0,
         )
-        return jnp.moveaxis(jnp.concatenate([interior, halo_rows[:, :, lo:hi]], axis=1), 2, 0)
-
-    from_left = jnp.moveaxis(send(stack_cols(col_count - width, col_count), "col", True), 0, 2)
-    from_right = jnp.moveaxis(send(stack_cols(0, width), "col", False), 0, 2)
+
+    first, last, every = slice(0, width), slice(-width, None), slice(None)
+    from_above = send(piece(last, every), 1, 0, 1)
+    from_below = send(piece(first, every), -1, 0, 1)
+    from_left = send(piece(every, last), 0, 1, 2)
+    from_right = send(piece(every, first), 0, -1, 2)
+    above_left = send(piece(last, last), 1, 1, 0)
+    above_right = send(piece(last, first), 1, -1, 0)
+    below_left = send(piece(first, last), -1, 1, 0)
+    below_right = send(piece(first, first), -1, -1, 0)
+    stacked_total = from_above.shape[0]
+    gap_rows = 8 - 2 * width
+    halo_rows = jnp.concatenate(
+        [from_below, jnp.zeros((stacked_total, gap_rows, col_count), f32), from_above], axis=1
+    )
+    gap_block = jnp.zeros((stacked_total, gap_rows, width), f32)
+    right_cols = jnp.concatenate([from_right, below_right, gap_block, above_right], axis=1)
+    left_cols = jnp.concatenate([from_left, below_left, gap_block, above_left], axis=1)
     halo_cols = jnp.concatenate(
-        [from_right, jnp.zeros((stacked_total, ext_rows, col_count - 2 * width), f32), from_left], axis=2
+        [right_cols, jnp.zeros((stacked_total, ext_rows, col_count - 2 * width), f32), left_cols], axis=2
     )
     inside = circular_inside("row", row_count, width, ext_rows)[:, None] & circular_inside(
         "col", col_count, width, ext_cols
@@ -188,8 +198,7 @@
         inside.astype(f32), recharge, halo_rows, halo_cols, logarithmic_conductivity, starting_head, 8
     )
     group_total, well_count = well_cells.shape
-    wells = well_cells.reshape(-1)
-    local_data = hydraulic_head[:, wells // col_count, wells % col_count]
+    local_data = jnp.take(hydraulic_head.reshape(member_count, row_count * col_count), well_cells.reshape(-1), axis=1)
     me = lax.axis_index("row") * lax.axis_size("col") + lax.axis_index("col")
     mine = jnp.repeat(well_owner == me, well_count)
     local_data = jnp.where(mine[None, :], local_data, 0.0)

time: 160 us -> 176 us (1.10)
  starting transfers between devices: 27.3 us -> 41 us
  local copies, waits for them, and re-layouts: 42.8 us -> 46 us
  waiting for transfers between devices: 23.9 us -> 20.7 us
  other arithmetic: 28.4 us -> 30.7 us
    ppermute x4 -> x8, starting transfers between devices: 11.5 us -> 25.3 us  [the longest x4 15.1 us: send(): return jnp.moveaxis(lax.ppermute(moved, ('row', 'col'), pairs), -1, 0)]
    ppermute x2, local copies, waits for them, and re-layouts: 6.34 us -> 12.6 us  [send(): return jnp.moveaxis(lax.ppermute(moved, ('row', 'col'), pairs), 0, carried)]
    gather x3, local copies, waits for them, and re-layouts: 10.8 us -> 5.21 us  [per_device(): jnp.take(hydraulic_head.reshape(member_count, row_count * col_count), wel...]
    reshape x0 -> x2, local copies, waits for them, and re-layouts: none -> 3.85 us  [the longest x1 3.83 us: per_device(): hydraulic_head.reshape(member_count, row_count * col_count)]
    pallas_call x1 -> x0, local copies, waits for them, and re-layouts: 3.82 us -> none  [run_stencil(): pl.pallas_call(stencil_kernel, grid=(blocks,), in_specs=[full2(mask.shape...]
    unnamed x26 -> x28, local copies, waits for them, and re-layouts: 8.52 us -> 12.3 us
    ppermute x4 -> x8, waiting for transfers between devices: 3.8 us -> 0.57 us  [the longest x4 0.56 us: send(): return jnp.moveaxis(lax.ppermute(moved, ('row', 'col'), pairs), 0, carried)]
    slice x6 -> x4, local copies, waits for them, and re-layouts: 8.79 us -> 6.17 us  [the longest x3 4.36 us: piece(): logarithmic_conductivity[:, rows, cols]]
  transfers between devices with their start and end apart: 6 -> 10, of which waited for: 4 -> 3; matrix products, arithmetic and copies ran while one was open for 12% -> 24% of each run, Pallas kernels for 0% -> 0%
where the time goes in v2:
time: 176 us
  local copies, waits for them, and re-layouts  46 us (26%)
  starting transfers between devices  41 us (23%)
  other arithmetic  30.7 us (17%)
  Pallas kernels  28 us (16%)
  waiting for transfers between devices  20.7 us (12%)
  matrix products  8.04 us (5%)
    pallas_call x1, Pallas kernels, run_stencil(): pl.pallas_call(stencil_kernel, grid=(blocks,), in_specs=[full2(mask.shape...  28 us
    ppermute x4, starting transfers between devices, send(): return jnp.moveaxis(lax.ppermute(moved, ('row', 'col'), pairs), -1, 0)  15.1 us
    ppermute x2, local copies, waits for them, and re-layouts, send(): return jnp.moveaxis(lax.ppermute(moved, ('row', 'col'), pairs), 0, carried)  12.6 us
    unnamed x28, local copies, waits for them, and re-layouts  12.3 us
    all_to_all x1, starting transfers between devices, broadcast_from_owners(): own_chunk = lax.all_to_all(chunks, axes, 0, 0, tiled=True).sum(axis=0)  11.4 us
    all_to_all x1, waiting for transfers between devices, broadcast_from_owners(): own_chunk = lax.all_to_all(chunks, axes, 0, 0, tiled=True).sum(axis=0)  10.4 us
    ppermute x4, starting transfers between devices, send(): return jnp.moveaxis(lax.ppermute(moved, ('row', 'col'), pairs), 0, carried)  10.2 us
    all_to_all x1, waiting for transfers between devices, broadcast_from_owners(): return lax.all_to_all(spread, axes, 0, 0, tiled=True).reshape(value.shape)  9.66 us
  transfers between devices with their start and end apart: 10, of which 3 were waited for; matrix products, arithmetic and copies ran while one was open for 24% of the time, Pallas kernels for 0%

profile of v2, /device:TPU:1, one launch (start us, length us, event | category | flops | bytes accessed | tf_op | source)
XLA Modules:
  0.0 175.6 jit_solution(233198876960079589)
XLA Ops:
  0.6 1.5 fusion.27
  2.2 1.3 slice_convert_fusion.3
  3.4 0.8 slice_bitcast_fusion.5
  4.3 0.8 maximum_bitcast_fusion.2
  5.1 1.3 collective-permute-start.3
  6.3 0.8 maximum_bitcast_fusion.3
  7.1 1.3 collective-permute-start.4
  8.4 0.8 maximum_bitcast_fusion.4
  9.2 6.0 %collective-permute-start.6 = (f32[3,3,129]{1,0,2:T(4,128)}, f32[3,3,129]{1,0,2:T(4,128)}, u32[]{:S(2)}, u32[]{:S(2)}) collective-permute-start(f32[3,3,129]{1,0,2:T(4,128)} %maximum_bitcast_fusion.4), channel_id=1, source_target_pairs={{16,1},{17,2},{18,3},{19,4},{20,5},{21,6},{22,7},{23,8},{24,9},{25... | collective-permute-start | bytes 13940 | tf_op jit(solution)/shard_map/ppermute | solution.py:27
  15.2 0.8 maximum_bitcast_fusion.5
  15.9 6.6 %collective-permute-start.7 = (f32[3,3,129]{1,0,2:T(4,128)}, f32[3,3,129]{1,0,2:T(4,128)}, u32[]{:S(2)}, u32[]{:S(2)}) collective-permute-start(f32[3,3,129]{1,0,2:T(4,128)} %maximum_bitcast_fusion.5), channel_id=1, source_target_pairs={{0,17},{1,18},{2,19},{3,20},{4,21},{5,22},{6,23},{7,24},{8,25},{9,... | collective-permute-start | bytes 13940 | tf_op jit(solution)/shard_map/ppermute | solution.py:27
  22.5 2.8 %fusion.26 = (f32[64,64,3]{2,1,0:T(8,128)}, f32[64,64,3]{2,1,0:T(8,128)}) fusion(f32[64,64,128]{2,1,0:T(8,128)S(1)} %copy-done), kind=kLoop, calls=%fused_computation.75 | loop fusion | bytes 196608 | tf_op jit(solution)/shard_map/slice | solution.py:167
  25.3 1.8 %fusion.29 = (bf16[64,64,3]{2,1,0:T(8,128)(2,1)}, bf16[64,64,3]{2,1,0:T(8,128)(2,1)}) fusion(bf16[64,64,128]{2,1,0:T(8,128)(2,1)S(1)} %copy-done.2), kind=kLoop, calls=%fused_computation.78 | loop fusion | bytes 98304 | tf_op jit(solution)/shard_map/slice | solution.py:168
  27.2 2.6 %copy.152 = f32[64,64,3]{0,1,2:T(8,128)S(1)} copy(f32[64,64,3]{2,1,0:T(8,128)} %get-tuple-element.28) | data formatting | bytes 98304
  29.8 2.4 %copy.153 = bf16[64,64,3]{0,1,2:T(8,128)(2,1)S(1)} copy(bf16[64,64,3]{2,1,0:T(8,128)(2,1)} %get-tuple-element.36) | data formatting | bytes 49152
  32.8 0.8 maximum_bitcast_fusion.7
  33.6 3.2 %collective-permute-start.5 = (f32[3,129,64]{1,2,0:T(8,128)}, f32[3,129,64]{1,2,0:T(8,128)}, u32[]{:S(2)}, u32[]{:S(2)}) collective-permute-start(f32[3,129,64]{1,2,0:T(8,128)} %maximum_bitcast_fusion.7), channel_id=1, source_target_pairs={{0,1},{1,2},{2,3},{3,4},{4,5},{5,6},{6,7},{7,8},{8,9},{9,10},{10,1... | collective-permute-start | bytes 297224 | tf_op jit(solution)/shard_map/ppermute | solution.py:25
  36.9 2.7 %copy.150 = f32[64,64,3]{0,1,2:T(8,128)S(1)} copy(f32[64,64,3]{2,1,0:T(8,128)} %get-tuple-element.27) | data formatting | bytes 98304
  39.6 1.3 copy.151
  41.7 0.7 and_convert_fusion.mask_ref
  42.6 1.3 collective-permute-start.2
  44.7 6.8 %copy.135 = f32[3,129,64]{0,2,1:T(8,128)} copy(f32[3,129,64]{1,2,0:T(8,128)} %collective-permute-done.5) | data formatting | bytes 198144 | tf_op jit(solution)/shard_map/ppermute | solution.py:25
  51.4 0.6 collective-permute-done.2
  52.0 2.7 %collective-permute-start = (f32[3,129,128]{2,0,1:T(4,128)S(1)}, f32[3,129,128]{2,0,1:T(4,128)S(1)}, u32[]{:S(2)}, u32[]{:S(2)}) collective-permute-start(f32[3,129,128]{2,0,1:T(4,128)S(1)} %maximum_bitcast_fusion), channel_id=1, source_target_pairs={{16,0},{17,1},{18,2},{19,3},{20,4},{21,5},{22,6},{23,7},{24,8},{25... | collective-permute-start | bytes 594440 | tf_op jit(solution)/shard_map/ppermute | solution.py:25
  54.7 5.9 %copy.130 = f32[3,129,64]{0,2,1:T(8,128)} copy(f32[3,129,64]{1,2,0:T(8,128)S(1)} %collective-permute-done.2) | data formatting | bytes 198144 | tf_op jit(solution)/shard_map/ppermute | solution.py:25
  60.6 3.0 %collective-permute-start.1 = (f32[3,129,128]{2,0,1:T(4,128)S(1)}, f32[3,129,128]{2,0,1:T(4,128)S(1)}, u32[]{:S(2)}, u32[]{:S(2)}) collective-permute-start(f32[3,129,128]{2,0,1:T(4,128)S(1)} %maximum_bitcast_fusion.1), channel_id=1, source_target_pairs={{0,16},{1,17},{2,18},{3,19},{4,20},{5,21},{6,22},{7,23},{8,24},{9,... | collective-permute-start | bytes 594440 | tf_op jit(solution)/shard_map/ppermute | solution.py:25
  63.7 7.3 %maximum_maximum_fusion.source_cols_ref.perm_cols_ref.head_cols_ref = f32[129,72,128]{2,1,0:T(8,128)} fusion(f32[129,3,3]{2,1,0:T(4,128)} %bitcast.23, f32[129,2,3]{2,1,0:T(2,128)S(1)} %broadcast_in_dim.86, f32[129,3,3]{2,1,0:T(4,128)} %bitcast.20, f32[129,64,3]{2,1,0:T(8,128)} %bitcast.70, f32[129,3,3]{2,1,0:T(4,128)} %bitcast.14, f32[129,3,3]{2,1,0:T(4,128)} %bitcast.11, ...), kind=kLoop, calls=%fused_computation.1 | loop fusion | flops 9510912 | bytes 4975784 | tf_op jit(solution)/shard_map/concatenate | solution.py:191
  70.9 0.9 pad_maximum_fusion.source_rows_ref.perm_rows_ref.head_rows_ref
  71.9 28.0 %shard_map.103 = (bf16[64,64,128]{2,1,0:T(8,128)(2,1)}, f32[64,64,128]{2,1,0:T(8,128)}) custom-call(f32[72,256]{1,0:T(8,128)} %and_convert_fusion.mask_ref, f32[64,128]{1,0:T(8,128)} %source_ref.1, f32[129,8,128]{2,1,0:T(8,128)} %pad_maximum_fusion.source_rows_ref.perm_rows_ref.head_rows_ref, ...), custom_call_target="tpu_custom_call" | custom-call | flops 94371840 | bytes 7340032 | tf_op jit(solution)/shard_map/pallas_call | solution.py:79
  99.9 3.8 %copy.149 = f32[64,64,128]{0,2,1:T(8,128)} copy(f32[64,64,128]{2,1,0:T(8,128)} %get-tuple-element.6) | data formatting | bytes 4194304 | tf_op jit(solution)/shard_map/reshape | solution.py:201
  103.7 5.0 %gather_fusion = f32[1024,64]{1,0:T(8,128)S(1)} fusion(f32[64,8192]{0,1:T(8,128)} %bitcast.72, s32[1024]{0:T(1024)S(1)} %broadcast_clamp_fusion), kind=kCustom, calls=%fused_computation | custom fusion | bytes 528384 | tf_op jit(solution)/shard_map/jit(_take)/gather | solution.py:201
  109.0 1.0 copy.138
  110.0 11.4 %all-to-all-start = ((f32[128,1,512]{2,1,0:T(1,128)}), f32[128,1,512]{2,1,0:T(1,128)S(1)}, u32[]{:S(2)}, u32[]{:S(2)}) async-start(f32[128,1,512]{2,1,0:T(1,128)} %copy.138), calls=%async_computation | async-start | bytes 524288 | tf_op jit(solution)/shard_map/all_to_all | solution.py:110
  122.1 10.4 %all-to-all-done = f32[128,1,512]{2,1,0:T(1,128)S(1)} async-done(((f32[128,1,512]{2,1,0:T(1,128)}), f32[128,1,512]{2,1,0:T(1,128)S(1)}, u32[]{:S(2)}, u32[]{:S(2)}) %all-to-all-start) | async-done | bytes 262176 | tf_op jit(solution)/shard_map/all_to_all | solution.py:110
  132.7 0.8 broadcast_in_dim.101
  133.6 4.3 %all-to-all-start.1 = ((f32[128,1,512]{2,1,0:T(1,128)}), f32[128,1,512]{2,1,0:T(1,128)S(1)}, u32[]{:S(2)}, u32[]{:S(2)}) async-start(f32[128,1,512]{2,1,0:T(1,128)} %broadcast_in_dim.101), calls=%async_computation.1 | async-start | bytes 524288 | tf_op jit(solution)/shard_map/all_to_all | solution.py:112
  137.8 1.6 subtract_multiply_fusion
  139.4 9.7 %all-to-all-done.1 = f32[128,1,512]{2,1,0:T(1,128)S(1)} async-done(((f32[128,1,512]{2,1,0:T(1,128)}), f32[128,1,512]{2,1,0:T(1,128)S(1)}, u32[]{:S(2)}, u32[]{:S(2)}) %all-to-all-start.1) | async-done | bytes 262176 | tf_op jit(solution)/shard_map/all_to_all | solution.py:112
  149.1 0.6 reduce.7
  149.8 0.6 copy-done.4
  151.0 1.6 fusion.25
  153.2 5.8 %cholesky.17 = f32[64,64]{1,0:T(8,128)S(1)} custom-call(f32[64,64]{1,0:T(8,128)S(1)} %fusion.21), custom_call_target="Cholesky" | custom-call | tf_op jit(solution)/shard_map/jit(cholesky)/cholesky | solution.py:142
  159.1 0.7 compare_reduce_fusion
  159.8 0.6 fusion.16
  160.5 4.9 %custom-call.8 = f32[1,64,64]{1,2,0:T(8,128)S(1)} custom-call(f32[1,64,64]{2,1,0:T(8,128)S(1)} %fusion.16), custom_call_target="InvertDiagBlocksLowerTriangular" | custom-call | tf_op jit(solution)/shard_map/triangular_solve | solution.py:144
  165.4 1.5 fusion.4
  167.4 5.7 %copy_add_fusion = f32[64,64,128]{2,0,1:T(8,128)S(1)} fusion(f32[64,64,128]{2,1,0:T(8,128)S(1)} %copy-done.1, f32[64,64,1]{0,1,2:T(8,128)S(1)} %convolution_bitcast_fusion, f32[64,64,128]{2,1,0:T(8,128)} %subtract_multiply_fusion), kind=kOutput, calls=%fused_computation.2 | convolution fusion | flops 403177472 | bytes 6307840 | tf_op jit(solution)/shard_map/mrc,mn->nrc/dot_general | solution.py:211
  173.1 2.5 %copy.143 = f32[64,64,128]{2,1,0:T(8,128)} copy(f32[64,64,128]{2,0,1:T(8,128)S(1)} %copy_add_fusion) | data formatting | bytes 4194304
  (81 shorter events, 5.3 us)
Async XLA Ops:
  0.6 21.9 %copy-start = (f32[64,64,128]{2,1,0:T(8,128)S(1)}, f32[64,64,128]{2,1,0:T(8,128)}, u32[]{:S(2)}) copy-start(f32[64,64,128]{2,1,0:T(8,128)} %perm_ref.1) | copy-start | bytes 6291460
  5.1 55.6 %collective-permute-start.3 = (f32[3,3,129]{1,0,2:T(4,128)}, f32[3,3,129]{1,0,2:T(4,128)}, u32[]{:S(2)}, u32[]{:S(2)}) collective-permute-start(f32[3,3,129]{1,0,2:T(4,128)} %maximum_bitcast_fusion.2), channel_id=1, source_target_pairs={{17,0},{18,1},{19,2},{20,3},{21,4},{22,5},{23,6},{24,7},{25,8},{26... | collective-permute-start | bytes 13940 | tf_op jit(solution)/shard_map/ppermute | solution.py:27
  7.1 56.5 %collective-permute-start.4 = (f32[3,3,129]{1,0,2:T(4,128)}, f32[3,3,129]{1,0,2:T(4,128)}, u32[]{:S(2)}, u32[]{:S(2)}) collective-permute-start(f32[3,3,129]{1,0,2:T(4,128)} %maximum_bitcast_fusion.3), channel_id=1, source_target_pairs={{1,16},{2,17},{3,18},{4,19},{5,20},{6,21},{7,22},{8,23},{9,24},{10... | collective-permute-start | bytes 13940 | tf_op jit(solution)/shard_map/ppermute | solution.py:27
  9.2 54.4 %collective-permute-start.6 = (f32[3,3,129]{1,0,2:T(4,128)}, f32[3,3,129]{1,0,2:T(4,128)}, u32[]{:S(2)}, u32[]{:S(2)}) collective-permute-start(f32[3,3,129]{1,0,2:T(4,128)} %maximum_bitcast_fusion.4), channel_id=1, source_target_pairs={{16,1},{17,2},{18,3},{19,4},{20,5},{21,6},{22,7},{23,8},{24,9},{25... | collective-permute-start | bytes 13940 | tf_op jit(solution)/shard_map/ppermute | solution.py:27
  15.9 9.3 %copy-start.2 = (bf16[64,64,128]{2,1,0:T(8,128)(2,1)S(1)}, bf16[64,64,128]{2,1,0:T(8,128)(2,1)}, u32[]{:S(2)}) copy-start(bf16[64,64,128]{2,1,0:T(8,128)(2,1)} %head_ref.1) | copy-start | bytes 3145732
  15.9 47.7 %collective-permute-start.7 = (f32[3,3,129]{1,0,2:T(4,128)}, f32[3,3,129]{1,0,2:T(4,128)}, u32[]{:S(2)}, u32[]{:S(2)}) collective-permute-start(f32[3,3,129]{1,0,2:T(4,128)} %maximum_bitcast_fusion.5), channel_id=1, source_target_pairs={{0,17},{1,18},{2,19},{3,20},{4,21},{5,22},{6,23},{7,24},{8,25},{9,... | collective-permute-start | bytes 13940 | tf_op jit(solution)/shard_map/ppermute | solution.py:27
  25.3 1.8 %copy-start.5 = (f32[64,128]{1,0:T(8,128)S(1)}, f32[64,128]{1,0:T(8,128)}, u32[]{:S(2)}) copy-start(f32[64,128]{1,0:T(8,128)} %source_ref.1) | copy-start | bytes 98308
  33.6 9.1 %collective-permute-start.5 = (f32[3,129,64]{1,2,0:T(8,128)}, f32[3,129,64]{1,2,0:T(8,128)}, u32[]{:S(2)}, u32[]{:S(2)}) collective-permute-start(f32[3,129,64]{1,2,0:T(8,128)} %maximum_bitcast_fusion.7), channel_id=1, source_target_pairs={{0,1},{1,2},{2,3},{3,4},{4,5},{5,6},{6,7},{7,8},{8,9},{9,10},{10,1... | collective-permute-start | bytes 297224 | tf_op jit(solution)/shard_map/ppermute | solution.py:25
  36.8 2.8 %copy-start.3 = (bf16[64,64,3]{2,1,0:T(8,128)(2,1)S(1)}, bf16[64,64,3]{2,1,0:T(8,128)(2,1)}, u32[]{:S(2)}) copy-start(bf16[64,64,3]{2,1,0:T(8,128)(2,1)} %get-tuple-element.35) | copy-start | bytes 73732
  36.8 4.6 %copy-start.6 = (s32[4,256]{1,0:T(4,128)S(1)}, s32[4,256]{1,0:T(4,128)}, u32[]{:S(2)}) copy-start(s32[4,256]{1,0:T(4,128)} %param.11) | copy-start | bytes 12292
  36.8 4.7 %copy-start.9 = (s32[4]{0:T(128)S(1)}, s32[4]{0:T(128)}, u32[]{:S(2)}) copy-start(s32[4]{0:T(128)} %param.12) | copy-start | bytes 52
  42.6 9.4 %collective-permute-start.2 = (f32[3,129,64]{1,2,0:T(8,128)S(1)}, f32[3,129,64]{1,2,0:T(8,128)S(1)}, u32[]{:S(2)}, u32[]{:S(2)}) collective-permute-start(f32[3,129,64]{1,2,0:T(8,128)S(1)} %maximum_bitcast_fusion.6), channel_id=1, source_target_pairs={{1,0},{2,1},{3,2},{4,3},{5,4},{6,5},{7,6},{8,7},{9,8},{10,9},{11,1... | collective-permute-start | bytes 297224 | tf_op jit(solution)/shard_map/ppermute | solution.py:25
  52.0 18.9 %collective-permute-start = (f32[3,129,128]{2,0,1:T(4,128)S(1)}, f32[3,129,128]{2,0,1:T(4,128)S(1)}, u32[]{:S(2)}, u32[]{:S(2)}) collective-permute-start(f32[3,129,128]{2,0,1:T(4,128)S(1)} %maximum_bitcast_fusion), channel_id=1, source_target_pairs={{16,0},{17,1},{18,2},{19,3},{20,4},{21,5},{22,6},{23,7},{24,8},{25... | collective-permute-start | bytes 594440 | tf_op jit(solution)/shard_map/ppermute | solution.py:25
  60.6 10.3 %collective-permute-start.1 = (f32[3,129,128]{2,0,1:T(4,128)S(1)}, f32[3,129,128]{2,0,1:T(4,128)S(1)}, u32[]{:S(2)}, u32[]{:S(2)}) collective-permute-start(f32[3,129,128]{2,0,1:T(4,128)S(1)} %maximum_bitcast_fusion.1), channel_id=1, source_target_pairs={{0,16},{1,17},{2,18},{3,19},{4,20},{5,21},{6,22},{7,23},{8,24},{9,... | collective-permute-start | bytes 594440 | tf_op jit(solution)/shard_map/ppermute | solution.py:25
  108.7 12.7 %copy-start.7 = (f32[1024]{0:T(1024)S(1)}, f32[1024]{0:T(1024)}, u32[]{:S(2)}) copy-start(f32[1024]{0:T(1024)} %param.14) | copy-start | bytes 12292
  108.7 12.7 %copy-start.1 = (f32[64,64,128]{2,1,0:T(8,128)S(1)}, f32[64,64,128]{2,1,0:T(8,128)}, u32[]{:S(2)}) copy-start(f32[64,64,128]{2,1,0:T(8,128)} %perm_ref.1) | copy-start | bytes 6291460
  110.0 22.5 %all-to-all-start = ((f32[128,1,512]{2,1,0:T(1,128)}), f32[128,1,512]{2,1,0:T(1,128)S(1)}, u32[]{:S(2)}, u32[]{:S(2)}) async-start(f32[128,1,512]{2,1,0:T(1,128)} %copy.138), calls=%async_computation | async-start | bytes 524288 | tf_op jit(solution)/shard_map/all_to_all | solution.py:110
  133.6 15.5 %all-to-all-start.1 = ((f32[128,1,512]{2,1,0:T(1,128)}), f32[128,1,512]{2,1,0:T(1,128)S(1)}, u32[]{:S(2)}, u32[]{:S(2)}) async-start(f32[128,1,512]{2,1,0:T(1,128)} %broadcast_in_dim.101), calls=%async_computation.1 | async-start | bytes 524288 | tf_op jit(solution)/shard_map/all_to_all | solution.py:112
  149.8 0.7 copy-start.4
  149.8 15.6 %copy-start.8 = (f32[1024]{0:T(1024)S(1)}, f32[1024]{0:T(1024)}, u32[]{:S(2)}) copy-start(f32[1024]{0:T(1024)} %param.13) | copy-start | bytes 12292

commit v3 on v1

--- a/solution.py
+++ b/solution.py
@@ -188,8 +188,7 @@
         inside.astype(f32), recharge, halo_rows, halo_cols, logarithmic_conductivity, starting_head, 8
     )
     group_total, well_count = well_cells.shape
-    wells = well_cells.reshape(-1)
-    local_data = hydraulic_head[:, wells // col_count, wells % col_count]
+    local_data = jnp.take(hydraulic_head.reshape(member_count, row_count * col_count), well_cells.reshape(-1), axis=1)
     me = lax.axis_index("row") * lax.axis_size("col") + lax.axis_index("col")
     mine = jnp.repeat(well_owner == me, well_count)
     local_data = jnp.where(mine[None, :], local_data, 0.0)

time: 160 us -> 155 us (0.969)
  local copies, waits for them, and re-layouts: 42.8 us -> 38.3 us
    gather x3, local copies, waits for them, and re-layouts: 10.8 us -> 5.21 us  [per_device(): jnp.take(hydraulic_head.reshape(member_count, row_count * col_count), wel...]
    reshape x0 -> x2, local copies, waits for them, and re-layouts: none -> 3.84 us  [the longest x1 3.82 us: per_device(): hydraulic_head.reshape(member_count, row_count * col_count)]
    pallas_call x1 -> x0, local copies, waits for them, and re-layouts: 3.82 us -> none  [run_stencil(): pl.pallas_call(stencil_kernel, grid=(blocks,), in_specs=[full2(mask.shape...]
    unnamed x26 -> x28, local copies, waits for them, and re-layouts: 8.52 us -> 8.65 us
  transfers between devices with their start and end apart: 6 -> 6, of which waited for: 4 -> 4; matrix products, arithmetic and copies ran while one was open for 12% -> 14% of each run, Pallas kernels for 0% -> 0%
where the time goes in v3:
time: 155 us
  local copies, waits for them, and re-layouts  38.3 us (25%)
  other arithmetic  28.5 us (18%)
  Pallas kernels  28 us (18%)
  starting transfers between devices  27.3 us (18%)
  waiting for transfers between devices  23.5 us (15%)
  matrix products  8.05 us (5%)
    pallas_call x1, Pallas kernels, run_stencil(): pl.pallas_call(stencil_kernel, grid=(blocks,), in_specs=[full2(mask.shape...  28 us
    all_to_all x1, starting transfers between devices, broadcast_from_owners(): own_chunk = lax.all_to_all(chunks, axes, 0, 0, tiled=True).sum(axis=0)  11.5 us
    ppermute x4, starting transfers between devices, send(): return lax.ppermute(piece, axis, pairs)  11.5 us
    all_to_all x1, waiting for transfers between devices, broadcast_from_owners(): own_chunk = lax.all_to_all(chunks, axes, 0, 0, tiled=True).sum(axis=0)  10.4 us
    all_to_all x1, waiting for transfers between devices, broadcast_from_owners(): return lax.all_to_all(spread, axes, 0, 0, tiled=True).reshape(value.shape)  9.47 us
    unnamed x28, local copies, waits for them, and re-layouts  8.65 us
    concatenate x1, other arithmetic, per_device(): jnp.concatenate([from_right, jnp.zeros((stacked_total, ext_rows, col_coun...  7.23 us
    another operation x3, other arithmetic, blending_weights(): factor = jnp.linalg.cholesky(system)  6.55 us
  transfers between devices with their start and end apart: 6, of which 4 were waited for; matrix products, arithmetic and copies ran while one was open for 14% of the time, Pallas kernels for 0%

profile of v3, /device:TPU:1, one launch (start us, length us, event | category | flops | bytes accessed | tf_op | source)
XLA Modules:
  0.0 154.7 jit_solution(11685767457594693506)
XLA Ops:
  0.6 1.1 fusion.27
  1.7 1.0 slice_convert_fusion.1
  2.7 0.7 slice_bitcast_fusion.3
  3.4 0.8 maximum_bitcast_fusion
  4.2 3.3 %collective-permute-start = (f32[3,129,128]{2,0,1:T(4,128)}, f32[3,129,128]{2,0,1:T(4,128)}, u32[]{:S(2)}, u32[]{:S(2)}) collective-permute-start(f32[3,129,128]{2,0,1:T(4,128)} %maximum_bitcast_fusion), channel_id=1, source_target_pairs={{16,0},{32,16},{48,32},{64,48},{80,64},{96,80},{112,96},{17,1},{33... | collective-permute-start | bytes 594440 | tf_op jit(solution)/shard_map/ppermute | solution.py:21
  7.5 0.8 maximum_bitcast_fusion.1
  8.3 3.7 %collective-permute-start.1 = (f32[3,129,128]{2,0,1:T(4,128)}, f32[3,129,128]{2,0,1:T(4,128)}, u32[]{:S(2)}, u32[]{:S(2)}) collective-permute-start(f32[3,129,128]{2,0,1:T(4,128)} %maximum_bitcast_fusion.1), channel_id=1, source_target_pairs={{0,16},{16,32},{32,48},{48,64},{64,80},{80,96},{96,112},{1,17},{17... | collective-permute-start | bytes 594440 | tf_op jit(solution)/shard_map/ppermute | solution.py:21
  12.0 5.0 %fusion.26 = (f32[64,64,3]{2,1,0:T(8,128)}, f32[64,64,3]{2,1,0:T(8,128)}) fusion(f32[64,64,128]{2,1,0:T(8,128)} %perm_ref.1), kind=kLoop, calls=%fused_computation.63 | loop fusion | bytes 196608 | tf_op jit(solution)/shard_map/slice | solution.py:174
  17.0 1.5 fusion.28
  18.6 2.4 %copy.92 = f32[64,64,3]{1,0,2:T(8,128)S(1)} copy(f32[64,64,3]{2,1,0:T(8,128)} %get-tuple-element.25) | data formatting | bytes 98304
  21.0 1.7 %copy.93 = bf16[64,64,3]{1,0,2:T(8,128)(2,1)S(1)} copy(bf16[64,64,3]{2,1,0:T(8,128)(2,1)} %get-tuple-element.29) | data formatting | bytes 49152
  22.8 0.7 copy.90
  23.5 0.5 copy.91
  24.4 0.7 and_convert_fusion.mask_ref
  25.2 1.2 pad_maximum_fusion.1.source_rows_ref.perm_rows_ref.head_rows_ref
  26.5 0.9 copy.74
  27.6 3.2 %collective-permute-start.3 = (f32[3,129,72]{2,1,0:T(8,128)S(1)}, f32[3,129,72]{2,1,0:T(8,128)S(1)}, u32[]{:S(2)}, u32[]{:S(2)}) collective-permute-start(f32[3,129,72]{2,1,0:T(8,128)S(1)} %maximum_bitcast_fusion.3), channel_id=1, source_target_pairs={{0,1},{1,2},{2,3},{3,4},{4,5},{5,6},{6,7},{7,8},{8,9},{9,10},{10,1... | collective-permute-start | bytes 334376 | tf_op jit(solution)/shard_map/ppermute | solution.py:21
  30.8 0.9 copy.68
  31.8 1.3 collective-permute-start.2
  33.8 1.9 %collective-permute-done.3 = f32[3,129,72]{2,1,0:T(8,128)S(1)} collective-permute-done((f32[3,129,72]{2,1,0:T(8,128)S(1)}, f32[3,129,72]{2,1,0:T(8,128)S(1)}, u32[]{:S(2)}, u32[]{:S(2)}) %collective-permute-start.3) | collective-permute-done | bytes 111488 | tf_op jit(solution)/shard_map/ppermute | solution.py:21
  35.6 3.2 %copy.75 = f32[3,129,72]{0,2,1:T(8,128)} copy(f32[3,129,72]{2,1,0:T(8,128)S(1)} %collective-permute-done.3) | data formatting | bytes 222912 | tf_op jit(solution)/shard_map/ppermute | solution.py:21
  38.8 1.7 %collective-permute-done.2 = f32[3,129,72]{2,1,0:T(8,128)S(1)} collective-permute-done((f32[3,129,72]{2,1,0:T(8,128)S(1)}, f32[3,129,72]{2,1,0:T(8,128)S(1)}, u32[]{:S(2)}, u32[]{:S(2)}) %collective-permute-start.2) | collective-permute-done | bytes 111488 | tf_op jit(solution)/shard_map/ppermute | solution.py:21
  40.5 3.2 %copy.69 = f32[3,129,72]{0,2,1:T(8,128)} copy(f32[3,129,72]{2,1,0:T(8,128)S(1)} %collective-permute-done.2) | data formatting | bytes 222912 | tf_op jit(solution)/shard_map/ppermute | solution.py:21
  43.6 7.2 %pad_maximum_fusion.source_cols_ref.perm_cols_ref.head_cols_ref = f32[129,72,128]{2,1,0:T(8,128)} fusion(f32[129,72,3]{2,1,0:T(8,128)} %bitcast.50, f32[129,72,3]{2,1,0:T(8,128)} %bitcast.51, f32[128]{0:T(128)S(1)} %pad.1.clone), kind=kLoop, calls=%fused_computation.1 | loop fusion | flops 2377728 | bytes 4978880 | tf_op jit(solution)/shard_map/concatenate | solution.py:181
  50.9 28.0 %shard_map.103 = (bf16[64,64,128]{2,1,0:T(8,128)(2,1)}, f32[64,64,128]{2,1,0:T(8,128)}) custom-call(f32[72,256]{1,0:T(8,128)} %and_convert_fusion.mask_ref, f32[64,128]{1,0:T(8,128)} %source_ref.1, f32[129,8,128]{2,1,0:T(8,128)} %copy-done.1, f32[129,72,128]{2,1,0:T(8,128)} %pad_maximum_fusion.source_cols_ref.perm_cols_ref.head_cols_ref, ...), custom_call_target="tpu_custom_call" | custom-call | flops 94371840 | bytes 7340032 | tf_op jit(solution)/shard_map/pallas_call | solution.py:73
  78.9 3.8 %copy.89 = f32[64,64,128]{0,2,1:T(8,128)} copy(f32[64,64,128]{2,1,0:T(8,128)} %get-tuple-element.6) | data formatting | bytes 4194304 | tf_op jit(solution)/shard_map/reshape | solution.py:191
  82.7 5.0 %gather_fusion = f32[1024,64]{1,0:T(8,128)S(1)} fusion(f32[64,8192]{0,1:T(8,128)} %bitcast.52, s32[1024]{0:T(1024)S(1)} %broadcast_clamp_fusion), kind=kCustom, calls=%fused_computation | custom fusion | bytes 528384 | tf_op jit(solution)/shard_map/jit(_take)/gather | solution.py:191
  88.0 1.0 copy.78
  89.0 11.5 %all-to-all-start = ((f32[128,1,512]{2,1,0:T(1,128)}), f32[128,1,512]{2,1,0:T(1,128)S(1)}, u32[]{:S(2)}, u32[]{:S(2)}) async-start(f32[128,1,512]{2,1,0:T(1,128)} %copy.78), calls=%async_computation | async-start | bytes 524288 | tf_op jit(solution)/shard_map/all_to_all | solution.py:104
  100.8 0.4 div.70
  101.2 10.4 %all-to-all-done = f32[128,1,512]{2,1,0:T(1,128)S(1)} async-done(((f32[128,1,512]{2,1,0:T(1,128)}), f32[128,1,512]{2,1,0:T(1,128)S(1)}, u32[]{:S(2)}, u32[]{:S(2)}) %all-to-all-start) | async-done | bytes 262176 | tf_op jit(solution)/shard_map/all_to_all | solution.py:104
  111.9 0.8 broadcast_in_dim.81
  112.7 4.3 %all-to-all-start.1 = ((f32[128,1,512]{2,1,0:T(1,128)}), f32[128,1,512]{2,1,0:T(1,128)S(1)}, u32[]{:S(2)}, u32[]{:S(2)}) async-start(f32[128,1,512]{2,1,0:T(1,128)} %broadcast_in_dim.81), calls=%async_computation.1 | async-start | bytes 524288 | tf_op jit(solution)/shard_map/all_to_all | solution.py:106
  117.0 1.7 %subtract_multiply_fusion = f32[64,64,128]{2,1,0:T(8,128)} fusion(f32[64,64,128]{2,1,0:T(8,128)S(1)} %copy-done, f32[64,128]{1,0:T(8,128)S(1)} %broadcast_multiply_fusion), kind=kLoop, calls=%fused_computation.5 | loop fusion | flops 1048576 | bytes 4227072 | tf_op jit(solution)/shard_map/div | solution.py:198
  118.7 9.5 %all-to-all-done.1 = f32[128,1,512]{2,1,0:T(1,128)S(1)} async-done(((f32[128,1,512]{2,1,0:T(1,128)}), f32[128,1,512]{2,1,0:T(1,128)S(1)}, u32[]{:S(2)}, u32[]{:S(2)}) %all-to-all-start.1) | async-done | bytes 262176 | tf_op jit(solution)/shard_map/all_to_all | solution.py:106
  128.2 0.6 reduce.7
  129.0 0.6 copy-done.4
  129.7 0.4 sub.44
  130.1 1.6 %fusion.25 = (f32[128,512]{1,0:T(8,128)S(1)}, f32[128,512]{1,0:T(8,128)S(1)}) fusion(f32[128,1,512]{2,1,0:T(1,128)S(1)} %all-to-all-done.1, f32[128,1,512]{2,1,0:T(1,128)S(1)} %sub.44, f32[128,1,512]{2,1,0:T(1,128)S(1)} %div.70), kind=kLoop, calls=%fused_computation.62 | loop fusion | flops 196608 | bytes 1310720 | tf_op jit(solution)/shard_map/div | solution.py:129
  131.9 0.4 fusion.30
  132.4 5.8 %cholesky.17 = f32[64,64]{1,0:T(8,128)S(1)} custom-call(f32[64,64]{1,0:T(8,128)S(1)} %fusion.21), custom_call_target="Cholesky" | custom-call | tf_op jit(solution)/shard_map/jit(cholesky)/cholesky | solution.py:136
  138.3 0.7 compare_reduce_fusion
  138.9 0.6 fusion.16
  139.6 4.9 %custom-call.8 = f32[1,64,64]{1,2,0:T(8,128)S(1)} custom-call(f32[1,64,64]{2,1,0:T(8,128)S(1)} %fusion.16), custom_call_target="InvertDiagBlocksLowerTriangular" | custom-call | tf_op jit(solution)/shard_map/triangular_solve | solution.py:138
  144.5 1.5 fusion.4
  146.3 0.2 convolution_bitcast_fusion
  146.5 5.7 %copy_add_fusion = f32[64,64,128]{2,0,1:T(8,128)S(1)} fusion(f32[64,64,128]{2,1,0:T(8,128)S(1)} %copy-done, f32[64,64,1]{0,1,2:T(8,128)S(1)} %convolution_bitcast_fusion, f32[64,64,128]{2,1,0:T(8,128)} %subtract_multiply_fusion), kind=kOutput, calls=%fused_computation.2 | convolution fusion | flops 403177472 | bytes 6307840 | tf_op jit(solution)/shard_map/mrc,mn->nrc/dot_general | solution.py:201
  152.2 2.5 %copy.83 = f32[64,64,128]{2,1,0:T(8,128)} copy(f32[64,64,128]{2,0,1:T(8,128)S(1)} %copy_add_fusion) | data formatting | bytes 4194304
  (68 shorter events, 3.1 us)
Async XLA Ops:
  4.2 20.9 %collective-permute-start = (f32[3,129,128]{2,0,1:T(4,128)}, f32[3,129,128]{2,0,1:T(4,128)}, u32[]{:S(2)}, u32[]{:S(2)}) collective-permute-start(f32[3,129,128]{2,0,1:T(4,128)} %maximum_bitcast_fusion), channel_id=1, source_target_pairs={{16,0},{32,16},{48,32},{64,48},{80,64},{96,80},{112,96},{17,1},{33... | collective-permute-start | bytes 594440 | tf_op jit(solution)/shard_map/ppermute | solution.py:21
  8.3 8.7 %copy-start.2 = (bf16[64,64,128]{2,1,0:T(8,128)(2,1)S(1)}, bf16[64,64,128]{2,1,0:T(8,128)(2,1)}, u32[]{:S(2)}) copy-start(bf16[64,64,128]{2,1,0:T(8,128)(2,1)} %head_ref.1) | copy-start | bytes 3145732
  8.3 16.9 %collective-permute-start.1 = (f32[3,129,128]{2,0,1:T(4,128)}, f32[3,129,128]{2,0,1:T(4,128)}, u32[]{:S(2)}, u32[]{:S(2)}) collective-permute-start(f32[3,129,128]{2,0,1:T(4,128)} %maximum_bitcast_fusion.1), channel_id=1, source_target_pairs={{0,16},{16,32},{32,48},{48,64},{64,80},{80,96},{96,112},{1,17},{17... | collective-permute-start | bytes 594440 | tf_op jit(solution)/shard_map/ppermute | solution.py:21
  17.0 1.5 copy-start.5
  18.5 4.3 %copy-start.3 = (f32[64,64,3]{2,1,0:T(8,128)S(1)}, f32[64,64,3]{2,1,0:T(8,128)}, u32[]{:S(2)}) copy-start(f32[64,64,3]{2,1,0:T(8,128)} %get-tuple-element.24) | copy-start | bytes 147460
  22.7 1.5 copy-start.6
  22.7 1.5 copy-start.9
  26.3 5.3 %copy-start.1 = (f32[129,8,128]{2,1,0:T(8,128)}, f32[129,8,128]{2,1,0:T(8,128)S(1)}, u32[]{:S(2)}) copy-start(f32[129,8,128]{2,1,0:T(8,128)S(1)} %pad_maximum_fusion.1.source_rows_ref.perm_rows_ref.head_rows_ref) | copy-start | bytes 1585156
  27.6 8.0 %collective-permute-start.3 = (f32[3,129,72]{2,1,0:T(8,128)S(1)}, f32[3,129,72]{2,1,0:T(8,128)S(1)}, u32[]{:S(2)}, u32[]{:S(2)}) collective-permute-start(f32[3,129,72]{2,1,0:T(8,128)S(1)} %maximum_bitcast_fusion.3), channel_id=1, source_target_pairs={{0,1},{1,2},{2,3},{3,4},{4,5},{5,6},{6,7},{7,8},{8,9},{9,10},{10,1... | collective-permute-start | bytes 334376 | tf_op jit(solution)/shard_map/ppermute | solution.py:21
  31.8 8.7 %collective-permute-start.2 = (f32[3,129,72]{2,1,0:T(8,128)S(1)}, f32[3,129,72]{2,1,0:T(8,128)S(1)}, u32[]{:S(2)}, u32[]{:S(2)}) collective-permute-start(f32[3,129,72]{2,1,0:T(8,128)S(1)} %maximum_bitcast_fusion.2), channel_id=1, source_target_pairs={{1,0},{2,1},{3,2},{4,3},{5,4},{6,5},{7,6},{8,7},{9,8},{10,9},{11,1... | collective-permute-start | bytes 334376 | tf_op jit(solution)/shard_map/ppermute | solution.py:21
  87.7 12.8 %copy-start.7 = (f32[1024]{0:T(1024)S(1)}, f32[1024]{0:T(1024)}, u32[]{:S(2)}) copy-start(f32[1024]{0:T(1024)} %param.14) | copy-start | bytes 12292
  87.7 12.9 %copy-start = (f32[64,64,128]{2,1,0:T(8,128)S(1)}, f32[64,64,128]{2,1,0:T(8,128)}, u32[]{:S(2)}) copy-start(f32[64,64,128]{2,1,0:T(8,128)} %perm_ref.1) | copy-start | bytes 6291460
  89.0 22.7 %all-to-all-start = ((f32[128,1,512]{2,1,0:T(1,128)}), f32[128,1,512]{2,1,0:T(1,128)S(1)}, u32[]{:S(2)}, u32[]{:S(2)}) async-start(f32[128,1,512]{2,1,0:T(1,128)} %copy.78), calls=%async_computation | async-start | bytes 524288 | tf_op jit(solution)/shard_map/all_to_all | solution.py:104
  112.7 15.5 %all-to-all-start.1 = ((f32[128,1,512]{2,1,0:T(1,128)}), f32[128,1,512]{2,1,0:T(1,128)S(1)}, u32[]{:S(2)}, u32[]{:S(2)}) async-start(f32[128,1,512]{2,1,0:T(1,128)} %broadcast_in_dim.81), calls=%async_computation.1 | async-start | bytes 524288 | tf_op jit(solution)/shard_map/all_to_all | solution.py:106
  128.9 0.7 copy-start.4
  128.9 15.5 %copy-start.8 = (f32[1024]{0:T(1024)S(1)}, f32[1024]{0:T(1024)}, u32[]{:S(2)}) copy-start(f32[1024]{0:T(1024)} %param.13) | copy-start | bytes 12292

commit v4 on v3

--- a/solution.py
+++ b/solution.py
@@ -123,6 +123,35 @@
     return centre_press + time_step * (flux_total + source)
 
 
+def update_kernel(mix_t_ref, perm_ref, out_ref):
+    members = mix_t_ref.shape[0]
+    rows = perm_ref.shape[0] // members
+    mix_t = mix_t_ref[...]
+    spread = math.sqrt(members - 1)
+
+    def body(r, carry):
+        values = perm_ref[pl.ds(r, members, stride=rows)]
+        anomalies = (values - jnp.mean(values, axis=0, keepdims=True)) / spread
+        shift = jnp.dot(mix_t, anomalies, precision=lax.Precision.HIGHEST, preferred_element_type=jnp.float32)
+        out_ref[pl.ds(r, members, stride=rows)] = values + shift
+        return carry
+
+    lax.fori_loop(0, rows, body, 0)
+
+
+def run_update(perm, mixing):
+    members, rows, cols = perm.shape
+    flat = perm.reshape(members * rows, cols)
+    out = pl.pallas_call(
+        update_kernel,
+        out_shape=jax.ShapeDtypeStruct(flat.shape, jnp.float32),
+        cost_estimate=pl.CostEstimate(
+            flops=2 * members * members * rows * cols, transcendentals=0, bytes_accessed=8 * members * rows * cols
+        ),
+    )(mixing.T, flat)
+    return out.reshape(perm.shape)
+
+
 def blending_weights(predicted, observed, obs_var, perturb):
     member_count = predicted.shape[0]
     ensemble_spread = math.sqrt(member_count - 1)
@@ -194,13 +223,7 @@
     local_data = jnp.where(mine[None, :], local_data, 0.0)
     predicted = broadcast_from_owners(local_data, ("row", "col"))
     mixing = blending_weights(predicted, observed, obs_var, perturb)
-    ensemble_spread = math.sqrt(member_count - 1)
-    anomalies = (
-        logarithmic_conductivity - jnp.mean(logarithmic_conductivity, axis=0, keepdims=True)
-    ) / ensemble_spread
-    updated_perm = logarithmic_conductivity + jnp.einsum(
-        "mrc,mn->nrc", anomalies, mixing, precision=lax.Precision.HIGHEST
-    )
+    updated_perm = run_update(logarithmic_conductivity, mixing)
     return (pressure_low, predicted, updated_perm)
 
 

time: 155 us -> 162 us (1.045)
  blocking collectives: 0 us -> 22.5 us
  Pallas kernels: 28 us -> 45.9 us
  starting transfers between devices: 27.3 us -> 15.7 us
  waiting for transfers between devices: 23.5 us -> 14.2 us
  matrix products: 8.05 us -> 1.83 us
  local copies, waits for them, and re-layouts: 38.3 us -> 33.6 us
  other arithmetic: 28.5 us -> 26.6 us
    all_to_all x0 -> x1, blocking collectives: none -> 22.5 us  [broadcast_from_owners(): own_chunk = lax.all_to_all(chunks, axes, 0, 0, tiled=True).sum(axis=0)]
    pallas_call x0 -> x1, Pallas kernels: none -> 17.9 us  [run_update(): pl.pallas_call(update_kernel, out_shape=jax.ShapeDtypeStruct(flat.shape,...]
    all_to_all x1 -> x0, starting transfers between devices: 11.5 us -> none  [broadcast_from_owners(): own_chunk = lax.all_to_all(chunks, axes, 0, 0, tiled=True).sum(axis=0)]
    all_to_all x1 -> x0, waiting for transfers between devices: 10.4 us -> none  [broadcast_from_owners(): own_chunk = lax.all_to_all(chunks, axes, 0, 0, tiled=True).sum(axis=0)]
    dot_general x1 -> x0, matrix products: 5.69 us -> none  [per_device(): jnp.einsum('mrc,mn->nrc', anomalies, mixing, precision=lax.Precision.HIGH...]
    unnamed x28 -> x25, local copies, waits for them, and re-layouts: 8.65 us -> 5.35 us
    div x2 -> x0, other arithmetic: 1.74 us -> none  [the longest x1 1.74 us: per_device(): (logarithmic_conductivity - jnp.mean(logarithmic_conductivity, axis=0, ke...]
  transfers between devices with their start and end apart: 6 -> 5, of which waited for: 4 -> 3; matrix products, arithmetic and copies ran while one was open for 14% -> 11% of each run, Pallas kernels for 0% -> 0%
where the time goes in v4:
time: 162 us; the launch traced here: 161 us
  Pallas kernels  45.9 us (28%)
  local copies, waits for them, and re-layouts  33.6 us (21%)
  other arithmetic  26.6 us (16%)
  blocking collectives  22.5 us (14%)
  starting transfers between devices  15.7 us (10%)
  waiting for transfers between devices  14.2 us (9%)
  matrix products  1.83 us (1%)
    pallas_call x1, Pallas kernels, run_stencil(): pl.pallas_call(stencil_kernel, grid=(blocks,), in_specs=[full2(mask.shape...  28 us
    all_to_all x1, blocking collectives, broadcast_from_owners(): own_chunk = lax.all_to_all(chunks, axes, 0, 0, tiled=True).sum(axis=0)  22.5 us
    pallas_call x1, Pallas kernels, run_update(): pl.pallas_call(update_kernel, out_shape=jax.ShapeDtypeStruct(flat.shape,...  17.9 us
    ppermute x4, starting transfers between devices, send(): return lax.ppermute(piece, axis, pairs)  11.5 us
    all_to_all x1, waiting for transfers between devices, broadcast_from_owners(): return lax.all_to_all(spread, axes, 0, 0, tiled=True).reshape(value.shape)  10.7 us
    concatenate x1, other arithmetic, per_device(): jnp.concatenate([from_right, jnp.zeros((stacked_total, ext_rows, col_coun...  7.23 us
    another operation x3, other arithmetic, blending_weights(): factor = jnp.linalg.cholesky(system)  6.52 us
    ppermute x2, local copies, waits for them, and re-layouts, send(): return lax.ppermute(piece, axis, pairs)  6.35 us
  transfers between devices with their start and end apart: 5, of which 3 were waited for; matrix products, arithmetic and copies ran while one was open for 11% of the time, Pallas kernels for 0%

profile of v4, /device:TPU:1, one launch (start us, length us, event | category | flops | bytes accessed | tf_op | source)
XLA Modules:
  0.0 161.5 jit_solution(4632543036769710315)
XLA Ops:
  0.6 1.1 fusion.24
  1.7 1.0 slice_convert_fusion.1
  2.7 0.7 slice_bitcast_fusion.3
  3.4 0.8 maximum_bitcast_fusion
  4.2 3.3 %collective-permute-start = (f32[3,129,128]{2,0,1:T(4,128)}, f32[3,129,128]{2,0,1:T(4,128)}, u32[]{:S(2)}, u32[]{:S(2)}) collective-permute-start(f32[3,129,128]{2,0,1:T(4,128)} %maximum_bitcast_fusion), channel_id=1, source_target_pairs={{16,0},{32,16},{48,32},{64,48},{80,64},{96,80},{112,96},{17,1},{33... | collective-permute-start | bytes 594440 | tf_op jit(solution)/shard_map/ppermute | solution.py:21
  7.5 0.8 maximum_bitcast_fusion.1
  8.3 3.7 %collective-permute-start.1 = (f32[3,129,128]{2,0,1:T(4,128)}, f32[3,129,128]{2,0,1:T(4,128)}, u32[]{:S(2)}, u32[]{:S(2)}) collective-permute-start(f32[3,129,128]{2,0,1:T(4,128)} %maximum_bitcast_fusion.1), channel_id=1, source_target_pairs={{0,16},{16,32},{32,48},{48,64},{64,80},{80,96},{96,112},{1,17},{17... | collective-permute-start | bytes 594440 | tf_op jit(solution)/shard_map/ppermute | solution.py:21
  11.9 4.3 %fusion.23 = (f32[64,64,3]{2,1,0:T(8,128)S(1)}, f32[64,64,3]{2,1,0:T(8,128)}) fusion(f32[64,64,128]{2,1,0:T(8,128)} %perm_ref.1), kind=kLoop, calls=%fused_computation.58 | loop fusion | bytes 196608 | tf_op jit(solution)/shard_map/slice | solution.py:203
  16.2 1.5 fusion.25
  17.8 2.3 %copy.73 = f32[64,64,3]{1,0,2:T(8,128)S(1)} copy(f32[64,64,3]{2,1,0:T(8,128)} %get-tuple-element.10) | data formatting | bytes 98304
  20.1 1.7 %copy.74 = bf16[64,64,3]{1,0,2:T(8,128)(2,1)S(1)} copy(bf16[64,64,3]{2,1,0:T(8,128)(2,1)} %get-tuple-element.14) | data formatting | bytes 49152
  21.9 0.7 copy.71
  22.6 0.5 copy.72
  23.5 0.7 and_convert_fusion.mask_ref
  24.2 1.2 pad_maximum_fusion.1.source_rows_ref.perm_rows_ref.head_rows_ref
  25.4 0.2 fusion.26
  25.6 0.9 copy.60
  26.6 3.2 %collective-permute-start.3 = (f32[3,129,72]{2,1,0:T(8,128)S(1)}, f32[3,129,72]{2,1,0:T(8,128)S(1)}, u32[]{:S(2)}, u32[]{:S(2)}) collective-permute-start(f32[3,129,72]{2,1,0:T(8,128)S(1)} %maximum_bitcast_fusion.3), channel_id=1, source_target_pairs={{0,1},{1,2},{2,3},{3,4},{4,5},{5,6},{6,7},{7,8},{8,9},{9,10},{10,1... | collective-permute-start | bytes 334376 | tf_op jit(solution)/shard_map/ppermute | solution.py:21
  29.9 0.9 copy.54
  30.9 1.3 collective-permute-start.2
  32.8 1.9 %collective-permute-done.3 = f32[3,129,72]{2,1,0:T(8,128)S(1)} collective-permute-done((f32[3,129,72]{2,1,0:T(8,128)S(1)}, f32[3,129,72]{2,1,0:T(8,128)S(1)}, u32[]{:S(2)}, u32[]{:S(2)}) %collective-permute-start.3) | collective-permute-done | bytes 111488 | tf_op jit(solution)/shard_map/ppermute | solution.py:21
  34.7 3.2 %copy.61 = f32[3,129,72]{0,2,1:T(8,128)} copy(f32[3,129,72]{2,1,0:T(8,128)S(1)} %collective-permute-done.3) | data formatting | bytes 222912 | tf_op jit(solution)/shard_map/ppermute | solution.py:21
  37.9 1.7 %collective-permute-done.2 = f32[3,129,72]{2,1,0:T(8,128)S(1)} collective-permute-done((f32[3,129,72]{2,1,0:T(8,128)S(1)}, f32[3,129,72]{2,1,0:T(8,128)S(1)}, u32[]{:S(2)}, u32[]{:S(2)}) %collective-permute-start.2) | collective-permute-done | bytes 111488 | tf_op jit(solution)/shard_map/ppermute | solution.py:21
  39.6 3.2 %copy.55 = f32[3,129,72]{0,2,1:T(8,128)} copy(f32[3,129,72]{2,1,0:T(8,128)S(1)} %collective-permute-done.2) | data formatting | bytes 222912 | tf_op jit(solution)/shard_map/ppermute | solution.py:21
  42.7 7.2 %pad_maximum_fusion.source_cols_ref.perm_cols_ref.head_cols_ref = f32[129,72,128]{2,1,0:T(8,128)} fusion(f32[129,72,3]{2,1,0:T(8,128)} %bitcast.50, f32[129,72,3]{2,1,0:T(8,128)} %bitcast.51, f32[128]{0:T(128)S(1)} %pad.1.clone), kind=kLoop, calls=%fused_computation.1 | loop fusion | flops 2377728 | bytes 4978880 | tf_op jit(solution)/shard_map/concatenate | solution.py:210
  49.9 28.0 %shard_map.103 = (bf16[64,64,128]{2,1,0:T(8,128)(2,1)}, f32[64,64,128]{2,1,0:T(8,128)}) custom-call(f32[72,256]{1,0:T(8,128)} %and_convert_fusion.mask_ref, f32[64,128]{1,0:T(8,128)} %source_ref.1, f32[129,8,128]{2,1,0:T(8,128)} %copy-done, f32[129,72,128]{2,1,0:T(8,128)} %pad_maximum_fusion.source_cols_ref.perm_cols_ref.head_cols_ref, ...), custom_call_target="tpu_custom_call" | custom-call | flops 94371840 | bytes 7340032 | tf_op jit(solution)/shard_map/pallas_call | solution.py:73
  77.9 3.8 %copy.70 = f32[64,64,128]{0,2,1:T(8,128)} copy(f32[64,64,128]{2,1,0:T(8,128)} %get-tuple-element.6) | data formatting | bytes 4194304 | tf_op jit(solution)/shard_map/reshape | solution.py:220
  81.8 5.0 %gather_fusion = f32[1024,64]{1,0:T(8,128)S(1)} fusion(f32[64,8192]{0,1:T(8,128)} %bitcast.52, s32[1024]{0:T(1024)S(1)} %broadcast_clamp_fusion), kind=kCustom, calls=%fused_computation | custom fusion | bytes 528384 | tf_op jit(solution)/shard_map/jit(_take)/gather | solution.py:220
  86.8 0.2 copy.63
  87.1 0.3 copy.64
  87.4 22.5 %all_to_all.12 = f32[128,1,512]{2,1,0:T(1,128)S(1)} all-to-all(f32[128,1,512]{2,1,0:T(1,128)S(1)} %copy.64), channel_id=1, replica_groups=mesh['row'=8,'col'=16] {'row','col'}, dimensions={0} | all-to-all | bytes 524288 | tf_op jit(solution)/shard_map/all_to_all | solution.py:104
  109.9 0.2 reduce_sum.18
  110.1 0.8 broadcast_in_dim.80
  110.9 4.3 %all-to-all-start.1 = ((f32[128,1,512]{2,1,0:T(1,128)}), f32[128,1,512]{2,1,0:T(1,128)S(1)}, u32[]{:S(2)}, u32[]{:S(2)}) async-start(f32[128,1,512]{2,1,0:T(1,128)} %broadcast_in_dim.80), calls=%async_computation.1 | async-start | bytes 524288 | tf_op jit(solution)/shard_map/all_to_all | solution.py:106
  115.3 0.4 div.58
  115.7 10.7 %all-to-all-done.1 = f32[128,1,512]{2,1,0:T(1,128)S(1)} async-done(((f32[128,1,512]{2,1,0:T(1,128)}), f32[128,1,512]{2,1,0:T(1,128)S(1)}, u32[]{:S(2)}, u32[]{:S(2)}) %all-to-all-start.1) | async-done | bytes 262176 | tf_op jit(solution)/shard_map/all_to_all | solution.py:106
  126.4 0.6 reduce.7
  127.3 0.4 sub.36
  127.7 1.6 %fusion.22 = (f32[128,512]{1,0:T(8,128)S(1)}, f32[128,512]{1,0:T(8,128)S(1)}) fusion(f32[128,1,512]{2,1,0:T(1,128)S(1)} %all-to-all-done.1, f32[128,1,512]{2,1,0:T(1,128)S(1)} %sub.36, f32[128,1,512]{2,1,0:T(1,128)S(1)} %div.58), kind=kLoop, calls=%fused_computation.57 | loop fusion | flops 196608 | bytes 1310720 | tf_op jit(solution)/shard_map/div | solution.py:158
  129.5 0.4 fusion.27
  130.0 5.8 %cholesky.17 = f32[64,64]{1,0:T(8,128)S(1)} custom-call(f32[64,64]{1,0:T(8,128)S(1)} %fusion.18), custom_call_target="Cholesky" | custom-call | tf_op jit(solution)/shard_map/jit(cholesky)/cholesky | solution.py:165
  135.8 0.6 compare_reduce_fusion
  136.5 0.7 fusion.12
  137.1 4.9 %custom-call.8 = f32[1,64,64]{1,2,0:T(8,128)S(1)} custom-call(f32[1,64,64]{2,1,0:T(8,128)S(1)} %fusion.12), custom_call_target="InvertDiagBlocksLowerTriangular" | custom-call | tf_op jit(solution)/shard_map/triangular_solve | solution.py:167
  142.1 0.4 fusion
  142.5 0.2 fusion.15
  142.7 0.8 fusion.13.mix_t_ref
  143.5 17.9 %shard_map.104 = f32[4096,128]{1,0:T(8,128)} custom-call(f32[64,64]{1,0:T(8,128)} %fusion.13.mix_t_ref, f32[4096,128]{1,0:T(8,128)} %bitcast.49), custom_call_target="tpu_custom_call" | custom-call | flops 67108864 | bytes 4194304 | tf_op jit(solution)/shard_map/pallas_call | solution.py:145
  (61 shorter events, 2.1 us)
Async XLA Ops:
  4.2 20.0 %collective-permute-start = (f32[3,129,128]{2,0,1:T(4,128)}, f32[3,129,128]{2,0,1:T(4,128)}, u32[]{:S(2)}, u32[]{:S(2)}) collective-permute-start(f32[3,129,128]{2,0,1:T(4,128)} %maximum_bitcast_fusion), channel_id=1, source_target_pairs={{16,0},{32,16},{48,32},{64,48},{80,64},{96,80},{112,96},{17,1},{33... | collective-permute-start | bytes 594440 | tf_op jit(solution)/shard_map/ppermute | solution.py:21
  8.3 8.0 %copy-start.1 = (bf16[64,64,128]{2,1,0:T(8,128)(2,1)S(1)}, bf16[64,64,128]{2,1,0:T(8,128)(2,1)}, u32[]{:S(2)}) copy-start(bf16[64,64,128]{2,1,0:T(8,128)(2,1)} %head_ref.1) | copy-start | bytes 3145732
  8.3 9.5 %copy-start.3 = (f32[64,128]{1,0:T(8,128)S(1)}, f32[64,128]{1,0:T(8,128)}, u32[]{:S(2)}) copy-start(f32[64,128]{1,0:T(8,128)} %source_ref.1) | copy-start | bytes 98308
  8.3 16.0 %collective-permute-start.1 = (f32[3,129,128]{2,0,1:T(4,128)}, f32[3,129,128]{2,0,1:T(4,128)}, u32[]{:S(2)}, u32[]{:S(2)}) collective-permute-start(f32[3,129,128]{2,0,1:T(4,128)} %maximum_bitcast_fusion.1), channel_id=1, source_target_pairs={{0,16},{16,32},{32,48},{48,64},{64,80},{80,96},{96,112},{1,17},{17... | collective-permute-start | bytes 594440 | tf_op jit(solution)/shard_map/ppermute | solution.py:21
  17.7 5.5 %copy-start.4 = (s32[4,256]{1,0:T(4,128)S(1)}, s32[4,256]{1,0:T(4,128)}, u32[]{:S(2)}) copy-start(s32[4,256]{1,0:T(4,128)} %param.11) | copy-start | bytes 12292
  17.7 5.6 %copy-start.8 = (s32[4]{0:T(128)S(1)}, s32[4]{0:T(128)}, u32[]{:S(2)}) copy-start(s32[4]{0:T(128)} %param.12) | copy-start | bytes 52
  25.4 12.5 %copy-start = (f32[129,8,128]{2,1,0:T(8,128)}, f32[129,8,128]{2,1,0:T(8,128)S(1)}, u32[]{:S(2)}) copy-start(f32[129,8,128]{2,1,0:T(8,128)S(1)} %pad_maximum_fusion.1.source_rows_ref.perm_rows_ref.head_rows_ref) | copy-start | bytes 1585156
  26.6 8.0 %collective-permute-start.3 = (f32[3,129,72]{2,1,0:T(8,128)S(1)}, f32[3,129,72]{2,1,0:T(8,128)S(1)}, u32[]{:S(2)}, u32[]{:S(2)}) collective-permute-start(f32[3,129,72]{2,1,0:T(8,128)S(1)} %maximum_bitcast_fusion.3), channel_id=1, source_target_pairs={{0,1},{1,2},{2,3},{3,4},{4,5},{5,6},{6,7},{7,8},{8,9},{9,10},{10,1... | collective-permute-start | bytes 334376 | tf_op jit(solution)/shard_map/ppermute | solution.py:21
  30.9 8.7 %collective-permute-start.2 = (f32[3,129,72]{2,1,0:T(8,128)S(1)}, f32[3,129,72]{2,1,0:T(8,128)S(1)}, u32[]{:S(2)}, u32[]{:S(2)}) collective-permute-start(f32[3,129,72]{2,1,0:T(8,128)S(1)} %maximum_bitcast_fusion.2), channel_id=1, source_target_pairs={{1,0},{2,1},{3,2},{4,3},{5,4},{6,5},{7,6},{8,7},{9,8},{10,9},{11,1... | collective-permute-start | bytes 334376 | tf_op jit(solution)/shard_map/ppermute | solution.py:21
  81.8 33.4 %copy-start.5 = (f32[1024]{0:T(1024)S(1)}, f32[1024]{0:T(1024)}, u32[]{:S(2)}) copy-start(f32[1024]{0:T(1024)} %param.14) | copy-start | bytes 12292
  87.1 55.0 %copy-start.6 = (f32[64,1024]{1,0:T(8,128)S(1)}, f32[64,1024]{1,0:T(8,128)}, u32[]{:S(2)}) copy-start(f32[64,1024]{1,0:T(8,128)} %param.15) | copy-start | bytes 786436
  87.1 55.0 %copy-start.7 = (f32[1024]{0:T(1024)S(1)}, f32[1024]{0:T(1024)}, u32[]{:S(2)}) copy-start(f32[1024]{0:T(1024)} %param.13) | copy-start | bytes 12292
  110.9 15.5 %all-to-all-start.1 = ((f32[128,1,512]{2,1,0:T(1,128)}), f32[128,1,512]{2,1,0:T(1,128)S(1)}, u32[]{:S(2)}, u32[]{:S(2)}) async-start(f32[128,1,512]{2,1,0:T(1,128)} %broadcast_in_dim.80), calls=%async_computation.1 | async-start | bytes 524288 | tf_op jit(solution)/shard_map/all_to_all | solution.py:106
  127.1 34.4 %copy-start.2 = (f32[64,1024]{1,0:T(8,128)}, f32[64,1024]{1,0:T(8,128)S(1)}, u32[]{:S(2)}) copy-start(f32[64,1024]{1,0:T(8,128)S(1)} %reshape.208) | copy-start | bytes 786436

commit v5 on v3

--- a/solution.py
+++ b/solution.py
@@ -169,18 +169,32 @@
         [from_below, jnp.zeros((stacked_total, 8 - 2 * width, col_count), f32), from_above], axis=1
     )
 
-    def stack_cols(lo, hi):
-        interior = jnp.concatenate(
-            [logarithmic_conductivity[:, :, lo:hi], starting_head[:, :, lo:hi].astype(f32), recharge[None, :, lo:hi]],
-            axis=0,
-        )
-        return jnp.moveaxis(jnp.concatenate([interior, halo_rows[:, :, lo:hi]], axis=1), 2, 0)
-
-    from_left = jnp.moveaxis(send(stack_cols(col_count - width, col_count), "col", True), 0, 2)
-    from_right = jnp.moveaxis(send(stack_cols(0, width), "col", False), 0, 2)
-    halo_cols = jnp.concatenate(
-        [from_right, jnp.zeros((stacked_total, ext_rows, col_count - 2 * width), f32), from_left], axis=2
-    )
+    highest = lax.Precision.HIGHEST
+    lane = jnp.arange(col_count)
+    pick = jnp.arange(8)
+    wanted = jnp.where(pick < width, pick, col_count - 8 + pick)
+    selector = ((pick[:, None] < width) | (pick[:, None] >= 8 - width)) & (lane[None, :] == wanted[:, None])
+    selector = selector.astype(f32)
+
+    def columns(block):
+        flat = block.reshape(-1, col_count)
+        if block.dtype == jnp.bfloat16:
+            return jnp.dot(selector.astype(jnp.bfloat16), flat.T, preferred_element_type=f32)
+        return jnp.dot(selector, flat.T, precision=highest)
+
+    interior_cols = jnp.concatenate(
+        [
+            columns(logarithmic_conductivity).reshape(8, member_count, row_count),
+            columns(starting_head).reshape(8, member_count, row_count),
+            columns(recharge).reshape(8, 1, row_count),
+        ],
+        axis=1,
+    )
+    border_cols = jnp.concatenate([interior_cols, columns(halo_rows).reshape(8, stacked_total, 8)], axis=2)
+    from_left = send(border_cols[8 - width :], "col", True)
+    from_right = send(border_cols[:width], "col", False)
+    received = jnp.concatenate([from_right, jnp.zeros((8 - 2 * width,) + from_right.shape[1:], f32), from_left], axis=0)
+    halo_cols = jnp.einsum("kmr,kl->mrl", received, selector, precision=highest)
     inside = circular_inside("row", row_count, width, ext_rows)[:, None] & circular_inside(
         "col", col_count, width, ext_cols
     )[None, :]

time: 155 us -> 141 us (0.910)
  local copies, waits for them, and re-layouts: 38.3 us -> 18.4 us
  matrix products: 8.05 us -> 19.6 us
  other arithmetic: 28.5 us -> 18.9 us
  starting transfers between devices: 27.3 us -> 29.7 us
  waiting for transfers between devices: 23.5 us -> 25.3 us
    dot_general x0 -> x5, matrix products: none -> 11.6 us  [the longest x1 5.72 us: per_device(): halo_cols = jnp.einsum('kmr,kl->mrl', received, selector, precision=highest)]
    slice x5 -> x1, local copies, waits for them, and re-layouts: 8.46 us -> 0.08 us  [per_device(): from_right = send(border_cols[:width], 'col', False)]
    concatenate x1, other arithmetic: 7.23 us -> 0.21 us  [per_device(): jnp.concatenate([interior_cols, columns(halo_rows).reshape(8, stacked_tot...]
    ppermute x2 -> x0, local copies, waits for them, and re-layouts: 6.35 us -> none  [send(): return lax.ppermute(piece, axis, pairs)]
    unnamed x28 -> x22, local copies, waits for them, and re-layouts: 8.65 us -> 3.23 us
    all_to_all x1, starting transfers between devices: 11.5 us -> 13.3 us  [broadcast_from_owners(): own_chunk = lax.all_to_all(chunks, axes, 0, 0, tiled=True).sum(axis=0)]
    ppermute x4, waiting for transfers between devices: 3.54 us -> 5.18 us  [send(): return lax.ppermute(piece, axis, pairs)]
  transfers between devices with their start and end apart: 6 -> 6, of which waited for: 4 -> 4; matrix products, arithmetic and copies ran while one was open for 14% -> 6% of each run, Pallas kernels for 0% -> 0%
where the time goes in v5:
time: 141 us
  starting transfers between devices  29.7 us (21%)
  Pallas kernels  28 us (20%)
  waiting for transfers between devices  25.3 us (18%)
  matrix products  19.6 us (14%)
  other arithmetic  18.9 us (13%)
  local copies, waits for them, and re-layouts  18.4 us (13%)
    pallas_call x1, Pallas kernels, run_stencil(): pl.pallas_call(stencil_kernel, grid=(blocks,), in_specs=[full2(mask.shape...  28 us
    all_to_all x1, starting transfers between devices, broadcast_from_owners(): own_chunk = lax.all_to_all(chunks, axes, 0, 0, tiled=True).sum(axis=0)  13.3 us
    ppermute x4, starting transfers between devices, send(): return lax.ppermute(piece, axis, pairs)  12.1 us
    all_to_all x1, waiting for transfers between devices, broadcast_from_owners(): own_chunk = lax.all_to_all(chunks, axes, 0, 0, tiled=True).sum(axis=0)  10.4 us
    all_to_all x1, waiting for transfers between devices, broadcast_from_owners(): return lax.all_to_all(spread, axes, 0, 0, tiled=True).reshape(value.shape)  9.65 us
    another operation x3, other arithmetic, blending_weights(): factor = jnp.linalg.cholesky(system)  6.6 us
    dot_general x1, matrix products, per_device(): halo_cols = jnp.einsum('kmr,kl->mrl', received, selector, precision=highest)  5.72 us
    dot_general x1, matrix products, per_device(): jnp.einsum('mrc,mn->nrc', anomalies, mixing, precision=lax.Precision.HIGH...  5.68 us
  transfers between devices with their start and end apart: 6, of which 4 were waited for; matrix products, arithmetic and copies ran while one was open for 6% of the time, Pallas kernels for 0%

profile of v5, /device:TPU:1, one launch (start us, length us, event | category | flops | bytes accessed | tf_op | source)
XLA Modules:
  0.0 140.9 jit_solution(15310581396687846942)
XLA Ops:
  0.6 1.2 fusion.55
  1.8 1.0 slice_convert_fusion.1
  2.8 0.7 slice_bitcast_fusion.1
  3.6 3.3 %collective-permute-start = (f32[3,129,128]{2,0,1:T(4,128)S(1)}, f32[3,129,128]{2,0,1:T(4,128)S(1)}, u32[]{:S(2)}, u32[]{:S(2)}) collective-permute-start(f32[3,129,128]{2,0,1:T(4,128)S(1)} %maximum_bitcast_fusion), channel_id=1, source_target_pairs={{16,0},{32,16},{48,32},{64,48},{80,64},{96,80},{112,96},{17,1},{33... | collective-permute-start | bytes 594440 | tf_op jit(solution)/shard_map/ppermute | solution.py:21
  7.0 3.6 %collective-permute-start.1 = (f32[3,129,128]{2,0,1:T(4,128)S(1)}, f32[3,129,128]{2,0,1:T(4,128)S(1)}, u32[]{:S(2)}, u32[]{:S(2)}) collective-permute-start(f32[3,129,128]{2,0,1:T(4,128)S(1)} %maximum_bitcast_fusion.1), channel_id=1, source_target_pairs={{0,16},{16,32},{32,48},{48,64},{64,80},{80,96},{96,112},{1,17},{17... | collective-permute-start | bytes 594440 | tf_op jit(solution)/shard_map/ppermute | solution.py:21
  10.6 4.1 %fusion.35 = f32[8,64,64]{2,0,1:T(8,128)S(1)} fusion(f32[64,64,128]{2,1,0:T(8,128)} %perm_ref.1, s32[8]{0:T(128)S(1)} %compare_select_fusion.4, pred[8]{0:T(512)(128)(4,1)S(1)} %compare_or_fusion), kind=kOutput, calls=%fused_computation.60 | convolution fusion | flops 50333696 | bytes 2228264 | tf_op jit(solution)/shard_map/dot_general | solution.py:183
  14.7 0.9 fusion.38
  15.7 0.2 convolution_bitcast_fusion.1
  16.2 0.7 and_convert_fusion.mask_ref
  17.0 0.1 pad_maximum_fusion.source_rows_ref.perm_rows_ref.head_rows_ref
  17.1 0.6 fusion.4
  17.7 0.4 copy.27
  18.1 0.2 pad_maximum_fusion.1
  18.4 1.3 collective-permute-start.2
  19.7 4.0 %collective-permute-start.3 = (f32[3,129,72]{2,0,1:T(4,128)S(1)}, f32[3,129,72]{2,0,1:T(4,128)S(1)}, u32[]{:S(2)}, u32[]{:S(2)}) collective-permute-start(f32[3,129,72]{2,0,1:T(4,128)S(1)} %get-tuple-element.23), channel_id=1, source_target_pairs={{0,1},{1,2},{2,3},{3,4},{4,5},{5,6},{6,7},{7,8},{8,9},{9,10},{10,1... | collective-permute-start | bytes 334376 | tf_op jit(solution)/shard_map/ppermute | solution.py:21
  23.9 0.2 broadcast_in_dim.72
  24.1 0.2 broadcast_in_dim.74
  24.3 3.4 %collective-permute-done.2 = f32[3,129,72]{2,0,1:T(4,128)S(1)} collective-permute-done((f32[3,129,72]{2,0,1:T(4,128)S(1)}, f32[3,129,72]{2,0,1:T(4,128)S(1)}, u32[]{:S(2)}, u32[]{:S(2)}) %collective-permute-start.2) | collective-permute-done | bytes 111488 | tf_op jit(solution)/shard_map/ppermute | solution.py:21
  27.7 1.8 %collective-permute-done.3 = f32[3,129,72]{2,0,1:T(4,128)S(1)} collective-permute-done((f32[3,129,72]{2,0,1:T(4,128)S(1)}, f32[3,129,72]{2,0,1:T(4,128)S(1)}, u32[]{:S(2)}, u32[]{:S(2)}) %collective-permute-start.3) | collective-permute-done | bytes 111488 | tf_op jit(solution)/shard_map/ppermute | solution.py:21
  29.5 5.7 %fusion.6.source_cols_ref.perm_cols_ref.head_cols_ref = f32[129,72,128]{2,1,0:T(8,128)} fusion(f32[3,129,72]{2,0,1:T(4,128)S(1)} %collective-permute-done.3, f32[3,129,72]{2,0,1:T(4,128)S(1)} %collective-permute-done.2, f32[8]{0:T(128)S(1)} %pad.8.clone, s32[8]{0:T(128)S(1)} %compare_select_fusion.4, pred[8]{0:T(512)(128)(4,1)S(1)} %compare_or_fusion), kind=kOutput, calls=%fused_computation.11 | convolution fusion | flops 114281600 | bytes 4978440 | tf_op jit(solution)/shard_map/kmr,kl->mrl/dot_general | solution.py:197
  35.2 28.0 %shard_map.103 = (bf16[64,64,128]{2,1,0:T(8,128)(2,1)}, f32[64,64,128]{2,1,0:T(8,128)}) custom-call(f32[72,256]{1,0:T(8,128)} %and_convert_fusion.mask_ref, f32[64,128]{1,0:T(8,128)} %source_ref.1, f32[129,8,128]{2,1,0:T(8,128)} %copy-done.1, f32[129,72,128]{2,1,0:T(8,128)} %fusion.6.source_cols_ref.perm_cols_ref.head_cols_ref, f32[64,64,128]{2,1,0:T(8,128)} %perm_ref.1, ...), custom_call_target="tpu_custom_call" | custom-call | flops 94371840 | bytes 7340032 | tf_op jit(solution)/shard_map/pallas_call | solution.py:73
  63.2 3.8 %copy.37 = f32[64,64,128]{0,2,1:T(8,128)} copy(f32[64,64,128]{2,1,0:T(8,128)} %get-tuple-element.6) | data formatting | bytes 4194304 | tf_op jit(solution)/shard_map/reshape | solution.py:205
  67.0 5.0 %gather_fusion = f32[1024,64]{1,0:T(8,128)S(1)} fusion(f32[64,8192]{0,1:T(8,128)} %bitcast.53, s32[1024]{0:T(1024)S(1)} %broadcast_clamp_fusion), kind=kCustom, calls=%fused_computation | custom fusion | bytes 528384 | tf_op jit(solution)/shard_map/jit(_take)/gather | solution.py:205
  72.0 0.2 copy.29
  72.3 1.0 copy.30
  73.3 13.3 %all-to-all-start = ((f32[128,1,512]{2,1,0:T(1,128)}), f32[128,1,512]{2,1,0:T(1,128)S(1)}, u32[]{:S(2)}, u32[]{:S(2)}) async-start(f32[128,1,512]{2,1,0:T(1,128)} %copy.30), calls=%async_computation | async-start | bytes 524288 | tf_op jit(solution)/shard_map/all_to_all | solution.py:104
  86.6 0.1 reduce_sum.29
  86.8 0.4 div.70
  87.2 10.4 %all-to-all-done = f32[128,1,512]{2,1,0:T(1,128)S(1)} async-done(((f32[128,1,512]{2,1,0:T(1,128)}), f32[128,1,512]{2,1,0:T(1,128)S(1)}, u32[]{:S(2)}, u32[]{:S(2)}) %all-to-all-start) | async-done | bytes 262176 | tf_op jit(solution)/shard_map/all_to_all | solution.py:104
  97.7 0.2 reduce_sum.27
  97.9 0.8 broadcast_in_dim.77
  98.7 4.3 %all-to-all-start.1 = ((f32[128,1,512]{2,1,0:T(1,128)}), f32[128,1,512]{2,1,0:T(1,128)S(1)}, u32[]{:S(2)}, u32[]{:S(2)}) async-start(f32[128,1,512]{2,1,0:T(1,128)} %broadcast_in_dim.77), calls=%async_computation.1 | async-start | bytes 524288 | tf_op jit(solution)/shard_map/all_to_all | solution.py:106
  103.0 1.6 %subtract_multiply_fusion = f32[64,64,128]{2,1,0:T(8,128)} fusion(f32[64,64,128]{2,1,0:T(8,128)S(1)} %copy-done, f32[64,128]{1,0:T(8,128)S(1)} %broadcast_multiply_fusion), kind=kLoop, calls=%fused_computation.4 | loop fusion | flops 1048576 | bytes 4227072 | tf_op jit(solution)/shard_map/div | solution.py:212
  104.6 9.6 %all-to-all-done.1 = f32[128,1,512]{2,1,0:T(1,128)S(1)} async-done(((f32[128,1,512]{2,1,0:T(1,128)}), f32[128,1,512]{2,1,0:T(1,128)S(1)}, u32[]{:S(2)}, u32[]{:S(2)}) %all-to-all-start.1) | async-done | bytes 262176 | tf_op jit(solution)/shard_map/all_to_all | solution.py:106
  114.2 0.6 reduce.7
  115.1 0.5 copy-done.3
  115.6 0.4 sub.44
  116.1 1.8 %fusion.54 = (f32[128,512]{1,0:T(8,128)S(1)}, f32[128,512]{1,0:T(8,128)S(1)}) fusion(f32[128,1,512]{2,1,0:T(1,128)S(1)} %all-to-all-done.1, f32[128,1,512]{2,1,0:T(1,128)S(1)} %sub.44, f32[128,1,512]{2,1,0:T(1,128)S(1)} %div.70), kind=kLoop, calls=%fused_computation.87 | loop fusion | flops 196608 | bytes 1310720 | tf_op jit(solution)/shard_map/div | solution.py:129
  118.0 0.4 fusion.57
  118.5 5.8 %cholesky.17 = f32[64,64]{1,0:T(8,128)S(1)} custom-call(f32[64,64]{1,0:T(8,128)S(1)} %fusion.29), custom_call_target="Cholesky" | custom-call | tf_op jit(solution)/shard_map/jit(cholesky)/cholesky | solution.py:136
  124.3 0.7 compare_reduce_fusion
  125.1 0.7 fusion.24
  125.8 4.9 %custom-call.8 = f32[1,64,64]{1,2,0:T(8,128)S(1)} custom-call(f32[1,64,64]{2,1,0:T(8,128)S(1)} %fusion.24), custom_call_target="InvertDiagBlocksLowerTriangular" | custom-call | tf_op jit(solution)/shard_map/triangular_solve | solution.py:138
  130.7 1.5 %fusion.12 = f32[64,64]{1,0:T(8,128)S(1)} fusion(f32[64,1024]{1,0:T(8,128)} %copy-done.3, f32[64,1024]{1,0:T(8,128)} %param.15, f32[1024]{0:T(1024)S(1)} %sqrt.3, f32[1024]{0:T(1024)S(1)} %copy-done.7, f32[1024]{0:T(1024)S(1)} %copy-done.6, f32[1024]{0:T(1024)S(1)} %broadcast_multiply_fusion.1), kind=kOutput, calls=%fused_computation.19 | convolution fusion | flops 50724864 | bytes 557056 | tf_op jit(solution)/shard_map/dot_general | solution.py:135
  132.2 0.2 fusion.26
  132.4 0.2 convolution_bitcast_fusion
  132.7 5.7 %copy_add_fusion = f32[64,64,128]{2,0,1:T(8,128)S(1)} fusion(f32[64,64,128]{2,1,0:T(8,128)S(1)} %copy-done, f32[64,64,1]{0,1,2:T(8,128)S(1)} %convolution_bitcast_fusion, f32[64,64,128]{2,1,0:T(8,128)} %subtract_multiply_fusion), kind=kOutput, calls=%fused_computation.1 | convolution fusion | flops 403177472 | bytes 6307840 | tf_op jit(solution)/shard_map/mrc,mn->nrc/dot_general | solution.py:215
  138.4 2.5 %copy.35 = f32[64,64,128]{2,1,0:T(8,128)} copy(f32[64,64,128]{2,0,1:T(8,128)S(1)} %copy_add_fusion) | data formatting | bytes 4194304
  (55 shorter events, 1.4 us)
Async XLA Ops:
  0.6 14.1 %copy-start.2 = (bf16[64,64,128]{2,1,0:T(8,128)(2,1)S(1)}, bf16[64,64,128]{2,1,0:T(8,128)(2,1)}, u32[]{:S(2)}) copy-start(bf16[64,64,128]{2,1,0:T(8,128)(2,1)} %head_ref.1) | copy-start | bytes 3145732
  3.6 13.3 %collective-permute-start = (f32[3,129,128]{2,0,1:T(4,128)S(1)}, f32[3,129,128]{2,0,1:T(4,128)S(1)}, u32[]{:S(2)}, u32[]{:S(2)}) collective-permute-start(f32[3,129,128]{2,0,1:T(4,128)S(1)} %maximum_bitcast_fusion), channel_id=1, source_target_pairs={{16,0},{32,16},{48,32},{64,48},{80,64},{96,80},{112,96},{17,1},{33... | collective-permute-start | bytes 594440 | tf_op jit(solution)/shard_map/ppermute | solution.py:21
  6.9 8.8 %copy-start.4 = (f32[64,128]{1,0:T(8,128)S(1)}, f32[64,128]{1,0:T(8,128)}, u32[]{:S(2)}) copy-start(f32[64,128]{1,0:T(8,128)} %source_ref.1) | copy-start | bytes 98308
  6.9 9.0 %copy-start.5 = (s32[4,256]{1,0:T(4,128)S(1)}, s32[4,256]{1,0:T(4,128)}, u32[]{:S(2)}) copy-start(s32[4,256]{1,0:T(4,128)} %param.11) | copy-start | bytes 12292
  6.9 9.1 %copy-start.8 = (s32[4]{0:T(128)S(1)}, s32[4]{0:T(128)}, u32[]{:S(2)}) copy-start(s32[4]{0:T(128)} %param.12) | copy-start | bytes 52
  7.0 9.9 %collective-permute-start.1 = (f32[3,129,128]{2,0,1:T(4,128)S(1)}, f32[3,129,128]{2,0,1:T(4,128)S(1)}, u32[]{:S(2)}, u32[]{:S(2)}) collective-permute-start(f32[3,129,128]{2,0,1:T(4,128)S(1)} %maximum_bitcast_fusion.1), channel_id=1, source_target_pairs={{0,16},{16,32},{32,48},{48,64},{64,80},{80,96},{96,112},{1,17},{17... | collective-permute-start | bytes 594440 | tf_op jit(solution)/shard_map/ppermute | solution.py:21
  17.1 6.9 %copy-start.1 = (f32[129,8,128]{2,1,0:T(8,128)}, f32[129,8,128]{2,1,0:T(8,128)S(1)}, u32[]{:S(2)}) copy-start(f32[129,8,128]{2,1,0:T(8,128)S(1)} %pad_maximum_fusion.source_rows_ref.perm_rows_ref.head_rows_ref) | copy-start | bytes 1585156
  18.4 9.3 %collective-permute-start.2 = (f32[3,129,72]{2,0,1:T(4,128)S(1)}, f32[3,129,72]{2,0,1:T(4,128)S(1)}, u32[]{:S(2)}, u32[]{:S(2)}) collective-permute-start(f32[3,129,72]{2,0,1:T(4,128)S(1)} %get-tuple-element.22), channel_id=1, source_target_pairs={{1,0},{2,1},{3,2},{4,3},{5,4},{6,5},{7,6},{8,7},{9,8},{10,9},{11,1... | collective-permute-start | bytes 334376 | tf_op jit(solution)/shard_map/ppermute | solution.py:21
  19.7 9.8 %collective-permute-start.3 = (f32[3,129,72]{2,0,1:T(4,128)S(1)}, f32[3,129,72]{2,0,1:T(4,128)S(1)}, u32[]{:S(2)}, u32[]{:S(2)}) collective-permute-start(f32[3,129,72]{2,0,1:T(4,128)S(1)} %get-tuple-element.23), channel_id=1, source_target_pairs={{0,1},{1,2},{2,3},{3,4},{4,5},{5,6},{6,7},{7,8},{8,9},{9,10},{10,1... | collective-permute-start | bytes 334376 | tf_op jit(solution)/shard_map/ppermute | solution.py:21
  72.0 14.6 %copy-start.6 = (f32[1024]{0:T(1024)S(1)}, f32[1024]{0:T(1024)}, u32[]{:S(2)}) copy-start(f32[1024]{0:T(1024)} %param.14) | copy-start | bytes 12292
  72.0 14.6 %copy-start = (f32[64,64,128]{2,1,0:T(8,128)S(1)}, f32[64,64,128]{2,1,0:T(8,128)}, u32[]{:S(2)}) copy-start(f32[64,64,128]{2,1,0:T(8,128)} %perm_ref.1) | copy-start | bytes 6291460
  73.3 24.4 %all-to-all-start = ((f32[128,1,512]{2,1,0:T(1,128)}), f32[128,1,512]{2,1,0:T(1,128)S(1)}, u32[]{:S(2)}, u32[]{:S(2)}) async-start(f32[128,1,512]{2,1,0:T(1,128)} %copy.30), calls=%async_computation | async-start | bytes 524288 | tf_op jit(solution)/shard_map/all_to_all | solution.py:104
  98.7 15.5 %all-to-all-start.1 = ((f32[128,1,512]{2,1,0:T(1,128)}), f32[128,1,512]{2,1,0:T(1,128)S(1)}, u32[]{:S(2)}, u32[]{:S(2)}) async-start(f32[128,1,512]{2,1,0:T(1,128)} %broadcast_in_dim.77), calls=%async_computation.1 | async-start | bytes 524288 | tf_op jit(solution)/shard_map/all_to_all | solution.py:106
  114.9 0.7 copy-start.3
  114.9 15.7 %copy-start.7 = (f32[1024]{0:T(1024)S(1)}, f32[1024]{0:T(1024)}, u32[]{:S(2)}) copy-start(f32[1024]{0:T(1024)} %param.13) | copy-start | bytes 12292

commit v6 on v5

--- a/solution.py
+++ b/solution.py
@@ -46,15 +46,21 @@
         vertical = jnp.exp(0.5 * (perm + pltpu.roll(perm, ext_rows - 1, 0)))
         horizontal = jnp.exp(0.5 * (perm + pltpu.roll(perm, ext_cols - 1, 1)))
         faces = (pltpu.roll(vertical, 1, 0), vertical, pltpu.roll(horizontal, 1, 1), horizontal)
-        for _ in range(STEPS):
+        for step_index in range(STEPS):
             near = (pltpu.roll(head, 1, 0), pltpu.roll(head, ext_rows - 1, 0),
                     pltpu.roll(head, 1, 1), pltpu.roll(head, ext_cols - 1, 1))
-            flux_total = jnp.zeros_like(head)
-            for weight_face, near_press in zip(faces, near):
-                flux_total = flux_total + weight_face * (near_press - head)
-            head = head + time_step * (flux_total + source)
-            head = jnp.where(inside, head, 0.0)
-        final = head[:rows, :cols]
+            if step_index == STEPS - 1:
+                crop = lambda x: x[:rows, :cols]
+                near, weights, centre, src = [crop(x) for x in near], [crop(x) for x in faces], crop(head), crop(source)
+            else:
+                weights, centre, src = faces, head, source
+            flux_total = jnp.zeros_like(centre)
+            for weight_face, near_press in zip(weights, near):
+                flux_total = flux_total + weight_face * (near_press - centre)
+            head = centre + time_step * (flux_total + src)
+            if step_index < STEPS - 1:
+                head = jnp.where(inside, head, 0.0)
+        final = head
         out32_ref[j] = final
         out16_ref[j] = final.astype(jnp.bfloat16)
         return carry

time: 141 us -> 142 us (level)
  no operation moved by 1% of the time
where the time goes in v6:
time: 142 us; the launch traced here: 141 us
  starting transfers between devices  29.7 us (21%)
  Pallas kernels  28 us (20%)
  waiting for transfers between devices  25.3 us (18%)
  matrix products  19.6 us (14%)
  other arithmetic  18.9 us (13%)
  local copies, waits for them, and re-layouts  18.4 us (13%)
    pallas_call x1, Pallas kernels, run_stencil(): pl.pallas_call(stencil_kernel, grid=(blocks,), in_specs=[full2(mask.shape...  28 us
    all_to_all x1, starting transfers between devices, broadcast_from_owners(): own_chunk = lax.all_to_all(chunks, axes, 0, 0, tiled=True).sum(axis=0)  13.3 us
    ppermute x4, starting transfers between devices, send(): return lax.ppermute(piece, axis, pairs)  12.1 us
    all_to_all x1, waiting for transfers between devices, broadcast_from_owners(): own_chunk = lax.all_to_all(chunks, axes, 0, 0, tiled=True).sum(axis=0)  10.4 us
    all_to_all x1, waiting for transfers between devices, broadcast_from_owners(): return lax.all_to_all(spread, axes, 0, 0, tiled=True).reshape(value.shape)  9.65 us
    another operation x3, other arithmetic, blending_weights(): factor = jnp.linalg.cholesky(system)  6.6 us
    dot_general x1, matrix products, per_device(): halo_cols = jnp.einsum('kmr,kl->mrl', received, selector, precision=highest)  5.72 us
    dot_general x1, matrix products, per_device(): jnp.einsum('mrc,mn->nrc', anomalies, mixing, precision=lax.Precision.HIGH...  5.68 us
  transfers between devices with their start and end apart: 6, of which 4 were waited for; matrix products, arithmetic and copies ran while one was open for 6% of the time, Pallas kernels for 0%

profile of v6, /device:TPU:1, one launch (start us, length us, event | category | flops | bytes accessed | tf_op | source)
XLA Modules:
  0.0 141.0 jit_solution(12690156533560760303)
XLA Ops:
  0.6 1.2 fusion.55
  1.8 1.0 slice_convert_fusion.1
  2.8 0.7 slice_bitcast_fusion.1
  3.6 3.3 %collective-permute-start = (f32[3,129,128]{2,0,1:T(4,128)S(1)}, f32[3,129,128]{2,0,1:T(4,128)S(1)}, u32[]{:S(2)}, u32[]{:S(2)}) collective-permute-start(f32[3,129,128]{2,0,1:T(4,128)S(1)} %maximum_bitcast_fusion), channel_id=1, source_target_pairs={{16,0},{32,16},{48,32},{64,48},{80,64},{96,80},{112,96},{17,1},{33... | collective-permute-start | bytes 594440 | tf_op jit(solution)/shard_map/ppermute | solution.py:21
  7.0 3.6 %collective-permute-start.1 = (f32[3,129,128]{2,0,1:T(4,128)S(1)}, f32[3,129,128]{2,0,1:T(4,128)S(1)}, u32[]{:S(2)}, u32[]{:S(2)}) collective-permute-start(f32[3,129,128]{2,0,1:T(4,128)S(1)} %maximum_bitcast_fusion.1), channel_id=1, source_target_pairs={{0,16},{16,32},{32,48},{48,64},{64,80},{80,96},{96,112},{1,17},{17... | collective-permute-start | bytes 594440 | tf_op jit(solution)/shard_map/ppermute | solution.py:21
  10.6 4.1 %fusion.35 = f32[8,64,64]{2,0,1:T(8,128)S(1)} fusion(f32[64,64,128]{2,1,0:T(8,128)} %perm_ref.1, s32[8]{0:T(128)S(1)} %compare_select_fusion.4, pred[8]{0:T(512)(128)(4,1)S(1)} %compare_or_fusion), kind=kOutput, calls=%fused_computation.60 | convolution fusion | flops 50333696 | bytes 2228264 | tf_op jit(solution)/shard_map/dot_general | solution.py:189
  14.7 0.9 fusion.38
  15.7 0.2 convolution_bitcast_fusion.1
  16.2 0.7 and_convert_fusion.mask_ref
  17.0 0.1 pad_maximum_fusion.source_rows_ref.perm_rows_ref.head_rows_ref
  17.1 0.6 fusion.4
  17.7 0.4 copy.27
  18.1 0.2 pad_maximum_fusion.1
  18.4 1.3 collective-permute-start.2
  19.7 4.0 %collective-permute-start.3 = (f32[3,129,72]{2,0,1:T(4,128)S(1)}, f32[3,129,72]{2,0,1:T(4,128)S(1)}, u32[]{:S(2)}, u32[]{:S(2)}) collective-permute-start(f32[3,129,72]{2,0,1:T(4,128)S(1)} %get-tuple-element.23), channel_id=1, source_target_pairs={{0,1},{1,2},{2,3},{3,4},{4,5},{5,6},{6,7},{7,8},{8,9},{9,10},{10,1... | collective-permute-start | bytes 334376 | tf_op jit(solution)/shard_map/ppermute | solution.py:21
  23.9 0.2 broadcast_in_dim.72
  24.1 0.2 broadcast_in_dim.74
  24.3 3.4 %collective-permute-done.2 = f32[3,129,72]{2,0,1:T(4,128)S(1)} collective-permute-done((f32[3,129,72]{2,0,1:T(4,128)S(1)}, f32[3,129,72]{2,0,1:T(4,128)S(1)}, u32[]{:S(2)}, u32[]{:S(2)}) %collective-permute-start.2) | collective-permute-done | bytes 111488 | tf_op jit(solution)/shard_map/ppermute | solution.py:21
  27.7 1.8 %collective-permute-done.3 = f32[3,129,72]{2,0,1:T(4,128)S(1)} collective-permute-done((f32[3,129,72]{2,0,1:T(4,128)S(1)}, f32[3,129,72]{2,0,1:T(4,128)S(1)}, u32[]{:S(2)}, u32[]{:S(2)}) %collective-permute-start.3) | collective-permute-done | bytes 111488 | tf_op jit(solution)/shard_map/ppermute | solution.py:21
  29.5 5.7 %fusion.6.source_cols_ref.perm_cols_ref.head_cols_ref = f32[129,72,128]{2,1,0:T(8,128)} fusion(f32[3,129,72]{2,0,1:T(4,128)S(1)} %collective-permute-done.3, f32[3,129,72]{2,0,1:T(4,128)S(1)} %collective-permute-done.2, f32[8]{0:T(128)S(1)} %pad.8.clone, s32[8]{0:T(128)S(1)} %compare_select_fusion.4, pred[8]{0:T(512)(128)(4,1)S(1)} %compare_or_fusion), kind=kOutput, calls=%fused_computation.11 | convolution fusion | flops 114281600 | bytes 4978440 | tf_op jit(solution)/shard_map/kmr,kl->mrl/dot_general | solution.py:203
  35.2 28.0 %shard_map.103 = (bf16[64,64,128]{2,1,0:T(8,128)(2,1)}, f32[64,64,128]{2,1,0:T(8,128)}) custom-call(f32[72,256]{1,0:T(8,128)} %and_convert_fusion.mask_ref, f32[64,128]{1,0:T(8,128)} %source_ref.1, f32[129,8,128]{2,1,0:T(8,128)} %copy-done.1, f32[129,72,128]{2,1,0:T(8,128)} %fusion.6.source_cols_ref.perm_cols_ref.head_cols_ref, f32[64,64,128]{2,1,0:T(8,128)} %perm_ref.1, ...), custom_call_target="tpu_custom_call" | custom-call | flops 94371840 | bytes 7340032 | tf_op jit(solution)/shard_map/pallas_call | solution.py:79
  63.2 3.8 %copy.37 = f32[64,64,128]{0,2,1:T(8,128)} copy(f32[64,64,128]{2,1,0:T(8,128)} %get-tuple-element.6) | data formatting | bytes 4194304 | tf_op jit(solution)/shard_map/reshape | solution.py:211
  67.0 5.0 %gather_fusion = f32[1024,64]{1,0:T(8,128)S(1)} fusion(f32[64,8192]{0,1:T(8,128)} %bitcast.53, s32[1024]{0:T(1024)S(1)} %broadcast_clamp_fusion), kind=kCustom, calls=%fused_computation | custom fusion | bytes 528384 | tf_op jit(solution)/shard_map/jit(_take)/gather | solution.py:211
  72.0 0.2 copy.29
  72.3 1.0 copy.30
  73.3 13.3 %all-to-all-start = ((f32[128,1,512]{2,1,0:T(1,128)}), f32[128,1,512]{2,1,0:T(1,128)S(1)}, u32[]{:S(2)}, u32[]{:S(2)}) async-start(f32[128,1,512]{2,1,0:T(1,128)} %copy.30), calls=%async_computation | async-start | bytes 524288 | tf_op jit(solution)/shard_map/all_to_all | solution.py:110
  86.6 0.1 reduce_sum.29
  86.9 0.4 div.70
  87.3 10.4 %all-to-all-done = f32[128,1,512]{2,1,0:T(1,128)S(1)} async-done(((f32[128,1,512]{2,1,0:T(1,128)}), f32[128,1,512]{2,1,0:T(1,128)S(1)}, u32[]{:S(2)}, u32[]{:S(2)}) %all-to-all-start) | async-done | bytes 262176 | tf_op jit(solution)/shard_map/all_to_all | solution.py:110
  97.7 0.2 reduce_sum.27
  97.9 0.8 broadcast_in_dim.77
  98.8 4.3 %all-to-all-start.1 = ((f32[128,1,512]{2,1,0:T(1,128)}), f32[128,1,512]{2,1,0:T(1,128)S(1)}, u32[]{:S(2)}, u32[]{:S(2)}) async-start(f32[128,1,512]{2,1,0:T(1,128)} %broadcast_in_dim.77), calls=%async_computation.1 | async-start | bytes 524288 | tf_op jit(solution)/shard_map/all_to_all | solution.py:112
  103.1 1.6 %subtract_multiply_fusion = f32[64,64,128]{2,1,0:T(8,128)} fusion(f32[64,64,128]{2,1,0:T(8,128)S(1)} %copy-done, f32[64,128]{1,0:T(8,128)S(1)} %broadcast_multiply_fusion), kind=kLoop, calls=%fused_computation.4 | loop fusion | flops 1048576 | bytes 4227072 | tf_op jit(solution)/shard_map/div | solution.py:218
  104.6 9.6 %all-to-all-done.1 = f32[128,1,512]{2,1,0:T(1,128)S(1)} async-done(((f32[128,1,512]{2,1,0:T(1,128)}), f32[128,1,512]{2,1,0:T(1,128)S(1)}, u32[]{:S(2)}, u32[]{:S(2)}) %all-to-all-start.1) | async-done | bytes 262176 | tf_op jit(solution)/shard_map/all_to_all | solution.py:112
  114.3 0.6 reduce.7
  115.1 0.5 copy-done.3
  115.7 0.4 sub.44
  116.1 1.8 %fusion.54 = (f32[128,512]{1,0:T(8,128)S(1)}, f32[128,512]{1,0:T(8,128)S(1)}) fusion(f32[128,1,512]{2,1,0:T(1,128)S(1)} %all-to-all-done.1, f32[128,1,512]{2,1,0:T(1,128)S(1)} %sub.44, f32[128,1,512]{2,1,0:T(1,128)S(1)} %div.70), kind=kLoop, calls=%fused_computation.87 | loop fusion | flops 196608 | bytes 1310720 | tf_op jit(solution)/shard_map/div | solution.py:135
  118.0 0.4 fusion.57
  118.5 5.8 %cholesky.17 = f32[64,64]{1,0:T(8,128)S(1)} custom-call(f32[64,64]{1,0:T(8,128)S(1)} %fusion.29), custom_call_target="Cholesky" | custom-call | tf_op jit(solution)/shard_map/jit(cholesky)/cholesky | solution.py:142
  124.4 0.7 compare_reduce_fusion
  125.1 0.7 fusion.24
  125.8 4.9 %custom-call.8 = f32[1,64,64]{1,2,0:T(8,128)S(1)} custom-call(f32[1,64,64]{2,1,0:T(8,128)S(1)} %fusion.24), custom_call_target="InvertDiagBlocksLowerTriangular" | custom-call | tf_op jit(solution)/shard_map/triangular_solve | solution.py:144
  130.7 1.5 %fusion.12 = f32[64,64]{1,0:T(8,128)S(1)} fusion(f32[64,1024]{1,0:T(8,128)} %copy-done.3, f32[64,1024]{1,0:T(8,128)} %param.15, f32[1024]{0:T(1024)S(1)} %sqrt.3, f32[1024]{0:T(1024)S(1)} %copy-done.7, f32[1024]{0:T(1024)S(1)} %copy-done.6, f32[1024]{0:T(1024)S(1)} %broadcast_multiply_fusion.1), kind=kOutput, calls=%fused_computation.19 | convolution fusion | flops 50724864 | bytes 557056 | tf_op jit(solution)/shard_map/dot_general | solution.py:141
  132.3 0.2 fusion.26
  132.5 0.2 convolution_bitcast_fusion
  132.7 5.7 %copy_add_fusion = f32[64,64,128]{2,0,1:T(8,128)S(1)} fusion(f32[64,64,128]{2,1,0:T(8,128)S(1)} %copy-done, f32[64,64,1]{0,1,2:T(8,128)S(1)} %convolution_bitcast_fusion, f32[64,64,128]{2,1,0:T(8,128)} %subtract_multiply_fusion), kind=kOutput, calls=%fused_computation.1 | convolution fusion | flops 403177472 | bytes 6307840 | tf_op jit(solution)/shard_map/mrc,mn->nrc/dot_general | solution.py:221
  138.4 2.5 %copy.35 = f32[64,64,128]{2,1,0:T(8,128)} copy(f32[64,64,128]{2,0,1:T(8,128)S(1)} %copy_add_fusion) | data formatting | bytes 4194304
  (55 shorter events, 1.4 us)
Async XLA Ops:
  0.6 14.1 %copy-start.2 = (bf16[64,64,128]{2,1,0:T(8,128)(2,1)S(1)}, bf16[64,64,128]{2,1,0:T(8,128)(2,1)}, u32[]{:S(2)}) copy-start(bf16[64,64,128]{2,1,0:T(8,128)(2,1)} %head_ref.1) | copy-start | bytes 3145732
  3.6 13.3 %collective-permute-start = (f32[3,129,128]{2,0,1:T(4,128)S(1)}, f32[3,129,128]{2,0,1:T(4,128)S(1)}, u32[]{:S(2)}, u32[]{:S(2)}) collective-permute-start(f32[3,129,128]{2,0,1:T(4,128)S(1)} %maximum_bitcast_fusion), channel_id=1, source_target_pairs={{16,0},{32,16},{48,32},{64,48},{80,64},{96,80},{112,96},{17,1},{33... | collective-permute-start | bytes 594440 | tf_op jit(solution)/shard_map/ppermute | solution.py:21
  6.9 8.8 %copy-start.4 = (f32[64,128]{1,0:T(8,128)S(1)}, f32[64,128]{1,0:T(8,128)}, u32[]{:S(2)}) copy-start(f32[64,128]{1,0:T(8,128)} %source_ref.1) | copy-start | bytes 98308
  6.9 9.0 %copy-start.5 = (s32[4,256]{1,0:T(4,128)S(1)}, s32[4,256]{1,0:T(4,128)}, u32[]{:S(2)}) copy-start(s32[4,256]{1,0:T(4,128)} %param.11) | copy-start | bytes 12292
  6.9 9.1 %copy-start.8 = (s32[4]{0:T(128)S(1)}, s32[4]{0:T(128)}, u32[]{:S(2)}) copy-start(s32[4]{0:T(128)} %param.12) | copy-start | bytes 52
  7.0 9.9 %collective-permute-start.1 = (f32[3,129,128]{2,0,1:T(4,128)S(1)}, f32[3,129,128]{2,0,1:T(4,128)S(1)}, u32[]{:S(2)}, u32[]{:S(2)}) collective-permute-start(f32[3,129,128]{2,0,1:T(4,128)S(1)} %maximum_bitcast_fusion.1), channel_id=1, source_target_pairs={{0,16},{16,32},{32,48},{48,64},{64,80},{80,96},{96,112},{1,17},{17... | collective-permute-start | bytes 594440 | tf_op jit(solution)/shard_map/ppermute | solution.py:21
  17.1 6.9 %copy-start.1 = (f32[129,8,128]{2,1,0:T(8,128)}, f32[129,8,128]{2,1,0:T(8,128)S(1)}, u32[]{:S(2)}) copy-start(f32[129,8,128]{2,1,0:T(8,128)S(1)} %pad_maximum_fusion.source_rows_ref.perm_rows_ref.head_rows_ref) | copy-start | bytes 1585156
  18.4 9.3 %collective-permute-start.2 = (f32[3,129,72]{2,0,1:T(4,128)S(1)}, f32[3,129,72]{2,0,1:T(4,128)S(1)}, u32[]{:S(2)}, u32[]{:S(2)}) collective-permute-start(f32[3,129,72]{2,0,1:T(4,128)S(1)} %get-tuple-element.22), channel_id=1, source_target_pairs={{1,0},{2,1},{3,2},{4,3},{5,4},{6,5},{7,6},{8,7},{9,8},{10,9},{11,1... | collective-permute-start | bytes 334376 | tf_op jit(solution)/shard_map/ppermute | solution.py:21
  19.7 9.8 %collective-permute-start.3 = (f32[3,129,72]{2,0,1:T(4,128)S(1)}, f32[3,129,72]{2,0,1:T(4,128)S(1)}, u32[]{:S(2)}, u32[]{:S(2)}) collective-permute-start(f32[3,129,72]{2,0,1:T(4,128)S(1)} %get-tuple-element.23), channel_id=1, source_target_pairs={{0,1},{1,2},{2,3},{3,4},{4,5},{5,6},{6,7},{7,8},{8,9},{9,10},{10,1... | collective-permute-start | bytes 334376 | tf_op jit(solution)/shard_map/ppermute | solution.py:21
  72.0 14.6 %copy-start.6 = (f32[1024]{0:T(1024)S(1)}, f32[1024]{0:T(1024)}, u32[]{:S(2)}) copy-start(f32[1024]{0:T(1024)} %param.14) | copy-start | bytes 12292
  72.0 14.6 %copy-start = (f32[64,64,128]{2,1,0:T(8,128)S(1)}, f32[64,64,128]{2,1,0:T(8,128)}, u32[]{:S(2)}) copy-start(f32[64,64,128]{2,1,0:T(8,128)} %perm_ref.1) | copy-start | bytes 6291460
  73.3 24.4 %all-to-all-start = ((f32[128,1,512]{2,1,0:T(1,128)}), f32[128,1,512]{2,1,0:T(1,128)S(1)}, u32[]{:S(2)}, u32[]{:S(2)}) async-start(f32[128,1,512]{2,1,0:T(1,128)} %copy.30), calls=%async_computation | async-start | bytes 524288 | tf_op jit(solution)/shard_map/all_to_all | solution.py:110
  98.8 15.5 %all-to-all-start.1 = ((f32[128,1,512]{2,1,0:T(1,128)}), f32[128,1,512]{2,1,0:T(1,128)S(1)}, u32[]{:S(2)}, u32[]{:S(2)}) async-start(f32[128,1,512]{2,1,0:T(1,128)} %broadcast_in_dim.77), calls=%async_computation.1 | async-start | bytes 524288 | tf_op jit(solution)/shard_map/all_to_all | solution.py:112
  115.0 0.7 copy-start.3
  115.0 15.7 %copy-start.7 = (f32[1024]{0:T(1024)S(1)}, f32[1024]{0:T(1024)}, u32[]{:S(2)}) copy-start(f32[1024]{0:T(1024)} %param.13) | copy-start | bytes 12292

commit v7 on v6

--- a/solution.py
+++ b/solution.py
@@ -29,13 +29,19 @@
     return (~gap) & (global_index >= 0) & (global_index < local * lax.axis_size(axis))
 
 
-def stencil_kernel(mask_ref, source_ref, source_rows_ref, source_cols_ref, perm_ref, head_ref,
+def stencil_kernel(mask_ref, selector_ref, source_ref, source_rows_ref, source_cols_ref, perm_ref, head_ref,
                    perm_rows_ref, head_rows_ref, perm_cols_ref, head_cols_ref, out16_ref, out32_ref):
     rows, cols = perm_ref.shape[1], perm_ref.shape[2]
     ext_rows, ext_cols = rows + 8, 2 * cols
 
+    selector = selector_ref[...]
+
     def extend(interior, halo_rows, halo_cols):
-        return jnp.concatenate([jnp.concatenate([interior, halo_rows], axis=0), halo_cols], axis=1)
+        placed = lax.dot_general(
+            halo_cols, selector, (((0,), (0,)), ((), ())), precision=lax.Precision.HIGHEST,
+            preferred_element_type=jnp.float32,
+        )
+        return jnp.concatenate([jnp.concatenate([interior, halo_rows], axis=0), placed], axis=1)
 
     inside = mask_ref[...] > 0.5
     source = extend(source_ref[...], source_rows_ref[0], source_cols_ref[0])
@@ -68,7 +74,7 @@
     lax.fori_loop(0, perm_ref.shape[0], member, 0)
 
 
-def run_stencil(mask, source, halo_rows, halo_cols, perm, head, block):
+def run_stencil(mask, selector, source, halo_rows, halo_cols, perm, head, block):
     members, rows, cols = perm.shape
     blocks = members // block
     full2 = lambda shape: pl.BlockSpec(shape, lambda i: (0, 0))
@@ -81,15 +87,16 @@
         grid=(blocks,),
         in_specs=[
             full2(mask.shape),
+            full2(selector.shape),
             full2(source.shape),
             last((8, cols)),
-            last((ext_rows, cols)),
+            last((8, ext_rows)),
             member_block((rows, cols), 0),
             member_block((rows, cols), 0),
             member_block((8, cols), 0),
             member_block((8, cols), blocks),
-            member_block((ext_rows, cols), 0),
-            member_block((ext_rows, cols), blocks),
+            member_block((8, ext_rows), 0),
+            member_block((8, ext_rows), blocks),
         ],
         out_specs=[member_block((rows, cols), 0), member_block((rows, cols), 0)],
         out_shape=[
@@ -99,7 +106,7 @@
         cost_estimate=pl.CostEstimate(
             flops=cells * 80, transcendentals=cells * 2, bytes_accessed=members * rows * cols * 14
         ),
-    )(mask, source, halo_rows, halo_cols, perm, head, halo_rows, halo_rows, halo_cols, halo_cols)
+    )(mask, selector, source, halo_rows, halo_cols, perm, head, halo_rows, halo_rows, halo_cols, halo_cols)
 
 
 def broadcast_from_owners(value, axes):
@@ -200,12 +207,12 @@
     from_left = send(border_cols[8 - width :], "col", True)
     from_right = send(border_cols[:width], "col", False)
     received = jnp.concatenate([from_right, jnp.zeros((8 - 2 * width,) + from_right.shape[1:], f32), from_left], axis=0)
-    halo_cols = jnp.einsum("kmr,kl->mrl", received, selector, precision=highest)
+    halo_cols = jnp.moveaxis(received, 0, 1)
     inside = circular_inside("row", row_count, width, ext_rows)[:, None] & circular_inside(
         "col", col_count, width, ext_cols
     )[None, :]
     pressure_low, hydraulic_head = run_stencil(
-        inside.astype(f32), recharge, halo_rows, halo_cols, logarithmic_conductivity, starting_head, 8
+        inside.astype(f32), selector, recharge, halo_rows, halo_cols, logarithmic_conductivity, starting_head, 8
     )
     group_total, well_count = well_cells.shape
     local_data = jnp.take(hydraulic_head.reshape(member_count, row_count * col_count), well_cells.reshape(-1), axis=1)

time: 142 us -> 155 us (1.092)
  Pallas kernels: 28 us -> 45.5 us
  matrix products: 19.6 us -> 13.8 us
  other arithmetic: 18.9 us -> 20.5 us
    pallas_call x1, Pallas kernels: 28 us -> 45.5 us  [run_stencil(): pl.pallas_call(stencil_kernel, grid=(blocks,), in_specs=[full2(mask.shape...]
    dot_general x1 -> x0, matrix products: 5.72 us -> none  [per_device(): halo_cols = jnp.einsum('kmr,kl->mrl', received, selector, precision=highest)]
where the time goes in v7:
time: 155 us; the launch traced here: 154 us
  Pallas kernels  45.5 us (29%)
  starting transfers between devices  29.7 us (19%)
  waiting for transfers between devices  25.3 us (16%)
  other arithmetic  20.5 us (13%)
  local copies, waits for them, and re-layouts  18.4 us (12%)
  matrix products  13.8 us (9%)
    pallas_call x1, Pallas kernels, run_stencil(): pl.pallas_call(stencil_kernel, grid=(blocks,), in_specs=[full2(mask.shape...  45.5 us
    all_to_all x1, starting transfers between devices, broadcast_from_owners(): own_chunk = lax.all_to_all(chunks, axes, 0, 0, tiled=True).sum(axis=0)  13.3 us
    ppermute x4, starting transfers between devices, send(): return lax.ppermute(piece, axis, pairs)  12.1 us
    all_to_all x1, waiting for transfers between devices, broadcast_from_owners(): own_chunk = lax.all_to_all(chunks, axes, 0, 0, tiled=True).sum(axis=0)  10.4 us
    all_to_all x1, waiting for transfers between devices, broadcast_from_owners(): return lax.all_to_all(spread, axes, 0, 0, tiled=True).reshape(value.shape)  9.65 us
    another operation x3, other arithmetic, blending_weights(): factor = jnp.linalg.cholesky(system)  6.6 us
    dot_general x1, matrix products, per_device(): jnp.einsum('mrc,mn->nrc', anomalies, mixing, precision=lax.Precision.HIGH...  5.68 us
    another operation x2, other arithmetic, blending_weights(): lax.linalg.triangular_solve(factor, half_solved, left_side=True, lower=Tr...  5.59 us
  transfers between devices with their start and end apart: 6, of which 4 were waited for; matrix products, arithmetic and copies ran while one was open for 6% of the time, Pallas kernels for 0%

profile of v7, /device:TPU:1, one launch (start us, length us, event | category | flops | bytes accessed | tf_op | source)
XLA Modules:
  0.0 154.4 jit_solution(982542874521889276)
XLA Ops:
  0.6 1.2 fusion.45
  1.8 1.0 slice_convert_fusion.1
  2.8 0.7 slice_bitcast_fusion.1
  3.6 3.3 %collective-permute-start = (f32[3,129,128]{2,0,1:T(4,128)S(1)}, f32[3,129,128]{2,0,1:T(4,128)S(1)}, u32[]{:S(2)}, u32[]{:S(2)}) collective-permute-start(f32[3,129,128]{2,0,1:T(4,128)S(1)} %maximum_bitcast_fusion.1), channel_id=1, source_target_pairs={{16,0},{32,16},{48,32},{64,48},{80,64},{96,80},{112,96},{17,1},{33... | collective-permute-start | bytes 594440 | tf_op jit(solution)/shard_map/ppermute | solution.py:21
  7.0 3.6 %collective-permute-start.1 = (f32[3,129,128]{2,0,1:T(4,128)S(1)}, f32[3,129,128]{2,0,1:T(4,128)S(1)}, u32[]{:S(2)}, u32[]{:S(2)}) collective-permute-start(f32[3,129,128]{2,0,1:T(4,128)S(1)} %maximum_bitcast_fusion.2), channel_id=1, source_target_pairs={{0,16},{16,32},{32,48},{48,64},{64,80},{80,96},{96,112},{1,17},{17... | collective-permute-start | bytes 594440 | tf_op jit(solution)/shard_map/ppermute | solution.py:21
  10.6 4.1 %fusion.29 = f32[8,64,64]{2,0,1:T(8,128)S(1)} fusion(f32[64,64,128]{2,1,0:T(8,128)} %perm_ref.1, s32[8]{0:T(128)S(1)} %compare_select_fusion.4, pred[8]{0:T(512)(128)(4,1)S(1)} %compare_or_fusion), kind=kOutput, calls=%fused_computation.54 | convolution fusion | flops 50333696 | bytes 2228264 | tf_op jit(solution)/shard_map/dot_general | solution.py:196
  14.7 0.9 fusion.31
  15.7 0.2 convolution_bitcast_fusion.1
  16.2 0.7 and_convert_fusion.mask_ref
  16.9 0.7 fusion.27.selector_ref
  17.6 0.1 pad_maximum_fusion.source_rows_ref.perm_rows_ref.head_rows_ref
  17.8 0.6 fusion.4
  18.3 0.4 copy.27
  18.7 0.2 pad_maximum_fusion.1
  19.0 1.3 collective-permute-start.2
  20.3 4.0 %collective-permute-start.3 = (f32[3,129,72]{2,0,1:T(4,128)S(1)}, f32[3,129,72]{2,0,1:T(4,128)S(1)}, u32[]{:S(2)}, u32[]{:S(2)}) collective-permute-start(f32[3,129,72]{2,0,1:T(4,128)S(1)} %get-tuple-element.23), channel_id=1, source_target_pairs={{0,1},{1,2},{2,3},{3,4},{4,5},{5,6},{6,7},{7,8},{8,9},{9,10},{10,1... | collective-permute-start | bytes 334376 | tf_op jit(solution)/shard_map/ppermute | solution.py:21
  24.5 0.2 broadcast_in_dim.72
  24.8 0.2 broadcast_in_dim.74
  24.9 3.4 %collective-permute-done.2 = f32[3,129,72]{2,0,1:T(4,128)S(1)} collective-permute-done((f32[3,129,72]{2,0,1:T(4,128)S(1)}, f32[3,129,72]{2,0,1:T(4,128)S(1)}, u32[]{:S(2)}, u32[]{:S(2)}) %collective-permute-start.2) | collective-permute-done | bytes 111488 | tf_op jit(solution)/shard_map/ppermute | solution.py:21
  28.3 1.8 %collective-permute-done.3 = f32[3,129,72]{2,0,1:T(4,128)S(1)} collective-permute-done((f32[3,129,72]{2,0,1:T(4,128)S(1)}, f32[3,129,72]{2,0,1:T(4,128)S(1)}, u32[]{:S(2)}, u32[]{:S(2)}) %collective-permute-start.3) | collective-permute-done | bytes 111488 | tf_op jit(solution)/shard_map/ppermute | solution.py:21
  30.1 1.0 maximum_bitcast_fusion.source_cols_ref.perm_cols_ref.head_cols_ref
  31.1 45.5 %shard_map.103 = (bf16[64,64,128]{2,1,0:T(8,128)(2,1)}, f32[64,64,128]{2,1,0:T(8,128)}) custom-call(f32[72,256]{1,0:T(8,128)} %and_convert_fusion.mask_ref, f32[8,128]{1,0:T(8,128)} %fusion.27.selector_ref, f32[64,128]{1,0:T(8,128)} %source_ref.1, f32[129,8,128]{2,1,0:T(8,128)} %copy-done.1, ...), custom_call_target="tpu_custom_call" | custom-call | flops 94371840 | bytes 7340032 | tf_op jit(solution)/shard_map/pallas_call | solution.py:85
  76.6 3.8 %copy.37 = f32[64,64,128]{0,2,1:T(8,128)} copy(f32[64,64,128]{2,1,0:T(8,128)} %get-tuple-element.6) | data formatting | bytes 4194304 | tf_op jit(solution)/shard_map/reshape | solution.py:218
  80.4 5.0 %gather_fusion = f32[1024,64]{1,0:T(8,128)S(1)} fusion(f32[64,8192]{0,1:T(8,128)} %bitcast.54, s32[1024]{0:T(1024)S(1)} %broadcast_clamp_fusion), kind=kCustom, calls=%fused_computation | custom fusion | bytes 528384 | tf_op jit(solution)/shard_map/jit(_take)/gather | solution.py:218
  85.4 0.2 copy.29
  85.7 1.0 copy.30
  86.7 13.3 %all-to-all-start = ((f32[128,1,512]{2,1,0:T(1,128)}), f32[128,1,512]{2,1,0:T(1,128)S(1)}, u32[]{:S(2)}, u32[]{:S(2)}) async-start(f32[128,1,512]{2,1,0:T(1,128)} %copy.30), calls=%async_computation | async-start | bytes 524288 | tf_op jit(solution)/shard_map/all_to_all | solution.py:117
  100.2 0.4 div.70
  100.7 10.4 %all-to-all-done = f32[128,1,512]{2,1,0:T(1,128)S(1)} async-done(((f32[128,1,512]{2,1,0:T(1,128)}), f32[128,1,512]{2,1,0:T(1,128)S(1)}, u32[]{:S(2)}, u32[]{:S(2)}) %all-to-all-start) | async-done | bytes 262176 | tf_op jit(solution)/shard_map/all_to_all | solution.py:117
  111.1 0.2 reduce_sum.27
  111.3 0.8 broadcast_in_dim.77
  112.2 4.3 %all-to-all-start.1 = ((f32[128,1,512]{2,1,0:T(1,128)}), f32[128,1,512]{2,1,0:T(1,128)S(1)}, u32[]{:S(2)}, u32[]{:S(2)}) async-start(f32[128,1,512]{2,1,0:T(1,128)} %broadcast_in_dim.77), calls=%async_computation.1 | async-start | bytes 524288 | tf_op jit(solution)/shard_map/all_to_all | solution.py:119
  116.5 1.6 %subtract_multiply_fusion = f32[64,64,128]{2,1,0:T(8,128)} fusion(f32[64,64,128]{2,1,0:T(8,128)S(1)} %copy-done, f32[64,128]{1,0:T(8,128)S(1)} %broadcast_multiply_fusion), kind=kLoop, calls=%fused_computation.4 | loop fusion | flops 1048576 | bytes 4227072 | tf_op jit(solution)/shard_map/div | solution.py:225
  118.0 9.6 %all-to-all-done.1 = f32[128,1,512]{2,1,0:T(1,128)S(1)} async-done(((f32[128,1,512]{2,1,0:T(1,128)}), f32[128,1,512]{2,1,0:T(1,128)S(1)}, u32[]{:S(2)}, u32[]{:S(2)}) %all-to-all-start.1) | async-done | bytes 262176 | tf_op jit(solution)/shard_map/all_to_all | solution.py:119
  127.7 0.6 reduce.7
  128.5 0.5 copy-done.3
  129.1 0.4 sub.44
  129.5 1.8 %fusion.44 = (f32[128,512]{1,0:T(8,128)S(1)}, f32[128,512]{1,0:T(8,128)S(1)}) fusion(f32[128,1,512]{2,1,0:T(1,128)S(1)} %all-to-all-done.1, f32[128,1,512]{2,1,0:T(1,128)S(1)} %sub.44, f32[128,1,512]{2,1,0:T(1,128)S(1)} %div.70), kind=kLoop, calls=%fused_computation.78 | loop fusion | flops 196608 | bytes 1310720 | tf_op jit(solution)/shard_map/div | solution.py:142
  131.4 0.4 fusion.47
  131.9 5.8 %cholesky.17 = f32[64,64]{1,0:T(8,128)S(1)} custom-call(f32[64,64]{1,0:T(8,128)S(1)} %fusion.23), custom_call_target="Cholesky" | custom-call | tf_op jit(solution)/shard_map/jit(cholesky)/cholesky | solution.py:149
  137.8 0.7 compare_reduce_fusion
  138.5 0.7 fusion.18
  139.2 4.9 %custom-call.8 = f32[1,64,64]{1,2,0:T(8,128)S(1)} custom-call(f32[1,64,64]{2,1,0:T(8,128)S(1)} %fusion.18), custom_call_target="InvertDiagBlocksLowerTriangular" | custom-call | tf_op jit(solution)/shard_map/triangular_solve | solution.py:151
  144.1 1.5 fusion.6
  145.6 0.2 fusion.20
  145.9 0.2 convolution_bitcast_fusion
  146.1 5.7 %copy_add_fusion = f32[64,64,128]{2,0,1:T(8,128)S(1)} fusion(f32[64,64,128]{2,1,0:T(8,128)S(1)} %copy-done, f32[64,64,1]{0,1,2:T(8,128)S(1)} %convolution_bitcast_fusion, f32[64,64,128]{2,1,0:T(8,128)} %subtract_multiply_fusion), kind=kOutput, calls=%fused_computation.1 | convolution fusion | flops 403177472 | bytes 6307840 | tf_op jit(solution)/shard_map/mrc,mn->nrc/dot_general | solution.py:228
  151.8 2.5 %copy.35 = f32[64,64,128]{2,1,0:T(8,128)} copy(f32[64,64,128]{2,0,1:T(8,128)S(1)} %copy_add_fusion) | data formatting | bytes 4194304
  (56 shorter events, 1.6 us)
Async XLA Ops:
  0.6 14.1 %copy-start.2 = (bf16[64,64,128]{2,1,0:T(8,128)(2,1)S(1)}, bf16[64,64,128]{2,1,0:T(8,128)(2,1)}, u32[]{:S(2)}) copy-start(bf16[64,64,128]{2,1,0:T(8,128)(2,1)} %head_ref.1) | copy-start | bytes 3145732
  3.6 14.0 %collective-permute-start = (f32[3,129,128]{2,0,1:T(4,128)S(1)}, f32[3,129,128]{2,0,1:T(4,128)S(1)}, u32[]{:S(2)}, u32[]{:S(2)}) collective-permute-start(f32[3,129,128]{2,0,1:T(4,128)S(1)} %maximum_bitcast_fusion.1), channel_id=1, source_target_pairs={{16,0},{32,16},{48,32},{64,48},{80,64},{96,80},{112,96},{17,1},{33... | collective-permute-start | bytes 594440 | tf_op jit(solution)/shard_map/ppermute | solution.py:21
  6.9 8.8 %copy-start.4 = (f32[64,128]{1,0:T(8,128)S(1)}, f32[64,128]{1,0:T(8,128)}, u32[]{:S(2)}) copy-start(f32[64,128]{1,0:T(8,128)} %source_ref.1) | copy-start | bytes 98308
  6.9 9.0 %copy-start.5 = (s32[4,256]{1,0:T(4,128)S(1)}, s32[4,256]{1,0:T(4,128)}, u32[]{:S(2)}) copy-start(s32[4,256]{1,0:T(4,128)} %param.11) | copy-start | bytes 12292
  6.9 9.1 %copy-start.8 = (s32[4]{0:T(128)S(1)}, s32[4]{0:T(128)}, u32[]{:S(2)}) copy-start(s32[4]{0:T(128)} %param.12) | copy-start | bytes 52
  7.0 10.6 %collective-permute-start.1 = (f32[3,129,128]{2,0,1:T(4,128)S(1)}, f32[3,129,128]{2,0,1:T(4,128)S(1)}, u32[]{:S(2)}, u32[]{:S(2)}) collective-permute-start(f32[3,129,128]{2,0,1:T(4,128)S(1)} %maximum_bitcast_fusion.2), channel_id=1, source_target_pairs={{0,16},{16,32},{32,48},{48,64},{64,80},{80,96},{96,112},{1,17},{17... | collective-permute-start | bytes 594440 | tf_op jit(solution)/shard_map/ppermute | solution.py:21
  17.8 6.9 %copy-start.1 = (f32[129,8,128]{2,1,0:T(8,128)}, f32[129,8,128]{2,1,0:T(8,128)S(1)}, u32[]{:S(2)}) copy-start(f32[129,8,128]{2,1,0:T(8,128)S(1)} %pad_maximum_fusion.source_rows_ref.perm_rows_ref.head_rows_ref) | copy-start | bytes 1585156
  19.0 9.3 %collective-permute-start.2 = (f32[3,129,72]{2,0,1:T(4,128)S(1)}, f32[3,129,72]{2,0,1:T(4,128)S(1)}, u32[]{:S(2)}, u32[]{:S(2)}) collective-permute-start(f32[3,129,72]{2,0,1:T(4,128)S(1)} %get-tuple-element.22), channel_id=1, source_target_pairs={{1,0},{2,1},{3,2},{4,3},{5,4},{6,5},{7,6},{8,7},{9,8},{10,9},{11,1... | collective-permute-start | bytes 334376 | tf_op jit(solution)/shard_map/ppermute | solution.py:21
  20.3 9.8 %collective-permute-start.3 = (f32[3,129,72]{2,0,1:T(4,128)S(1)}, f32[3,129,72]{2,0,1:T(4,128)S(1)}, u32[]{:S(2)}, u32[]{:S(2)}) collective-permute-start(f32[3,129,72]{2,0,1:T(4,128)S(1)} %get-tuple-element.23), channel_id=1, source_target_pairs={{0,1},{1,2},{2,3},{3,4},{4,5},{5,6},{6,7},{7,8},{8,9},{9,10},{10,1... | collective-permute-start | bytes 334376 | tf_op jit(solution)/shard_map/ppermute | solution.py:21
  85.4 14.6 %copy-start.6 = (f32[1024]{0:T(1024)S(1)}, f32[1024]{0:T(1024)}, u32[]{:S(2)}) copy-start(f32[1024]{0:T(1024)} %param.14) | copy-start | bytes 12292
  85.4 14.6 %copy-start = (f32[64,64,128]{2,1,0:T(8,128)S(1)}, f32[64,64,128]{2,1,0:T(8,128)}, u32[]{:S(2)}) copy-start(f32[64,64,128]{2,1,0:T(8,128)} %perm_ref.1) | copy-start | bytes 6291460
  86.7 24.4 %all-to-all-start = ((f32[128,1,512]{2,1,0:T(1,128)}), f32[128,1,512]{2,1,0:T(1,128)S(1)}, u32[]{:S(2)}, u32[]{:S(2)}) async-start(f32[128,1,512]{2,1,0:T(1,128)} %copy.30), calls=%async_computation | async-start | bytes 524288 | tf_op jit(solution)/shard_map/all_to_all | solution.py:117
  112.2 15.5 %all-to-all-start.1 = ((f32[128,1,512]{2,1,0:T(1,128)}), f32[128,1,512]{2,1,0:T(1,128)S(1)}, u32[]{:S(2)}, u32[]{:S(2)}) async-start(f32[128,1,512]{2,1,0:T(1,128)} %broadcast_in_dim.77), calls=%async_computation.1 | async-start | bytes 524288 | tf_op jit(solution)/shard_map/all_to_all | solution.py:119
  128.4 0.7 copy-start.3
  128.4 15.7 %copy-start.7 = (f32[1024]{0:T(1024)S(1)}, f32[1024]{0:T(1024)}, u32[]{:S(2)}) copy-start(f32[1024]{0:T(1024)} %param.13) | copy-start | bytes 12292

commit v8 on v6

--- a/solution.py
+++ b/solution.py
@@ -65,7 +65,7 @@
         out16_ref[j] = final.astype(jnp.bfloat16)
         return carry
 
-    lax.fori_loop(0, perm_ref.shape[0], member, 0)
+    lax.fori_loop(0, perm_ref.shape[0], member, 0, unroll=2)
 
 
 def run_stencil(mask, source, halo_rows, halo_cols, perm, head, block):

time: 142 us -> 135 us (0.951)
  Pallas kernels: 28 us -> 21.6 us
    pallas_call x1, Pallas kernels: 28 us -> 21.6 us  [run_stencil(): pl.pallas_call(stencil_kernel, grid=(blocks,), in_specs=[full2(mask.shape...]
  transfers between devices with their start and end apart: 6 -> 6, of which waited for: 4 -> 4; matrix products, arithmetic and copies ran while one was open for 6% -> 7% of each run, Pallas kernels for 0% -> 0%
where the time goes in v8:
time: 135 us
  starting transfers between devices  29.7 us (22%)
  waiting for transfers between devices  25.3 us (19%)
  Pallas kernels  21.6 us (16%)
  matrix products  19.6 us (15%)
  other arithmetic  18.9 us (14%)
  local copies, waits for them, and re-layouts  18.4 us (14%)
    pallas_call x1, Pallas kernels, run_stencil(): pl.pallas_call(stencil_kernel, grid=(blocks,), in_specs=[full2(mask.shape...  21.6 us
    all_to_all x1, starting transfers between devices, broadcast_from_owners(): own_chunk = lax.all_to_all(chunks, axes, 0, 0, tiled=True).sum(axis=0)  13.3 us
    ppermute x4, starting transfers between devices, send(): return lax.ppermute(piece, axis, pairs)  12.1 us
    all_to_all x1, waiting for transfers between devices, broadcast_from_owners(): own_chunk = lax.all_to_all(chunks, axes, 0, 0, tiled=True).sum(axis=0)  10.4 us
    all_to_all x1, waiting for transfers between devices, broadcast_from_owners(): return lax.all_to_all(spread, axes, 0, 0, tiled=True).reshape(value.shape)  9.65 us
    another operation x3, other arithmetic, blending_weights(): factor = jnp.linalg.cholesky(system)  6.6 us
    dot_general x1, matrix products, per_device(): halo_cols = jnp.einsum('kmr,kl->mrl', received, selector, precision=highest)  5.72 us
    dot_general x1, matrix products, per_device(): jnp.einsum('mrc,mn->nrc', anomalies, mixing, precision=lax.Precision.HIGH...  5.68 us
  transfers between devices with their start and end apart: 6, of which 4 were waited for; matrix products, arithmetic and copies ran while one was open for 7% of the time, Pallas kernels for 0%

profile of v8, /device:TPU:1, one launch (start us, length us, event | category | flops | bytes accessed | tf_op | source)
XLA Modules:
  0.0 134.5 jit_solution(2105227920740969068)
XLA Ops:
  0.6 1.2 fusion.55
  1.8 1.0 slice_convert_fusion.1
  2.8 0.7 slice_bitcast_fusion.1
  3.6 3.3 %collective-permute-start = (f32[3,129,128]{2,0,1:T(4,128)S(1)}, f32[3,129,128]{2,0,1:T(4,128)S(1)}, u32[]{:S(2)}, u32[]{:S(2)}) collective-permute-start(f32[3,129,128]{2,0,1:T(4,128)S(1)} %maximum_bitcast_fusion), channel_id=1, source_target_pairs={{16,0},{32,16},{48,32},{64,48},{80,64},{96,80},{112,96},{17,1},{33... | collective-permute-start | bytes 594440 | tf_op jit(solution)/shard_map/ppermute | solution.py:21
  7.0 3.6 %collective-permute-start.1 = (f32[3,129,128]{2,0,1:T(4,128)S(1)}, f32[3,129,128]{2,0,1:T(4,128)S(1)}, u32[]{:S(2)}, u32[]{:S(2)}) collective-permute-start(f32[3,129,128]{2,0,1:T(4,128)S(1)} %maximum_bitcast_fusion.1), channel_id=1, source_target_pairs={{0,16},{16,32},{32,48},{48,64},{64,80},{80,96},{96,112},{1,17},{17... | collective-permute-start | bytes 594440 | tf_op jit(solution)/shard_map/ppermute | solution.py:21
  10.6 4.1 %fusion.35 = f32[8,64,64]{2,0,1:T(8,128)S(1)} fusion(f32[64,64,128]{2,1,0:T(8,128)} %perm_ref.1, s32[8]{0:T(128)S(1)} %compare_select_fusion.4, pred[8]{0:T(512)(128)(4,1)S(1)} %compare_or_fusion), kind=kOutput, calls=%fused_computation.60 | convolution fusion | flops 50333696 | bytes 2228264 | tf_op jit(solution)/shard_map/dot_general | solution.py:189
  14.7 0.9 fusion.38
  15.7 0.2 convolution_bitcast_fusion.1
  16.2 0.7 and_convert_fusion.mask_ref
  17.0 0.1 pad_maximum_fusion.source_rows_ref.perm_rows_ref.head_rows_ref
  17.1 0.6 fusion.4
  17.7 0.4 copy.27
  18.1 0.2 pad_maximum_fusion.1
  18.4 1.3 collective-permute-start.2
  19.7 4.0 %collective-permute-start.3 = (f32[3,129,72]{2,0,1:T(4,128)S(1)}, f32[3,129,72]{2,0,1:T(4,128)S(1)}, u32[]{:S(2)}, u32[]{:S(2)}) collective-permute-start(f32[3,129,72]{2,0,1:T(4,128)S(1)} %get-tuple-element.23), channel_id=1, source_target_pairs={{0,1},{1,2},{2,3},{3,4},{4,5},{5,6},{6,7},{7,8},{8,9},{9,10},{10,1... | collective-permute-start | bytes 334376 | tf_op jit(solution)/shard_map/ppermute | solution.py:21
  23.9 0.2 broadcast_in_dim.72
  24.1 0.2 broadcast_in_dim.74
  24.3 3.4 %collective-permute-done.2 = f32[3,129,72]{2,0,1:T(4,128)S(1)} collective-permute-done((f32[3,129,72]{2,0,1:T(4,128)S(1)}, f32[3,129,72]{2,0,1:T(4,128)S(1)}, u32[]{:S(2)}, u32[]{:S(2)}) %collective-permute-start.2) | collective-permute-done | bytes 111488 | tf_op jit(solution)/shard_map/ppermute | solution.py:21
  27.7 1.8 %collective-permute-done.3 = f32[3,129,72]{2,0,1:T(4,128)S(1)} collective-permute-done((f32[3,129,72]{2,0,1:T(4,128)S(1)}, f32[3,129,72]{2,0,1:T(4,128)S(1)}, u32[]{:S(2)}, u32[]{:S(2)}) %collective-permute-start.3) | collective-permute-done | bytes 111488 | tf_op jit(solution)/shard_map/ppermute | solution.py:21
  29.5 5.7 %fusion.6.source_cols_ref.perm_cols_ref.head_cols_ref = f32[129,72,128]{2,1,0:T(8,128)} fusion(f32[3,129,72]{2,0,1:T(4,128)S(1)} %collective-permute-done.3, f32[3,129,72]{2,0,1:T(4,128)S(1)} %collective-permute-done.2, f32[8]{0:T(128)S(1)} %pad.8.clone, s32[8]{0:T(128)S(1)} %compare_select_fusion.4, pred[8]{0:T(512)(128)(4,1)S(1)} %compare_or_fusion), kind=kOutput, calls=%fused_computation.11 | convolution fusion | flops 114281600 | bytes 4978440 | tf_op jit(solution)/shard_map/kmr,kl->mrl/dot_general | solution.py:203
  35.2 21.6 %shard_map.103 = (bf16[64,64,128]{2,1,0:T(8,128)(2,1)}, f32[64,64,128]{2,1,0:T(8,128)}) custom-call(f32[72,256]{1,0:T(8,128)} %and_convert_fusion.mask_ref, f32[64,128]{1,0:T(8,128)} %source_ref.1, f32[129,8,128]{2,1,0:T(8,128)} %copy-done.1, f32[129,72,128]{2,1,0:T(8,128)} %fusion.6.source_cols_ref.perm_cols_ref.head_cols_ref, f32[64,64,128]{2,1,0:T(8,128)} %perm_ref.1, ...), custom_call_target="tpu_custom_call" | custom-call | flops 94371840 | bytes 7340032 | tf_op jit(solution)/shard_map/pallas_call | solution.py:79
  56.8 3.8 %copy.37 = f32[64,64,128]{0,2,1:T(8,128)} copy(f32[64,64,128]{2,1,0:T(8,128)} %get-tuple-element.6) | data formatting | bytes 4194304 | tf_op jit(solution)/shard_map/reshape | solution.py:211
  60.6 5.0 %gather_fusion = f32[1024,64]{1,0:T(8,128)S(1)} fusion(f32[64,8192]{0,1:T(8,128)} %bitcast.53, s32[1024]{0:T(1024)S(1)} %broadcast_clamp_fusion), kind=kCustom, calls=%fused_computation | custom fusion | bytes 528384 | tf_op jit(solution)/shard_map/jit(_take)/gather | solution.py:211
  65.6 0.2 copy.29
  65.9 1.0 copy.30
  66.9 13.3 %all-to-all-start = ((f32[128,1,512]{2,1,0:T(1,128)}), f32[128,1,512]{2,1,0:T(1,128)S(1)}, u32[]{:S(2)}, u32[]{:S(2)}) async-start(f32[128,1,512]{2,1,0:T(1,128)} %copy.30), calls=%async_computation | async-start | bytes 524288 | tf_op jit(solution)/shard_map/all_to_all | solution.py:110
  80.2 0.1 reduce_sum.29
  80.4 0.4 div.70
  80.8 10.4 %all-to-all-done = f32[128,1,512]{2,1,0:T(1,128)S(1)} async-done(((f32[128,1,512]{2,1,0:T(1,128)}), f32[128,1,512]{2,1,0:T(1,128)S(1)}, u32[]{:S(2)}, u32[]{:S(2)}) %all-to-all-start) | async-done | bytes 262176 | tf_op jit(solution)/shard_map/all_to_all | solution.py:110
  91.3 0.2 reduce_sum.27
  91.5 0.8 broadcast_in_dim.77
  92.3 4.3 %all-to-all-start.1 = ((f32[128,1,512]{2,1,0:T(1,128)}), f32[128,1,512]{2,1,0:T(1,128)S(1)}, u32[]{:S(2)}, u32[]{:S(2)}) async-start(f32[128,1,512]{2,1,0:T(1,128)} %broadcast_in_dim.77), calls=%async_computation.1 | async-start | bytes 524288 | tf_op jit(solution)/shard_map/all_to_all | solution.py:112
  96.6 1.6 %subtract_multiply_fusion = f32[64,64,128]{2,1,0:T(8,128)} fusion(f32[64,64,128]{2,1,0:T(8,128)S(1)} %copy-done, f32[64,128]{1,0:T(8,128)S(1)} %broadcast_multiply_fusion), kind=kLoop, calls=%fused_computation.4 | loop fusion | flops 1048576 | bytes 4227072 | tf_op jit(solution)/shard_map/div | solution.py:218
  98.2 9.6 %all-to-all-done.1 = f32[128,1,512]{2,1,0:T(1,128)S(1)} async-done(((f32[128,1,512]{2,1,0:T(1,128)}), f32[128,1,512]{2,1,0:T(1,128)S(1)}, u32[]{:S(2)}, u32[]{:S(2)}) %all-to-all-start.1) | async-done | bytes 262176 | tf_op jit(solution)/shard_map/all_to_all | solution.py:112
  107.8 0.6 reduce.7
  108.7 0.5 copy-done.3
  109.2 0.4 sub.44
  109.7 1.8 %fusion.54 = (f32[128,512]{1,0:T(8,128)S(1)}, f32[128,512]{1,0:T(8,128)S(1)}) fusion(f32[128,1,512]{2,1,0:T(1,128)S(1)} %all-to-all-done.1, f32[128,1,512]{2,1,0:T(1,128)S(1)} %sub.44, f32[128,1,512]{2,1,0:T(1,128)S(1)} %div.70), kind=kLoop, calls=%fused_computation.87 | loop fusion | flops 196608 | bytes 1310720 | tf_op jit(solution)/shard_map/div | solution.py:135
  111.6 0.4 fusion.57
  112.1 5.8 %cholesky.17 = f32[64,64]{1,0:T(8,128)S(1)} custom-call(f32[64,64]{1,0:T(8,128)S(1)} %fusion.29), custom_call_target="Cholesky" | custom-call | tf_op jit(solution)/shard_map/jit(cholesky)/cholesky | solution.py:142
  117.9 0.7 compare_reduce_fusion
  118.7 0.7 fusion.24
  119.4 4.9 %custom-call.8 = f32[1,64,64]{1,2,0:T(8,128)S(1)} custom-call(f32[1,64,64]{2,1,0:T(8,128)S(1)} %fusion.24), custom_call_target="InvertDiagBlocksLowerTriangular" | custom-call | tf_op jit(solution)/shard_map/triangular_solve | solution.py:144
  124.3 1.5 %fusion.12 = f32[64,64]{1,0:T(8,128)S(1)} fusion(f32[64,1024]{1,0:T(8,128)} %copy-done.3, f32[64,1024]{1,0:T(8,128)} %param.15, f32[1024]{0:T(1024)S(1)} %sqrt.3, f32[1024]{0:T(1024)S(1)} %copy-done.7, f32[1024]{0:T(1024)S(1)} %copy-done.6, f32[1024]{0:T(1024)S(1)} %broadcast_multiply_fusion.1), kind=kOutput, calls=%fused_computation.19 | convolution fusion | flops 50724864 | bytes 557056 | tf_op jit(solution)/shard_map/dot_general | solution.py:141
  125.8 0.2 fusion.26
  126.1 0.2 convolution_bitcast_fusion
  126.3 5.7 %copy_add_fusion = f32[64,64,128]{2,0,1:T(8,128)S(1)} fusion(f32[64,64,128]{2,1,0:T(8,128)S(1)} %copy-done, f32[64,64,1]{0,1,2:T(8,128)S(1)} %convolution_bitcast_fusion, f32[64,64,128]{2,1,0:T(8,128)} %subtract_multiply_fusion), kind=kOutput, calls=%fused_computation.1 | convolution fusion | flops 403177472 | bytes 6307840 | tf_op jit(solution)/shard_map/mrc,mn->nrc/dot_general | solution.py:221
  132.0 2.5 %copy.35 = f32[64,64,128]{2,1,0:T(8,128)} copy(f32[64,64,128]{2,0,1:T(8,128)S(1)} %copy_add_fusion) | data formatting | bytes 4194304
  (55 shorter events, 1.4 us)
Async XLA Ops:
  0.6 14.1 %copy-start.2 = (bf16[64,64,128]{2,1,0:T(8,128)(2,1)S(1)}, bf16[64,64,128]{2,1,0:T(8,128)(2,1)}, u32[]{:S(2)}) copy-start(bf16[64,64,128]{2,1,0:T(8,128)(2,1)} %head_ref.1) | copy-start | bytes 3145732
  3.6 13.3 %collective-permute-start = (f32[3,129,128]{2,0,1:T(4,128)S(1)}, f32[3,129,128]{2,0,1:T(4,128)S(1)}, u32[]{:S(2)}, u32[]{:S(2)}) collective-permute-start(f32[3,129,128]{2,0,1:T(4,128)S(1)} %maximum_bitcast_fusion), channel_id=1, source_target_pairs={{16,0},{32,16},{48,32},{64,48},{80,64},{96,80},{112,96},{17,1},{33... | collective-permute-start | bytes 594440 | tf_op jit(solution)/shard_map/ppermute | solution.py:21
  6.9 8.8 %copy-start.4 = (f32[64,128]{1,0:T(8,128)S(1)}, f32[64,128]{1,0:T(8,128)}, u32[]{:S(2)}) copy-start(f32[64,128]{1,0:T(8,128)} %source_ref.1) | copy-start | bytes 98308
  6.9 9.0 %copy-start.5 = (s32[4,256]{1,0:T(4,128)S(1)}, s32[4,256]{1,0:T(4,128)}, u32[]{:S(2)}) copy-start(s32[4,256]{1,0:T(4,128)} %param.11) | copy-start | bytes 12292
  6.9 9.1 %copy-start.8 = (s32[4]{0:T(128)S(1)}, s32[4]{0:T(128)}, u32[]{:S(2)}) copy-start(s32[4]{0:T(128)} %param.12) | copy-start | bytes 52
  7.0 9.9 %collective-permute-start.1 = (f32[3,129,128]{2,0,1:T(4,128)S(1)}, f32[3,129,128]{2,0,1:T(4,128)S(1)}, u32[]{:S(2)}, u32[]{:S(2)}) collective-permute-start(f32[3,129,128]{2,0,1:T(4,128)S(1)} %maximum_bitcast_fusion.1), channel_id=1, source_target_pairs={{0,16},{16,32},{32,48},{48,64},{64,80},{80,96},{96,112},{1,17},{17... | collective-permute-start | bytes 594440 | tf_op jit(solution)/shard_map/ppermute | solution.py:21
  17.1 6.9 %copy-start.1 = (f32[129,8,128]{2,1,0:T(8,128)}, f32[129,8,128]{2,1,0:T(8,128)S(1)}, u32[]{:S(2)}) copy-start(f32[129,8,128]{2,1,0:T(8,128)S(1)} %pad_maximum_fusion.source_rows_ref.perm_rows_ref.head_rows_ref) | copy-start | bytes 1585156
  18.4 9.3 %collective-permute-start.2 = (f32[3,129,72]{2,0,1:T(4,128)S(1)}, f32[3,129,72]{2,0,1:T(4,128)S(1)}, u32[]{:S(2)}, u32[]{:S(2)}) collective-permute-start(f32[3,129,72]{2,0,1:T(4,128)S(1)} %get-tuple-element.22), channel_id=1, source_target_pairs={{1,0},{2,1},{3,2},{4,3},{5,4},{6,5},{7,6},{8,7},{9,8},{10,9},{11,1... | collective-permute-start | bytes 334376 | tf_op jit(solution)/shard_map/ppermute | solution.py:21
  19.7 9.8 %collective-permute-start.3 = (f32[3,129,72]{2,0,1:T(4,128)S(1)}, f32[3,129,72]{2,0,1:T(4,128)S(1)}, u32[]{:S(2)}, u32[]{:S(2)}) collective-permute-start(f32[3,129,72]{2,0,1:T(4,128)S(1)} %get-tuple-element.23), channel_id=1, source_target_pairs={{0,1},{1,2},{2,3},{3,4},{4,5},{5,6},{6,7},{7,8},{8,9},{9,10},{10,1... | collective-permute-start | bytes 334376 | tf_op jit(solution)/shard_map/ppermute | solution.py:21
  65.6 14.6 %copy-start.6 = (f32[1024]{0:T(1024)S(1)}, f32[1024]{0:T(1024)}, u32[]{:S(2)}) copy-start(f32[1024]{0:T(1024)} %param.14) | copy-start | bytes 12292
  65.6 14.6 %copy-start = (f32[64,64,128]{2,1,0:T(8,128)S(1)}, f32[64,64,128]{2,1,0:T(8,128)}, u32[]{:S(2)}) copy-start(f32[64,64,128]{2,1,0:T(8,128)} %perm_ref.1) | copy-start | bytes 6291460
  66.9 24.4 %all-to-all-start = ((f32[128,1,512]{2,1,0:T(1,128)}), f32[128,1,512]{2,1,0:T(1,128)S(1)}, u32[]{:S(2)}, u32[]{:S(2)}) async-start(f32[128,1,512]{2,1,0:T(1,128)} %copy.30), calls=%async_computation | async-start | bytes 524288 | tf_op jit(solution)/shard_map/all_to_all | solution.py:110
  92.3 15.5 %all-to-all-start.1 = ((f32[128,1,512]{2,1,0:T(1,128)}), f32[128,1,512]{2,1,0:T(1,128)S(1)}, u32[]{:S(2)}, u32[]{:S(2)}) async-start(f32[128,1,512]{2,1,0:T(1,128)} %broadcast_in_dim.77), calls=%async_computation.1 | async-start | bytes 524288 | tf_op jit(solution)/shard_map/all_to_all | solution.py:112
  108.5 0.7 copy-start.3
  108.5 15.7 %copy-start.7 = (f32[1024]{0:T(1024)S(1)}, f32[1024]{0:T(1024)}, u32[]{:S(2)}) copy-start(f32[1024]{0:T(1024)} %param.13) | copy-start | bytes 12292

commit v9 on v8

--- a/solution.py
+++ b/solution.py
@@ -65,7 +65,7 @@
         out16_ref[j] = final.astype(jnp.bfloat16)
         return carry
 
-    lax.fori_loop(0, perm_ref.shape[0], member, 0, unroll=2)
+    lax.fori_loop(0, perm_ref.shape[0], member, 0, unroll=4)
 
 
 def run_stencil(mask, source, halo_rows, halo_cols, perm, head, block):

time: 135 us -> 136 us (level)
  no operation moved by 1% of the time
where the time goes in v9:
time: 136 us
  starting transfers between devices  29.7 us (22%)
  waiting for transfers between devices  25.3 us (19%)
  Pallas kernels  22.7 us (17%)
  matrix products  19.6 us (14%)
  other arithmetic  18.9 us (14%)
  local copies, waits for them, and re-layouts  18.4 us (14%)
    pallas_call x1, Pallas kernels, run_stencil(): pl.pallas_call(stencil_kernel, grid=(blocks,), in_specs=[full2(mask.shape...  22.7 us
    all_to_all x1, starting transfers between devices, broadcast_from_owners(): own_chunk = lax.all_to_all(chunks, axes, 0, 0, tiled=True).sum(axis=0)  13.3 us
    ppermute x4, starting transfers between devices, send(): return lax.ppermute(piece, axis, pairs)  12.1 us
    all_to_all x1, waiting for transfers between devices, broadcast_from_owners(): own_chunk = lax.all_to_all(chunks, axes, 0, 0, tiled=True).sum(axis=0)  10.4 us
    all_to_all x1, waiting for transfers between devices, broadcast_from_owners(): return lax.all_to_all(spread, axes, 0, 0, tiled=True).reshape(value.shape)  9.65 us
    another operation x3, other arithmetic, blending_weights(): factor = jnp.linalg.cholesky(system)  6.6 us
    dot_general x1, matrix products, per_device(): halo_cols = jnp.einsum('kmr,kl->mrl', received, selector, precision=highest)  5.72 us
    dot_general x1, matrix products, per_device(): jnp.einsum('mrc,mn->nrc', anomalies, mixing, precision=lax.Precision.HIGH...  5.68 us
  transfers between devices with their start and end apart: 6, of which 4 were waited for; matrix products, arithmetic and copies ran while one was open for 7% of the time, Pallas kernels for 0%

profile of v9, /device:TPU:1, one launch (start us, length us, event | category | flops | bytes accessed | tf_op | source)
XLA Modules:
  0.0 135.7 jit_solution(9231313706221398104)
XLA Ops:
  0.6 1.2 fusion.55
  1.8 1.0 slice_convert_fusion.1
  2.8 0.7 slice_bitcast_fusion.1
  3.6 3.3 %collective-permute-start = (f32[3,129,128]{2,0,1:T(4,128)S(1)}, f32[3,129,128]{2,0,1:T(4,128)S(1)}, u32[]{:S(2)}, u32[]{:S(2)}) collective-permute-start(f32[3,129,128]{2,0,1:T(4,128)S(1)} %maximum_bitcast_fusion), channel_id=1, source_target_pairs={{16,0},{32,16},{48,32},{64,48},{80,64},{96,80},{112,96},{17,1},{33... | collective-permute-start | bytes 594440 | tf_op jit(solution)/shard_map/ppermute | solution.py:21
  7.0 3.6 %collective-permute-start.1 = (f32[3,129,128]{2,0,1:T(4,128)S(1)}, f32[3,129,128]{2,0,1:T(4,128)S(1)}, u32[]{:S(2)}, u32[]{:S(2)}) collective-permute-start(f32[3,129,128]{2,0,1:T(4,128)S(1)} %maximum_bitcast_fusion.1), channel_id=1, source_target_pairs={{0,16},{16,32},{32,48},{48,64},{64,80},{80,96},{96,112},{1,17},{17... | collective-permute-start | bytes 594440 | tf_op jit(solution)/shard_map/ppermute | solution.py:21
  10.6 4.1 %fusion.35 = f32[8,64,64]{2,0,1:T(8,128)S(1)} fusion(f32[64,64,128]{2,1,0:T(8,128)} %perm_ref.1, s32[8]{0:T(128)S(1)} %compare_select_fusion.4, pred[8]{0:T(512)(128)(4,1)S(1)} %compare_or_fusion), kind=kOutput, calls=%fused_computation.60 | convolution fusion | flops 50333696 | bytes 2228264 | tf_op jit(solution)/shard_map/dot_general | solution.py:189
  14.7 0.9 fusion.38
  15.7 0.2 convolution_bitcast_fusion.1
  16.2 0.7 and_convert_fusion.mask_ref
  17.0 0.1 pad_maximum_fusion.source_rows_ref.perm_rows_ref.head_rows_ref
  17.1 0.6 fusion.4
  17.7 0.4 copy.27
  18.1 0.2 pad_maximum_fusion.1
  18.4 1.3 collective-permute-start.2
  19.7 4.0 %collective-permute-start.3 = (f32[3,129,72]{2,0,1:T(4,128)S(1)}, f32[3,129,72]{2,0,1:T(4,128)S(1)}, u32[]{:S(2)}, u32[]{:S(2)}) collective-permute-start(f32[3,129,72]{2,0,1:T(4,128)S(1)} %get-tuple-element.23), channel_id=1, source_target_pairs={{0,1},{1,2},{2,3},{3,4},{4,5},{5,6},{6,7},{7,8},{8,9},{9,10},{10,1... | collective-permute-start | bytes 334376 | tf_op jit(solution)/shard_map/ppermute | solution.py:21
  23.9 0.2 broadcast_in_dim.72
  24.1 0.2 broadcast_in_dim.74
  24.3 3.4 %collective-permute-done.2 = f32[3,129,72]{2,0,1:T(4,128)S(1)} collective-permute-done((f32[3,129,72]{2,0,1:T(4,128)S(1)}, f32[3,129,72]{2,0,1:T(4,128)S(1)}, u32[]{:S(2)}, u32[]{:S(2)}) %collective-permute-start.2) | collective-permute-done | bytes 111488 | tf_op jit(solution)/shard_map/ppermute | solution.py:21
  27.7 1.8 %collective-permute-done.3 = f32[3,129,72]{2,0,1:T(4,128)S(1)} collective-permute-done((f32[3,129,72]{2,0,1:T(4,128)S(1)}, f32[3,129,72]{2,0,1:T(4,128)S(1)}, u32[]{:S(2)}, u32[]{:S(2)}) %collective-permute-start.3) | collective-permute-done | bytes 111488 | tf_op jit(solution)/shard_map/ppermute | solution.py:21
  29.5 5.7 %fusion.6.source_cols_ref.perm_cols_ref.head_cols_ref = f32[129,72,128]{2,1,0:T(8,128)} fusion(f32[3,129,72]{2,0,1:T(4,128)S(1)} %collective-permute-done.3, f32[3,129,72]{2,0,1:T(4,128)S(1)} %collective-permute-done.2, f32[8]{0:T(128)S(1)} %pad.8.clone, s32[8]{0:T(128)S(1)} %compare_select_fusion.4, pred[8]{0:T(512)(128)(4,1)S(1)} %compare_or_fusion), kind=kOutput, calls=%fused_computation.11 | convolution fusion | flops 114281600 | bytes 4978440 | tf_op jit(solution)/shard_map/kmr,kl->mrl/dot_general | solution.py:203
  35.2 22.7 %shard_map.103 = (bf16[64,64,128]{2,1,0:T(8,128)(2,1)}, f32[64,64,128]{2,1,0:T(8,128)}) custom-call(f32[72,256]{1,0:T(8,128)} %and_convert_fusion.mask_ref, f32[64,128]{1,0:T(8,128)} %source_ref.1, f32[129,8,128]{2,1,0:T(8,128)} %copy-done.1, f32[129,72,128]{2,1,0:T(8,128)} %fusion.6.source_cols_ref.perm_cols_ref.head_cols_ref, f32[64,64,128]{2,1,0:T(8,128)} %perm_ref.1, ...), custom_call_target="tpu_custom_call" | custom-call | flops 94371840 | bytes 7340032 | tf_op jit(solution)/shard_map/pallas_call | solution.py:79
  57.9 3.8 %copy.37 = f32[64,64,128]{0,2,1:T(8,128)} copy(f32[64,64,128]{2,1,0:T(8,128)} %get-tuple-element.6) | data formatting | bytes 4194304 | tf_op jit(solution)/shard_map/reshape | solution.py:211
  61.7 5.0 %gather_fusion = f32[1024,64]{1,0:T(8,128)S(1)} fusion(f32[64,8192]{0,1:T(8,128)} %bitcast.53, s32[1024]{0:T(1024)S(1)} %broadcast_clamp_fusion), kind=kCustom, calls=%fused_computation | custom fusion | bytes 528384 | tf_op jit(solution)/shard_map/jit(_take)/gather | solution.py:211
  66.7 0.2 copy.29
  67.0 1.0 copy.30
  68.0 13.3 %all-to-all-start = ((f32[128,1,512]{2,1,0:T(1,128)}), f32[128,1,512]{2,1,0:T(1,128)S(1)}, u32[]{:S(2)}, u32[]{:S(2)}) async-start(f32[128,1,512]{2,1,0:T(1,128)} %copy.30), calls=%async_computation | async-start | bytes 524288 | tf_op jit(solution)/shard_map/all_to_all | solution.py:110
  81.3 0.1 reduce_sum.29
  81.5 0.4 div.70
  82.0 10.4 %all-to-all-done = f32[128,1,512]{2,1,0:T(1,128)S(1)} async-done(((f32[128,1,512]{2,1,0:T(1,128)}), f32[128,1,512]{2,1,0:T(1,128)S(1)}, u32[]{:S(2)}, u32[]{:S(2)}) %all-to-all-start) | async-done | bytes 262176 | tf_op jit(solution)/shard_map/all_to_all | solution.py:110
  92.4 0.2 reduce_sum.27
  92.6 0.8 broadcast_in_dim.77
  93.5 4.3 %all-to-all-start.1 = ((f32[128,1,512]{2,1,0:T(1,128)}), f32[128,1,512]{2,1,0:T(1,128)S(1)}, u32[]{:S(2)}, u32[]{:S(2)}) async-start(f32[128,1,512]{2,1,0:T(1,128)} %broadcast_in_dim.77), calls=%async_computation.1 | async-start | bytes 524288 | tf_op jit(solution)/shard_map/all_to_all | solution.py:112
  97.7 1.6 %subtract_multiply_fusion = f32[64,64,128]{2,1,0:T(8,128)} fusion(f32[64,64,128]{2,1,0:T(8,128)S(1)} %copy-done, f32[64,128]{1,0:T(8,128)S(1)} %broadcast_multiply_fusion), kind=kLoop, calls=%fused_computation.4 | loop fusion | flops 1048576 | bytes 4227072 | tf_op jit(solution)/shard_map/div | solution.py:218
  99.3 9.6 %all-to-all-done.1 = f32[128,1,512]{2,1,0:T(1,128)S(1)} async-done(((f32[128,1,512]{2,1,0:T(1,128)}), f32[128,1,512]{2,1,0:T(1,128)S(1)}, u32[]{:S(2)}, u32[]{:S(2)}) %all-to-all-start.1) | async-done | bytes 262176 | tf_op jit(solution)/shard_map/all_to_all | solution.py:112
  108.9 0.6 reduce.7
  109.8 0.5 copy-done.3
  110.4 0.4 sub.44
  110.8 1.8 %fusion.54 = (f32[128,512]{1,0:T(8,128)S(1)}, f32[128,512]{1,0:T(8,128)S(1)}) fusion(f32[128,1,512]{2,1,0:T(1,128)S(1)} %all-to-all-done.1, f32[128,1,512]{2,1,0:T(1,128)S(1)} %sub.44, f32[128,1,512]{2,1,0:T(1,128)S(1)} %div.70), kind=kLoop, calls=%fused_computation.87 | loop fusion | flops 196608 | bytes 1310720 | tf_op jit(solution)/shard_map/div | solution.py:135
  112.7 0.4 fusion.57
  113.2 5.8 %cholesky.17 = f32[64,64]{1,0:T(8,128)S(1)} custom-call(f32[64,64]{1,0:T(8,128)S(1)} %fusion.29), custom_call_target="Cholesky" | custom-call | tf_op jit(solution)/shard_map/jit(cholesky)/cholesky | solution.py:142
  119.1 0.7 compare_reduce_fusion
  119.8 0.7 fusion.24
  120.5 4.9 %custom-call.8 = f32[1,64,64]{1,2,0:T(8,128)S(1)} custom-call(f32[1,64,64]{2,1,0:T(8,128)S(1)} %fusion.24), custom_call_target="InvertDiagBlocksLowerTriangular" | custom-call | tf_op jit(solution)/shard_map/triangular_solve | solution.py:144
  125.4 1.5 %fusion.12 = f32[64,64]{1,0:T(8,128)S(1)} fusion(f32[64,1024]{1,0:T(8,128)} %copy-done.3, f32[64,1024]{1,0:T(8,128)} %param.15, f32[1024]{0:T(1024)S(1)} %sqrt.3, f32[1024]{0:T(1024)S(1)} %copy-done.7, f32[1024]{0:T(1024)S(1)} %copy-done.6, f32[1024]{0:T(1024)S(1)} %broadcast_multiply_fusion.1), kind=kOutput, calls=%fused_computation.19 | convolution fusion | flops 50724864 | bytes 557056 | tf_op jit(solution)/shard_map/dot_general | solution.py:141
  126.9 0.2 fusion.26
  127.2 0.2 convolution_bitcast_fusion
  127.4 5.7 %copy_add_fusion = f32[64,64,128]{2,0,1:T(8,128)S(1)} fusion(f32[64,64,128]{2,1,0:T(8,128)S(1)} %copy-done, f32[64,64,1]{0,1,2:T(8,128)S(1)} %convolution_bitcast_fusion, f32[64,64,128]{2,1,0:T(8,128)} %subtract_multiply_fusion), kind=kOutput, calls=%fused_computation.1 | convolution fusion | flops 403177472 | bytes 6307840 | tf_op jit(solution)/shard_map/mrc,mn->nrc/dot_general | solution.py:221
  133.1 2.5 %copy.35 = f32[64,64,128]{2,1,0:T(8,128)} copy(f32[64,64,128]{2,0,1:T(8,128)S(1)} %copy_add_fusion) | data formatting | bytes 4194304
  (55 shorter events, 1.4 us)
Async XLA Ops:
  0.6 14.1 %copy-start.2 = (bf16[64,64,128]{2,1,0:T(8,128)(2,1)S(1)}, bf16[64,64,128]{2,1,0:T(8,128)(2,1)}, u32[]{:S(2)}) copy-start(bf16[64,64,128]{2,1,0:T(8,128)(2,1)} %head_ref.1) | copy-start | bytes 3145732
  3.6 13.3 %collective-permute-start = (f32[3,129,128]{2,0,1:T(4,128)S(1)}, f32[3,129,128]{2,0,1:T(4,128)S(1)}, u32[]{:S(2)}, u32[]{:S(2)}) collective-permute-start(f32[3,129,128]{2,0,1:T(4,128)S(1)} %maximum_bitcast_fusion), channel_id=1, source_target_pairs={{16,0},{32,16},{48,32},{64,48},{80,64},{96,80},{112,96},{17,1},{33... | collective-permute-start | bytes 594440 | tf_op jit(solution)/shard_map/ppermute | solution.py:21
  6.9 8.8 %copy-start.4 = (f32[64,128]{1,0:T(8,128)S(1)}, f32[64,128]{1,0:T(8,128)}, u32[]{:S(2)}) copy-start(f32[64,128]{1,0:T(8,128)} %source_ref.1) | copy-start | bytes 98308
  6.9 9.0 %copy-start.5 = (s32[4,256]{1,0:T(4,128)S(1)}, s32[4,256]{1,0:T(4,128)}, u32[]{:S(2)}) copy-start(s32[4,256]{1,0:T(4,128)} %param.11) | copy-start | bytes 12292
  6.9 9.1 %copy-start.8 = (s32[4]{0:T(128)S(1)}, s32[4]{0:T(128)}, u32[]{:S(2)}) copy-start(s32[4]{0:T(128)} %param.12) | copy-start | bytes 52
  7.0 9.9 %collective-permute-start.1 = (f32[3,129,128]{2,0,1:T(4,128)S(1)}, f32[3,129,128]{2,0,1:T(4,128)S(1)}, u32[]{:S(2)}, u32[]{:S(2)}) collective-permute-start(f32[3,129,128]{2,0,1:T(4,128)S(1)} %maximum_bitcast_fusion.1), channel_id=1, source_target_pairs={{0,16},{16,32},{32,48},{48,64},{64,80},{80,96},{96,112},{1,17},{17... | collective-permute-start | bytes 594440 | tf_op jit(solution)/shard_map/ppermute | solution.py:21
  17.1 6.9 %copy-start.1 = (f32[129,8,128]{2,1,0:T(8,128)}, f32[129,8,128]{2,1,0:T(8,128)S(1)}, u32[]{:S(2)}) copy-start(f32[129,8,128]{2,1,0:T(8,128)S(1)} %pad_maximum_fusion.source_rows_ref.perm_rows_ref.head_rows_ref) | copy-start | bytes 1585156
  18.4 9.3 %collective-permute-start.2 = (f32[3,129,72]{2,0,1:T(4,128)S(1)}, f32[3,129,72]{2,0,1:T(4,128)S(1)}, u32[]{:S(2)}, u32[]{:S(2)}) collective-permute-start(f32[3,129,72]{2,0,1:T(4,128)S(1)} %get-tuple-element.22), channel_id=1, source_target_pairs={{1,0},{2,1},{3,2},{4,3},{5,4},{6,5},{7,6},{8,7},{9,8},{10,9},{11,1... | collective-permute-start | bytes 334376 | tf_op jit(solution)/shard_map/ppermute | solution.py:21
  19.7 9.8 %collective-permute-start.3 = (f32[3,129,72]{2,0,1:T(4,128)S(1)}, f32[3,129,72]{2,0,1:T(4,128)S(1)}, u32[]{:S(2)}, u32[]{:S(2)}) collective-permute-start(f32[3,129,72]{2,0,1:T(4,128)S(1)} %get-tuple-element.23), channel_id=1, source_target_pairs={{0,1},{1,2},{2,3},{3,4},{4,5},{5,6},{6,7},{7,8},{8,9},{9,10},{10,1... | collective-permute-start | bytes 334376 | tf_op jit(solution)/shard_map/ppermute | solution.py:21
  66.7 14.6 %copy-start.6 = (f32[1024]{0:T(1024)S(1)}, f32[1024]{0:T(1024)}, u32[]{:S(2)}) copy-start(f32[1024]{0:T(1024)} %param.14) | copy-start | bytes 12292
  66.7 14.6 %copy-start = (f32[64,64,128]{2,1,0:T(8,128)S(1)}, f32[64,64,128]{2,1,0:T(8,128)}, u32[]{:S(2)}) copy-start(f32[64,64,128]{2,1,0:T(8,128)} %perm_ref.1) | copy-start | bytes 6291460
  68.0 24.4 %all-to-all-start = ((f32[128,1,512]{2,1,0:T(1,128)}), f32[128,1,512]{2,1,0:T(1,128)S(1)}, u32[]{:S(2)}, u32[]{:S(2)}) async-start(f32[128,1,512]{2,1,0:T(1,128)} %copy.30), calls=%async_computation | async-start | bytes 524288 | tf_op jit(solution)/shard_map/all_to_all | solution.py:110
  93.5 15.5 %all-to-all-start.1 = ((f32[128,1,512]{2,1,0:T(1,128)}), f32[128,1,512]{2,1,0:T(1,128)S(1)}, u32[]{:S(2)}, u32[]{:S(2)}) async-start(f32[128,1,512]{2,1,0:T(1,128)} %broadcast_in_dim.77), calls=%async_computation.1 | async-start | bytes 524288 | tf_op jit(solution)/shard_map/all_to_all | solution.py:112
  109.7 0.7 copy-start.3
  109.7 15.7 %copy-start.7 = (f32[1024]{0:T(1024)S(1)}, f32[1024]{0:T(1024)}, u32[]{:S(2)}) copy-start(f32[1024]{0:T(1024)} %param.13) | copy-start | bytes 12292

commit v10 on v8

--- a/solution.py
+++ b/solution.py
@@ -205,7 +205,7 @@
         "col", col_count, width, ext_cols
     )[None, :]
     pressure_low, hydraulic_head = run_stencil(
-        inside.astype(f32), recharge, halo_rows, halo_cols, logarithmic_conductivity, starting_head, 8
+        inside.astype(f32), recharge, halo_rows, halo_cols, logarithmic_conductivity, starting_head, 16
     )
     group_total, well_count = well_cells.shape
     local_data = jnp.take(hydraulic_head.reshape(member_count, row_count * col_count), well_cells.reshape(-1), axis=1)

time: 135 us -> 135 us (level)
  no operation moved by 1% of the time
where the time goes in v10:
time: 135 us
  starting transfers between devices  29.7 us (22%)
  waiting for transfers between devices  25.3 us (19%)
  Pallas kernels  21.6 us (16%)
  matrix products  19.6 us (15%)
  other arithmetic  18.9 us (14%)
  local copies, waits for them, and re-layouts  18.4 us (14%)
    pallas_call x1, Pallas kernels, run_stencil(): pl.pallas_call(stencil_kernel, grid=(blocks,), in_specs=[full2(mask.shape...  21.6 us
    all_to_all x1, starting transfers between devices, broadcast_from_owners(): own_chunk = lax.all_to_all(chunks, axes, 0, 0, tiled=True).sum(axis=0)  13.3 us
    ppermute x4, starting transfers between devices, send(): return lax.ppermute(piece, axis, pairs)  12.1 us
    all_to_all x1, waiting for transfers between devices, broadcast_from_owners(): own_chunk = lax.all_to_all(chunks, axes, 0, 0, tiled=True).sum(axis=0)  10.4 us
    all_to_all x1, waiting for transfers between devices, broadcast_from_owners(): return lax.all_to_all(spread, axes, 0, 0, tiled=True).reshape(value.shape)  9.65 us
    another operation x3, other arithmetic, blending_weights(): factor = jnp.linalg.cholesky(system)  6.6 us
    dot_general x1, matrix products, per_device(): halo_cols = jnp.einsum('kmr,kl->mrl', received, selector, precision=highest)  5.72 us
    dot_general x1, matrix products, per_device(): jnp.einsum('mrc,mn->nrc', anomalies, mixing, precision=lax.Precision.HIGH...  5.69 us
  transfers between devices with their start and end apart: 6, of which 4 were waited for; matrix products, arithmetic and copies ran while one was open for 7% of the time, Pallas kernels for 0%

profile of v10, /device:TPU:1, one launch (start us, length us, event | category | flops | bytes accessed | tf_op | source)
XLA Modules:
  0.0 134.5 jit_solution(11498735883258717186)
XLA Ops:
  0.6 1.2 fusion.55
  1.8 1.0 slice_convert_fusion.1
  2.8 0.7 slice_bitcast_fusion.1
  3.6 3.3 %collective-permute-start = (f32[3,129,128]{2,0,1:T(4,128)S(1)}, f32[3,129,128]{2,0,1:T(4,128)S(1)}, u32[]{:S(2)}, u32[]{:S(2)}) collective-permute-start(f32[3,129,128]{2,0,1:T(4,128)S(1)} %maximum_bitcast_fusion), channel_id=1, source_target_pairs={{16,0},{32,16},{48,32},{64,48},{80,64},{96,80},{112,96},{17,1},{33... | collective-permute-start | bytes 594440 | tf_op jit(solution)/shard_map/ppermute | solution.py:21
  7.0 3.6 %collective-permute-start.1 = (f32[3,129,128]{2,0,1:T(4,128)S(1)}, f32[3,129,128]{2,0,1:T(4,128)S(1)}, u32[]{:S(2)}, u32[]{:S(2)}) collective-permute-start(f32[3,129,128]{2,0,1:T(4,128)S(1)} %maximum_bitcast_fusion.1), channel_id=1, source_target_pairs={{0,16},{16,32},{32,48},{48,64},{64,80},{80,96},{96,112},{1,17},{17... | collective-permute-start | bytes 594440 | tf_op jit(solution)/shard_map/ppermute | solution.py:21
  10.6 4.1 %fusion.35 = f32[8,64,64]{2,0,1:T(8,128)S(1)} fusion(f32[64,64,128]{2,1,0:T(8,128)} %perm_ref.1, s32[8]{0:T(128)S(1)} %compare_select_fusion.4, pred[8]{0:T(512)(128)(4,1)S(1)} %compare_or_fusion), kind=kOutput, calls=%fused_computation.60 | convolution fusion | flops 50333696 | bytes 2228264 | tf_op jit(solution)/shard_map/dot_general | solution.py:189
  14.7 0.9 fusion.38
  15.7 0.2 convolution_bitcast_fusion.1
  16.2 0.7 and_convert_fusion.mask_ref
  17.0 0.1 pad_maximum_fusion.source_rows_ref.perm_rows_ref.head_rows_ref
  17.1 0.6 fusion.4
  17.7 0.4 copy.27
  18.1 0.2 pad_maximum_fusion.1
  18.4 1.3 collective-permute-start.2
  19.7 4.0 %collective-permute-start.3 = (f32[3,129,72]{2,0,1:T(4,128)S(1)}, f32[3,129,72]{2,0,1:T(4,128)S(1)}, u32[]{:S(2)}, u32[]{:S(2)}) collective-permute-start(f32[3,129,72]{2,0,1:T(4,128)S(1)} %get-tuple-element.23), channel_id=1, source_target_pairs={{0,1},{1,2},{2,3},{3,4},{4,5},{5,6},{6,7},{7,8},{8,9},{9,10},{10,1... | collective-permute-start | bytes 334376 | tf_op jit(solution)/shard_map/ppermute | solution.py:21
  23.9 0.2 broadcast_in_dim.72
  24.1 0.2 broadcast_in_dim.74
  24.3 3.4 %collective-permute-done.2 = f32[3,129,72]{2,0,1:T(4,128)S(1)} collective-permute-done((f32[3,129,72]{2,0,1:T(4,128)S(1)}, f32[3,129,72]{2,0,1:T(4,128)S(1)}, u32[]{:S(2)}, u32[]{:S(2)}) %collective-permute-start.2) | collective-permute-done | bytes 111488 | tf_op jit(solution)/shard_map/ppermute | solution.py:21
  27.7 1.8 %collective-permute-done.3 = f32[3,129,72]{2,0,1:T(4,128)S(1)} collective-permute-done((f32[3,129,72]{2,0,1:T(4,128)S(1)}, f32[3,129,72]{2,0,1:T(4,128)S(1)}, u32[]{:S(2)}, u32[]{:S(2)}) %collective-permute-start.3) | collective-permute-done | bytes 111488 | tf_op jit(solution)/shard_map/ppermute | solution.py:21
  29.5 5.7 %fusion.6.source_cols_ref.perm_cols_ref.head_cols_ref = f32[129,72,128]{2,1,0:T(8,128)} fusion(f32[3,129,72]{2,0,1:T(4,128)S(1)} %collective-permute-done.3, f32[3,129,72]{2,0,1:T(4,128)S(1)} %collective-permute-done.2, f32[8]{0:T(128)S(1)} %pad.8.clone, s32[8]{0:T(128)S(1)} %compare_select_fusion.4, pred[8]{0:T(512)(128)(4,1)S(1)} %compare_or_fusion), kind=kOutput, calls=%fused_computation.11 | convolution fusion | flops 114281600 | bytes 4978440 | tf_op jit(solution)/shard_map/kmr,kl->mrl/dot_general | solution.py:203
  35.2 21.6 %shard_map.103 = (bf16[64,64,128]{2,1,0:T(8,128)(2,1)}, f32[64,64,128]{2,1,0:T(8,128)}) custom-call(f32[72,256]{1,0:T(8,128)} %and_convert_fusion.mask_ref, f32[64,128]{1,0:T(8,128)} %source_ref.1, f32[129,8,128]{2,1,0:T(8,128)} %copy-done.1, f32[129,72,128]{2,1,0:T(8,128)} %fusion.6.source_cols_ref.perm_cols_ref.head_cols_ref, f32[64,64,128]{2,1,0:T(8,128)} %perm_ref.1, ...), custom_call_target="tpu_custom_call" | custom-call | flops 94371840 | bytes 7340032 | tf_op jit(solution)/shard_map/pallas_call | solution.py:79
  56.7 3.8 %copy.37 = f32[64,64,128]{0,2,1:T(8,128)} copy(f32[64,64,128]{2,1,0:T(8,128)} %get-tuple-element.6) | data formatting | bytes 4194304 | tf_op jit(solution)/shard_map/reshape | solution.py:211
  60.6 5.0 %gather_fusion = f32[1024,64]{1,0:T(8,128)S(1)} fusion(f32[64,8192]{0,1:T(8,128)} %bitcast.53, s32[1024]{0:T(1024)S(1)} %broadcast_clamp_fusion), kind=kCustom, calls=%fused_computation | custom fusion | bytes 528384 | tf_op jit(solution)/shard_map/jit(_take)/gather | solution.py:211
  65.6 0.2 copy.29
  65.9 1.0 copy.30
  66.8 13.3 %all-to-all-start = ((f32[128,1,512]{2,1,0:T(1,128)}), f32[128,1,512]{2,1,0:T(1,128)S(1)}, u32[]{:S(2)}, u32[]{:S(2)}) async-start(f32[128,1,512]{2,1,0:T(1,128)} %copy.30), calls=%async_computation | async-start | bytes 524288 | tf_op jit(solution)/shard_map/all_to_all | solution.py:110
  80.2 0.1 reduce_sum.29
  80.4 0.4 div.70
  80.8 10.4 %all-to-all-done = f32[128,1,512]{2,1,0:T(1,128)S(1)} async-done(((f32[128,1,512]{2,1,0:T(1,128)}), f32[128,1,512]{2,1,0:T(1,128)S(1)}, u32[]{:S(2)}, u32[]{:S(2)}) %all-to-all-start) | async-done | bytes 262176 | tf_op jit(solution)/shard_map/all_to_all | solution.py:110
  91.3 0.2 reduce_sum.27
  91.5 0.8 broadcast_in_dim.77
  92.3 4.3 %all-to-all-start.1 = ((f32[128,1,512]{2,1,0:T(1,128)}), f32[128,1,512]{2,1,0:T(1,128)S(1)}, u32[]{:S(2)}, u32[]{:S(2)}) async-start(f32[128,1,512]{2,1,0:T(1,128)} %broadcast_in_dim.77), calls=%async_computation.1 | async-start | bytes 524288 | tf_op jit(solution)/shard_map/all_to_all | solution.py:112
  96.6 1.6 %subtract_multiply_fusion = f32[64,64,128]{2,1,0:T(8,128)} fusion(f32[64,64,128]{2,1,0:T(8,128)S(1)} %copy-done, f32[64,128]{1,0:T(8,128)S(1)} %broadcast_multiply_fusion), kind=kLoop, calls=%fused_computation.4 | loop fusion | flops 1048576 | bytes 4227072 | tf_op jit(solution)/shard_map/div | solution.py:218
  98.1 9.6 %all-to-all-done.1 = f32[128,1,512]{2,1,0:T(1,128)S(1)} async-done(((f32[128,1,512]{2,1,0:T(1,128)}), f32[128,1,512]{2,1,0:T(1,128)S(1)}, u32[]{:S(2)}, u32[]{:S(2)}) %all-to-all-start.1) | async-done | bytes 262176 | tf_op jit(solution)/shard_map/all_to_all | solution.py:112
  107.8 0.6 reduce.7
  108.7 0.5 copy-done.3
  109.2 0.4 sub.44
  109.6 1.8 %fusion.54 = (f32[128,512]{1,0:T(8,128)S(1)}, f32[128,512]{1,0:T(8,128)S(1)}) fusion(f32[128,1,512]{2,1,0:T(1,128)S(1)} %all-to-all-done.1, f32[128,1,512]{2,1,0:T(1,128)S(1)} %sub.44, f32[128,1,512]{2,1,0:T(1,128)S(1)} %div.70), kind=kLoop, calls=%fused_computation.87 | loop fusion | flops 196608 | bytes 1310720 | tf_op jit(solution)/shard_map/div | solution.py:135
  111.6 0.4 fusion.57
  112.0 5.8 %cholesky.17 = f32[64,64]{1,0:T(8,128)S(1)} custom-call(f32[64,64]{1,0:T(8,128)S(1)} %fusion.29), custom_call_target="Cholesky" | custom-call | tf_op jit(solution)/shard_map/jit(cholesky)/cholesky | solution.py:142
  117.9 0.7 compare_reduce_fusion
  118.6 0.7 fusion.24
  119.4 4.9 %custom-call.8 = f32[1,64,64]{1,2,0:T(8,128)S(1)} custom-call(f32[1,64,64]{2,1,0:T(8,128)S(1)} %fusion.24), custom_call_target="InvertDiagBlocksLowerTriangular" | custom-call | tf_op jit(solution)/shard_map/triangular_solve | solution.py:144
  124.3 1.5 %fusion.12 = f32[64,64]{1,0:T(8,128)S(1)} fusion(f32[64,1024]{1,0:T(8,128)} %copy-done.3, f32[64,1024]{1,0:T(8,128)} %param.15, f32[1024]{0:T(1024)S(1)} %sqrt.3, f32[1024]{0:T(1024)S(1)} %copy-done.7, f32[1024]{0:T(1024)S(1)} %copy-done.6, f32[1024]{0:T(1024)S(1)} %broadcast_multiply_fusion.1), kind=kOutput, calls=%fused_computation.19 | convolution fusion | flops 50724864 | bytes 557056 | tf_op jit(solution)/shard_map/dot_general | solution.py:141
  125.8 0.2 fusion.26
  126.0 0.2 convolution_bitcast_fusion
  126.3 5.7 %copy_add_fusion = f32[64,64,128]{2,0,1:T(8,128)S(1)} fusion(f32[64,64,128]{2,1,0:T(8,128)S(1)} %copy-done, f32[64,64,1]{0,1,2:T(8,128)S(1)} %convolution_bitcast_fusion, f32[64,64,128]{2,1,0:T(8,128)} %subtract_multiply_fusion), kind=kOutput, calls=%fused_computation.1 | convolution fusion | flops 403177472 | bytes 6307840 | tf_op jit(solution)/shard_map/mrc,mn->nrc/dot_general | solution.py:221
  132.0 2.5 %copy.35 = f32[64,64,128]{2,1,0:T(8,128)} copy(f32[64,64,128]{2,0,1:T(8,128)S(1)} %copy_add_fusion) | data formatting | bytes 4194304
  (55 shorter events, 1.4 us)
Async XLA Ops:
  0.6 14.1 %copy-start.2 = (bf16[64,64,128]{2,1,0:T(8,128)(2,1)S(1)}, bf16[64,64,128]{2,1,0:T(8,128)(2,1)}, u32[]{:S(2)}) copy-start(bf16[64,64,128]{2,1,0:T(8,128)(2,1)} %head_ref.1) | copy-start | bytes 3145732
  3.6 13.3 %collective-permute-start = (f32[3,129,128]{2,0,1:T(4,128)S(1)}, f32[3,129,128]{2,0,1:T(4,128)S(1)}, u32[]{:S(2)}, u32[]{:S(2)}) collective-permute-start(f32[3,129,128]{2,0,1:T(4,128)S(1)} %maximum_bitcast_fusion), channel_id=1, source_target_pairs={{16,0},{32,16},{48,32},{64,48},{80,64},{96,80},{112,96},{17,1},{33... | collective-permute-start | bytes 594440 | tf_op jit(solution)/shard_map/ppermute | solution.py:21
  6.9 8.8 %copy-start.4 = (f32[64,128]{1,0:T(8,128)S(1)}, f32[64,128]{1,0:T(8,128)}, u32[]{:S(2)}) copy-start(f32[64,128]{1,0:T(8,128)} %source_ref.1) | copy-start | bytes 98308
  6.9 9.0 %copy-start.5 = (s32[4,256]{1,0:T(4,128)S(1)}, s32[4,256]{1,0:T(4,128)}, u32[]{:S(2)}) copy-start(s32[4,256]{1,0:T(4,128)} %param.11) | copy-start | bytes 12292
  6.9 9.1 %copy-start.8 = (s32[4]{0:T(128)S(1)}, s32[4]{0:T(128)}, u32[]{:S(2)}) copy-start(s32[4]{0:T(128)} %param.12) | copy-start | bytes 52
  7.0 9.9 %collective-permute-start.1 = (f32[3,129,128]{2,0,1:T(4,128)S(1)}, f32[3,129,128]{2,0,1:T(4,128)S(1)}, u32[]{:S(2)}, u32[]{:S(2)}) collective-permute-start(f32[3,129,128]{2,0,1:T(4,128)S(1)} %maximum_bitcast_fusion.1), channel_id=1, source_target_pairs={{0,16},{16,32},{32,48},{48,64},{64,80},{80,96},{96,112},{1,17},{17... | collective-permute-start | bytes 594440 | tf_op jit(solution)/shard_map/ppermute | solution.py:21
  17.1 6.9 %copy-start.1 = (f32[129,8,128]{2,1,0:T(8,128)}, f32[129,8,128]{2,1,0:T(8,128)S(1)}, u32[]{:S(2)}) copy-start(f32[129,8,128]{2,1,0:T(8,128)S(1)} %pad_maximum_fusion.source_rows_ref.perm_rows_ref.head_rows_ref) | copy-start | bytes 1585156
  18.4 9.3 %collective-permute-start.2 = (f32[3,129,72]{2,0,1:T(4,128)S(1)}, f32[3,129,72]{2,0,1:T(4,128)S(1)}, u32[]{:S(2)}, u32[]{:S(2)}) collective-permute-start(f32[3,129,72]{2,0,1:T(4,128)S(1)} %get-tuple-element.22), channel_id=1, source_target_pairs={{1,0},{2,1},{3,2},{4,3},{5,4},{6,5},{7,6},{8,7},{9,8},{10,9},{11,1... | collective-permute-start | bytes 334376 | tf_op jit(solution)/shard_map/ppermute | solution.py:21
  19.7 9.8 %collective-permute-start.3 = (f32[3,129,72]{2,0,1:T(4,128)S(1)}, f32[3,129,72]{2,0,1:T(4,128)S(1)}, u32[]{:S(2)}, u32[]{:S(2)}) collective-permute-start(f32[3,129,72]{2,0,1:T(4,128)S(1)} %get-tuple-element.23), channel_id=1, source_target_pairs={{0,1},{1,2},{2,3},{3,4},{4,5},{5,6},{6,7},{7,8},{8,9},{9,10},{10,1... | collective-permute-start | bytes 334376 | tf_op jit(solution)/shard_map/ppermute | solution.py:21
  65.6 14.6 %copy-start.6 = (f32[1024]{0:T(1024)S(1)}, f32[1024]{0:T(1024)}, u32[]{:S(2)}) copy-start(f32[1024]{0:T(1024)} %param.14) | copy-start | bytes 12292
  65.6 14.6 %copy-start = (f32[64,64,128]{2,1,0:T(8,128)S(1)}, f32[64,64,128]{2,1,0:T(8,128)}, u32[]{:S(2)}) copy-start(f32[64,64,128]{2,1,0:T(8,128)} %perm_ref.1) | copy-start | bytes 6291460
  66.8 24.4 %all-to-all-start = ((f32[128,1,512]{2,1,0:T(1,128)}), f32[128,1,512]{2,1,0:T(1,128)S(1)}, u32[]{:S(2)}, u32[]{:S(2)}) async-start(f32[128,1,512]{2,1,0:T(1,128)} %copy.30), calls=%async_computation | async-start | bytes 524288 | tf_op jit(solution)/shard_map/all_to_all | solution.py:110
  92.3 15.5 %all-to-all-start.1 = ((f32[128,1,512]{2,1,0:T(1,128)}), f32[128,1,512]{2,1,0:T(1,128)S(1)}, u32[]{:S(2)}, u32[]{:S(2)}) async-start(f32[128,1,512]{2,1,0:T(1,128)} %broadcast_in_dim.77), calls=%async_computation.1 | async-start | bytes 524288 | tf_op jit(solution)/shard_map/all_to_all | solution.py:112
  108.5 0.7 copy-start.3
  108.5 15.7 %copy-start.7 = (f32[1024]{0:T(1024)S(1)}, f32[1024]{0:T(1024)}, u32[]{:S(2)}) copy-start(f32[1024]{0:T(1024)} %param.13) | copy-start | bytes 12292

commit v11 on v8

--- a/solution.py
+++ b/solution.py
@@ -129,6 +129,35 @@
     return centre_press + time_step * (flux_total + source)
 
 
+def update_kernel(mix_t_ref, perm_ref, out_ref):
+    members = mix_t_ref.shape[0]
+    rows = perm_ref.shape[0] // members
+    mix_t = mix_t_ref[...]
+    spread = math.sqrt(members - 1)
+
+    def body(r, carry):
+        values = perm_ref[pl.ds(r, members, stride=rows)]
+        anomalies = (values - jnp.mean(values, axis=0, keepdims=True)) / spread
+        shift = jnp.dot(mix_t, anomalies, precision=lax.Precision.HIGHEST, preferred_element_type=jnp.float32)
+        out_ref[pl.ds(r, members, stride=rows)] = values + shift
+        return carry
+
+    lax.fori_loop(0, rows, body, 0, unroll=8)
+
+
+def run_update(perm, mixing):
+    members, rows, cols = perm.shape
+    flat = perm.reshape(members * rows, cols)
+    out = pl.pallas_call(
+        update_kernel,
+        out_shape=jax.ShapeDtypeStruct(flat.shape, jnp.float32),
+        cost_estimate=pl.CostEstimate(
+            flops=2 * members * members * rows * cols, transcendentals=0, bytes_accessed=8 * members * rows * cols
+        ),
+    )(mixing.T, flat)
+    return out.reshape(perm.shape)
+
+
 def blending_weights(predicted, observed, obs_var, perturb):
     member_count = predicted.shape[0]
     ensemble_spread = math.sqrt(member_count - 1)
@@ -214,13 +243,7 @@
     local_data = jnp.where(mine[None, :], local_data, 0.0)
     predicted = broadcast_from_owners(local_data, ("row", "col"))
     mixing = blending_weights(predicted, observed, obs_var, perturb)
-    ensemble_spread = math.sqrt(member_count - 1)
-    anomalies = (
-        logarithmic_conductivity - jnp.mean(logarithmic_conductivity, axis=0, keepdims=True)
-    ) / ensemble_spread
-    updated_perm = logarithmic_conductivity + jnp.einsum(
-        "mrc,mn->nrc", anomalies, mixing, precision=lax.Precision.HIGHEST
-    )
+    updated_perm = run_update(logarithmic_conductivity, mixing)
     return (pressure_low, predicted, updated_perm)
 
 

time: 135 us -> 132 us (0.978)
  blocking collectives: 0 us -> 24.2 us
  starting transfers between devices: 29.7 us -> 16.4 us
  waiting for transfers between devices: 25.3 us -> 15.9 us
  Pallas kernels: 21.6 us -> 29.3 us
  matrix products: 19.6 us -> 13.4 us
  local copies, waits for them, and re-layouts: 18.4 us -> 14.5 us
  other arithmetic: 18.9 us -> 17 us
    all_to_all x0 -> x1, blocking collectives: none -> 24.2 us  [broadcast_from_owners(): own_chunk = lax.all_to_all(chunks, axes, 0, 0, tiled=True).sum(axis=0)]
    all_to_all x1 -> x0, starting transfers between devices: 13.3 us -> none  [broadcast_from_owners(): own_chunk = lax.all_to_all(chunks, axes, 0, 0, tiled=True).sum(axis=0)]
    all_to_all x1 -> x0, waiting for transfers between devices: 10.4 us -> none  [broadcast_from_owners(): own_chunk = lax.all_to_all(chunks, axes, 0, 0, tiled=True).sum(axis=0)]
    pallas_call x0 -> x1, Pallas kernels: none -> 7.73 us  [run_update(): pl.pallas_call(update_kernel, out_shape=jax.ShapeDtypeStruct(flat.shape,...]
    dot_general x1 -> x0, matrix products: 5.68 us -> none  [per_device(): jnp.einsum('mrc,mn->nrc', anomalies, mixing, precision=lax.Precision.HIGH...]
    unnamed x22 -> x21, local copies, waits for them, and re-layouts: 3.23 us -> 0.15 us
    div x2 -> x0, other arithmetic: 1.57 us -> none  [the longest x1 1.56 us: per_device(): (logarithmic_conductivity - jnp.mean(logarithmic_conductivity, axis=0, ke...]
  transfers between devices with their start and end apart: 6 -> 5, of which waited for: 4 -> 3; matrix products, arithmetic and copies ran while one was open for 7% -> 6% of each run, Pallas kernels for 0% -> 0%
where the time goes in v11:
time: 132 us
  Pallas kernels  29.3 us (22%)
  blocking collectives  24.2 us (18%)
  other arithmetic  17 us (13%)
  starting transfers between devices  16.4 us (12%)
  waiting for transfers between devices  15.9 us (12%)
  local copies, waits for them, and re-layouts  14.5 us (11%)
  matrix products  13.4 us (10%)
    all_to_all x1, blocking collectives, broadcast_from_owners(): own_chunk = lax.all_to_all(chunks, axes, 0, 0, tiled=True).sum(axis=0)  24.2 us
    pallas_call x1, Pallas kernels, run_stencil(): pl.pallas_call(stencil_kernel, grid=(blocks,), in_specs=[full2(mask.shape...  21.6 us
    ppermute x4, starting transfers between devices, send(): return lax.ppermute(piece, axis, pairs)  12.1 us
    all_to_all x1, waiting for transfers between devices, broadcast_from_owners(): return lax.all_to_all(spread, axes, 0, 0, tiled=True).reshape(value.shape)  10.7 us
    pallas_call x1, Pallas kernels, run_update(): pl.pallas_call(update_kernel, out_shape=jax.ShapeDtypeStruct(flat.shape,...  7.73 us
    another operation x3, other arithmetic, blending_weights(): factor = jnp.linalg.cholesky(system)  6.52 us
    dot_general x1, matrix products, per_device(): halo_cols = jnp.einsum('kmr,kl->mrl', received, selector, precision=highest)  5.72 us
    another operation x2, other arithmetic, blending_weights(): lax.linalg.triangular_solve(factor, half_solved, left_side=True, lower=Tr...  5.55 us
  transfers between devices with their start and end apart: 5, of which 3 were waited for; matrix products, arithmetic and copies ran while one was open for 6% of the time, Pallas kernels for 0%

profile of v11, /device:TPU:1, one launch (start us, length us, event | category | flops | bytes accessed | tf_op | source)
XLA Modules:
  0.0 131.8 jit_solution(10036255237980317744)
XLA Ops:
  0.6 1.1 slice_convert_fusion.1
  1.7 1.1 fusion.52
  2.8 0.7 slice_bitcast_fusion.1
  3.6 3.3 %collective-permute-start = (f32[3,129,128]{2,0,1:T(4,128)S(1)}, f32[3,129,128]{2,0,1:T(4,128)S(1)}, u32[]{:S(2)}, u32[]{:S(2)}) collective-permute-start(f32[3,129,128]{2,0,1:T(4,128)S(1)} %maximum_bitcast_fusion), channel_id=1, source_target_pairs={{16,0},{32,16},{48,32},{64,48},{80,64},{96,80},{112,96},{17,1},{33... | collective-permute-start | bytes 594440 | tf_op jit(solution)/shard_map/ppermute | solution.py:21
  7.0 3.6 %collective-permute-start.1 = (f32[3,129,128]{2,0,1:T(4,128)S(1)}, f32[3,129,128]{2,0,1:T(4,128)S(1)}, u32[]{:S(2)}, u32[]{:S(2)}) collective-permute-start(f32[3,129,128]{2,0,1:T(4,128)S(1)} %maximum_bitcast_fusion.1), channel_id=1, source_target_pairs={{0,16},{16,32},{32,48},{48,64},{64,80},{80,96},{96,112},{1,17},{17... | collective-permute-start | bytes 594440 | tf_op jit(solution)/shard_map/ppermute | solution.py:21
  10.6 4.1 %fusion.32 = f32[8,64,64]{2,0,1:T(8,128)S(1)} fusion(f32[64,64,128]{2,1,0:T(8,128)} %perm_ref.1, s32[8]{0:T(128)S(1)} %compare_select_fusion.4, pred[8]{0:T(512)(128)(4,1)S(1)} %compare_or_fusion), kind=kOutput, calls=%fused_computation.55 | convolution fusion | flops 50333696 | bytes 2228264 | tf_op jit(solution)/shard_map/dot_general | solution.py:218
  14.7 0.9 fusion.35
  15.7 0.2 convolution_bitcast_fusion
  16.0 0.1 broadcast_in_dim.67
  16.2 0.7 and_convert_fusion.mask_ref
  16.9 0.1 pad_maximum_fusion.source_rows_ref.perm_rows_ref.head_rows_ref
  17.1 0.6 fusion
  17.7 0.4 copy.21
  18.1 0.2 pad_maximum_fusion.1
  18.3 0.1 fusion.53
  18.4 1.3 collective-permute-start.2
  19.7 4.0 %collective-permute-start.3 = (f32[3,129,72]{2,0,1:T(4,128)S(1)}, f32[3,129,72]{2,0,1:T(4,128)S(1)}, u32[]{:S(2)}, u32[]{:S(2)}) collective-permute-start(f32[3,129,72]{2,0,1:T(4,128)S(1)} %get-tuple-element.14), channel_id=1, source_target_pairs={{0,1},{1,2},{2,3},{3,4},{4,5},{5,6},{6,7},{7,8},{8,9},{9,10},{10,1... | collective-permute-start | bytes 334376 | tf_op jit(solution)/shard_map/ppermute | solution.py:21
  23.9 0.2 broadcast_in_dim.71
  24.1 0.2 broadcast_in_dim.73
  24.3 3.4 %collective-permute-done.2 = f32[3,129,72]{2,0,1:T(4,128)S(1)} collective-permute-done((f32[3,129,72]{2,0,1:T(4,128)S(1)}, f32[3,129,72]{2,0,1:T(4,128)S(1)}, u32[]{:S(2)}, u32[]{:S(2)}) %collective-permute-start.2) | collective-permute-done | bytes 111488 | tf_op jit(solution)/shard_map/ppermute | solution.py:21
  27.7 1.8 %collective-permute-done.3 = f32[3,129,72]{2,0,1:T(4,128)S(1)} collective-permute-done((f32[3,129,72]{2,0,1:T(4,128)S(1)}, f32[3,129,72]{2,0,1:T(4,128)S(1)}, u32[]{:S(2)}, u32[]{:S(2)}) %collective-permute-start.3) | collective-permute-done | bytes 111488 | tf_op jit(solution)/shard_map/ppermute | solution.py:21
  29.4 5.7 %fusion.2.source_cols_ref.perm_cols_ref.head_cols_ref = f32[129,72,128]{2,1,0:T(8,128)} fusion(f32[3,129,72]{2,0,1:T(4,128)S(1)} %collective-permute-done.3, f32[3,129,72]{2,0,1:T(4,128)S(1)} %collective-permute-done.2, f32[8]{0:T(128)S(1)} %pad.8.clone, s32[8]{0:T(128)S(1)} %compare_select_fusion.4, pred[8]{0:T(512)(128)(4,1)S(1)} %compare_or_fusion), kind=kOutput, calls=%fused_computation.6 | convolution fusion | flops 114281600 | bytes 4978440 | tf_op jit(solution)/shard_map/kmr,kl->mrl/dot_general | solution.py:232
  35.2 21.6 %shard_map.103 = (bf16[64,64,128]{2,1,0:T(8,128)(2,1)}, f32[64,64,128]{2,1,0:T(8,128)}) custom-call(f32[72,256]{1,0:T(8,128)} %and_convert_fusion.mask_ref, f32[64,128]{1,0:T(8,128)} %source_ref.1, f32[129,8,128]{2,1,0:T(8,128)} %copy-done, f32[129,72,128]{2,1,0:T(8,128)} %fusion.2.source_cols_ref.perm_cols_ref.head_cols_ref, f32[64,64,128]{2,1,0:T(8,128)} %perm_ref.1, ...), custom_call_target="tpu_custom_call" | custom-call | flops 94371840 | bytes 7340032 | tf_op jit(solution)/shard_map/pallas_call | solution.py:79
  56.8 3.8 %copy.26 = f32[64,64,128]{0,2,1:T(8,128)} copy(f32[64,64,128]{2,1,0:T(8,128)} %get-tuple-element.6) | data formatting | bytes 4194304 | tf_op jit(solution)/shard_map/reshape | solution.py:240
  60.6 5.0 %gather_fusion = f32[1024,64]{1,0:T(8,128)S(1)} fusion(f32[64,8192]{0,1:T(8,128)} %bitcast.53, s32[1024]{0:T(1024)S(1)} %broadcast_clamp_fusion), kind=kCustom, calls=%fused_computation | custom fusion | bytes 528384 | tf_op jit(solution)/shard_map/jit(_take)/gather | solution.py:240
  65.6 0.2 copy.23
  65.9 0.3 copy.24
  66.2 24.2 %all_to_all.12 = f32[128,1,512]{2,1,0:T(1,128)S(1)} all-to-all(f32[128,1,512]{2,1,0:T(1,128)S(1)} %copy.24), channel_id=1, replica_groups=mesh['row'=8,'col'=16] {'row','col'}, dimensions={0} | all-to-all | bytes 524288 | tf_op jit(solution)/shard_map/all_to_all | solution.py:110
  90.4 0.2 reduce_sum.18
  90.6 0.8 broadcast_in_dim.76
  91.4 4.3 %all-to-all-start.1 = ((f32[128,1,512]{2,1,0:T(1,128)}), f32[128,1,512]{2,1,0:T(1,128)S(1)}, u32[]{:S(2)}, u32[]{:S(2)}) async-start(f32[128,1,512]{2,1,0:T(1,128)} %broadcast_in_dim.76), calls=%async_computation.1 | async-start | bytes 524288 | tf_op jit(solution)/shard_map/all_to_all | solution.py:112
  95.8 0.4 div.58
  96.2 10.7 %all-to-all-done.1 = f32[128,1,512]{2,1,0:T(1,128)S(1)} async-done(((f32[128,1,512]{2,1,0:T(1,128)}), f32[128,1,512]{2,1,0:T(1,128)S(1)}, u32[]{:S(2)}, u32[]{:S(2)}) %all-to-all-start.1) | async-done | bytes 262176 | tf_op jit(solution)/shard_map/all_to_all | solution.py:112
  106.9 0.6 reduce.7
  107.5 0.1 reshape.242
  107.8 0.4 sub.36
  108.2 1.6 %fusion.51 = (f32[128,512]{1,0:T(8,128)S(1)}, f32[128,512]{1,0:T(8,128)S(1)}) fusion(f32[128,1,512]{2,1,0:T(1,128)S(1)} %all-to-all-done.1, f32[128,1,512]{2,1,0:T(1,128)S(1)} %sub.36, f32[128,1,512]{2,1,0:T(1,128)S(1)} %div.58), kind=kLoop, calls=%fused_computation.82 | loop fusion | flops 196608 | bytes 1310720 | tf_op jit(solution)/shard_map/div | solution.py:164
  109.8 0.1 div.60
  109.9 0.1 div.61
  110.0 0.4 fusion.54
  110.5 5.8 %cholesky.17 = f32[64,64]{1,0:T(8,128)S(1)} custom-call(f32[64,64]{1,0:T(8,128)S(1)} %fusion.26), custom_call_target="Cholesky" | custom-call | tf_op jit(solution)/shard_map/jit(cholesky)/cholesky | solution.py:171
  116.4 0.6 compare_reduce_fusion
  117.0 0.7 fusion.20
  117.7 4.9 %custom-call.8 = f32[1,64,64]{1,2,0:T(8,128)S(1)} custom-call(f32[1,64,64]{2,1,0:T(8,128)S(1)} %fusion.20), custom_call_target="InvertDiagBlocksLowerTriangular" | custom-call | tf_op jit(solution)/shard_map/triangular_solve | solution.py:173
  122.6 0.4 fusion.8
  123.0 0.2 fusion.23
  123.3 0.9 fusion.21.mix_t_ref
  124.1 7.7 %shard_map.104 = f32[4096,128]{1,0:T(8,128)} custom-call(f32[64,64]{1,0:T(8,128)} %fusion.21.mix_t_ref, f32[4096,128]{1,0:T(8,128)} %bitcast.52), custom_call_target="tpu_custom_call" | custom-call | flops 67108864 | bytes 4194304 | tf_op jit(solution)/shard_map/pallas_call | solution.py:151
  (50 shorter events, 1.0 us)
Async XLA Ops:
  0.6 14.1 %copy-start.1 = (bf16[64,64,128]{2,1,0:T(8,128)(2,1)S(1)}, bf16[64,64,128]{2,1,0:T(8,128)(2,1)}, u32[]{:S(2)}) copy-start(bf16[64,64,128]{2,1,0:T(8,128)(2,1)} %head_ref.1) | copy-start | bytes 3145732
  3.6 13.3 %collective-permute-start = (f32[3,129,128]{2,0,1:T(4,128)S(1)}, f32[3,129,128]{2,0,1:T(4,128)S(1)}, u32[]{:S(2)}, u32[]{:S(2)}) collective-permute-start(f32[3,129,128]{2,0,1:T(4,128)S(1)} %maximum_bitcast_fusion), channel_id=1, source_target_pairs={{16,0},{32,16},{48,32},{64,48},{80,64},{96,80},{112,96},{17,1},{33... | collective-permute-start | bytes 594440 | tf_op jit(solution)/shard_map/ppermute | solution.py:21
  6.9 8.8 %copy-start.3 = (f32[64,128]{1,0:T(8,128)S(1)}, f32[64,128]{1,0:T(8,128)}, u32[]{:S(2)}) copy-start(f32[64,128]{1,0:T(8,128)} %source_ref.1) | copy-start | bytes 98308
  6.9 9.0 %copy-start.4 = (s32[4,256]{1,0:T(4,128)S(1)}, s32[4,256]{1,0:T(4,128)}, u32[]{:S(2)}) copy-start(s32[4,256]{1,0:T(4,128)} %param.11) | copy-start | bytes 12292
  6.9 9.1 %copy-start.8 = (s32[4]{0:T(128)S(1)}, s32[4]{0:T(128)}, u32[]{:S(2)}) copy-start(s32[4]{0:T(128)} %param.12) | copy-start | bytes 52
  7.0 9.9 %collective-permute-start.1 = (f32[3,129,128]{2,0,1:T(4,128)S(1)}, f32[3,129,128]{2,0,1:T(4,128)S(1)}, u32[]{:S(2)}, u32[]{:S(2)}) collective-permute-start(f32[3,129,128]{2,0,1:T(4,128)S(1)} %maximum_bitcast_fusion.1), channel_id=1, source_target_pairs={{0,16},{16,32},{32,48},{48,64},{64,80},{80,96},{96,112},{1,17},{17... | collective-permute-start | bytes 594440 | tf_op jit(solution)/shard_map/ppermute | solution.py:21
  17.1 6.9 %copy-start = (f32[129,8,128]{2,1,0:T(8,128)}, f32[129,8,128]{2,1,0:T(8,128)S(1)}, u32[]{:S(2)}) copy-start(f32[129,8,128]{2,1,0:T(8,128)S(1)} %pad_maximum_fusion.source_rows_ref.perm_rows_ref.head_rows_ref) | copy-start | bytes 1585156
  18.4 9.3 %collective-permute-start.2 = (f32[3,129,72]{2,0,1:T(4,128)S(1)}, f32[3,129,72]{2,0,1:T(4,128)S(1)}, u32[]{:S(2)}, u32[]{:S(2)}) collective-permute-start(f32[3,129,72]{2,0,1:T(4,128)S(1)} %get-tuple-element.13), channel_id=1, source_target_pairs={{1,0},{2,1},{3,2},{4,3},{5,4},{6,5},{7,6},{8,7},{9,8},{10,9},{11,1... | collective-permute-start | bytes 334376 | tf_op jit(solution)/shard_map/ppermute | solution.py:21
  19.7 9.8 %collective-permute-start.3 = (f32[3,129,72]{2,0,1:T(4,128)S(1)}, f32[3,129,72]{2,0,1:T(4,128)S(1)}, u32[]{:S(2)}, u32[]{:S(2)}) collective-permute-start(f32[3,129,72]{2,0,1:T(4,128)S(1)} %get-tuple-element.14), channel_id=1, source_target_pairs={{0,1},{1,2},{2,3},{3,4},{4,5},{5,6},{6,7},{7,8},{8,9},{9,10},{10,1... | collective-permute-start | bytes 334376 | tf_op jit(solution)/shard_map/ppermute | solution.py:21
  65.6 30.1 %copy-start.5 = (f32[1024]{0:T(1024)S(1)}, f32[1024]{0:T(1024)}, u32[]{:S(2)}) copy-start(f32[1024]{0:T(1024)} %param.14) | copy-start | bytes 12292
  91.4 15.5 %all-to-all-start.1 = ((f32[128,1,512]{2,1,0:T(1,128)}), f32[128,1,512]{2,1,0:T(1,128)S(1)}, u32[]{:S(2)}, u32[]{:S(2)}) async-start(f32[128,1,512]{2,1,0:T(1,128)} %broadcast_in_dim.76), calls=%async_computation.1 | async-start | bytes 524288 | tf_op jit(solution)/shard_map/all_to_all | solution.py:112
  107.6 15.0 %copy-start.2 = (f32[64,1024]{1,0:T(8,128)}, f32[64,1024]{1,0:T(8,128)S(1)}, u32[]{:S(2)}) copy-start(f32[64,1024]{1,0:T(8,128)S(1)} %reshape.242) | copy-start | bytes 786436
  107.6 15.0 %copy-start.6 = (f32[64,1024]{1,0:T(8,128)S(1)}, f32[64,1024]{1,0:T(8,128)}, u32[]{:S(2)}) copy-start(f32[64,1024]{1,0:T(8,128)} %param.15) | copy-start | bytes 786436
  107.6 15.0 %copy-start.7 = (f32[1024]{0:T(1024)S(1)}, f32[1024]{0:T(1024)}, u32[]{:S(2)}) copy-start(f32[1024]{0:T(1024)} %param.13) | copy-start | bytes 12292

commit v12 on v11

--- a/solution.py
+++ b/solution.py
@@ -142,7 +142,7 @@
         out_ref[pl.ds(r, members, stride=rows)] = values + shift
         return carry
 
-    lax.fori_loop(0, rows, body, 0, unroll=8)
+    lax.fori_loop(0, rows, body, 0, unroll=16)
 
 
 def run_update(perm, mixing):

time: 132 us -> 132 us (level)
  no operation moved by 1% of the time
where the time goes in v12:
time: 132 us
  Pallas kernels  29 us (22%)
  blocking collectives  24.2 us (18%)
  other arithmetic  17 us (13%)
  starting transfers between devices  16.4 us (12%)
  waiting for transfers between devices  15.9 us (12%)
  local copies, waits for them, and re-layouts  14.5 us (11%)
  matrix products  13.4 us (10%)
    all_to_all x1, blocking collectives, broadcast_from_owners(): own_chunk = lax.all_to_all(chunks, axes, 0, 0, tiled=True).sum(axis=0)  24.2 us
    pallas_call x1, Pallas kernels, run_stencil(): pl.pallas_call(stencil_kernel, grid=(blocks,), in_specs=[full2(mask.shape...  21.6 us
    ppermute x4, starting transfers between devices, send(): return lax.ppermute(piece, axis, pairs)  12.1 us
    all_to_all x1, waiting for transfers between devices, broadcast_from_owners(): return lax.all_to_all(spread, axes, 0, 0, tiled=True).reshape(value.shape)  10.7 us
    pallas_call x1, Pallas kernels, run_update(): pl.pallas_call(update_kernel, out_shape=jax.ShapeDtypeStruct(flat.shape,...  7.41 us
    another operation x3, other arithmetic, blending_weights(): factor = jnp.linalg.cholesky(system)  6.52 us
    dot_general x1, matrix products, per_device(): halo_cols = jnp.einsum('kmr,kl->mrl', received, selector, precision=highest)  5.72 us
    another operation x2, other arithmetic, blending_weights(): lax.linalg.triangular_solve(factor, half_solved, left_side=True, lower=Tr...  5.55 us
  transfers between devices with their start and end apart: 5, of which 3 were waited for; matrix products, arithmetic and copies ran while one was open for 6% of the time, Pallas kernels for 0%

profile of v12, /device:TPU:1, one launch (start us, length us, event | category | flops | bytes accessed | tf_op | source)
XLA Modules:
  0.0 131.5 jit_solution(165813992525253323)
XLA Ops:
  0.6 1.1 slice_convert_fusion.1
  1.7 1.1 fusion.52
  2.8 0.7 slice_bitcast_fusion.1
  3.6 3.3 %collective-permute-start = (f32[3,129,128]{2,0,1:T(4,128)S(1)}, f32[3,129,128]{2,0,1:T(4,128)S(1)}, u32[]{:S(2)}, u32[]{:S(2)}) collective-permute-start(f32[3,129,128]{2,0,1:T(4,128)S(1)} %maximum_bitcast_fusion), channel_id=1, source_target_pairs={{16,0},{32,16},{48,32},{64,48},{80,64},{96,80},{112,96},{17,1},{33... | collective-permute-start | bytes 594440 | tf_op jit(solution)/shard_map/ppermute | solution.py:21
  7.0 3.6 %collective-permute-start.1 = (f32[3,129,128]{2,0,1:T(4,128)S(1)}, f32[3,129,128]{2,0,1:T(4,128)S(1)}, u32[]{:S(2)}, u32[]{:S(2)}) collective-permute-start(f32[3,129,128]{2,0,1:T(4,128)S(1)} %maximum_bitcast_fusion.1), channel_id=1, source_target_pairs={{0,16},{16,32},{32,48},{48,64},{64,80},{80,96},{96,112},{1,17},{17... | collective-permute-start | bytes 594440 | tf_op jit(solution)/shard_map/ppermute | solution.py:21
  10.6 4.1 %fusion.32 = f32[8,64,64]{2,0,1:T(8,128)S(1)} fusion(f32[64,64,128]{2,1,0:T(8,128)} %perm_ref.1, s32[8]{0:T(128)S(1)} %compare_select_fusion.4, pred[8]{0:T(512)(128)(4,1)S(1)} %compare_or_fusion), kind=kOutput, calls=%fused_computation.55 | convolution fusion | flops 50333696 | bytes 2228264 | tf_op jit(solution)/shard_map/dot_general | solution.py:218
  14.7 0.9 fusion.35
  15.7 0.2 convolution_bitcast_fusion
  16.0 0.1 broadcast_in_dim.67
  16.2 0.7 and_convert_fusion.mask_ref
  16.9 0.1 pad_maximum_fusion.source_rows_ref.perm_rows_ref.head_rows_ref
  17.1 0.6 fusion
  17.7 0.4 copy.21
  18.1 0.2 pad_maximum_fusion.1
  18.3 0.1 fusion.53
  18.4 1.3 collective-permute-start.2
  19.7 4.0 %collective-permute-start.3 = (f32[3,129,72]{2,0,1:T(4,128)S(1)}, f32[3,129,72]{2,0,1:T(4,128)S(1)}, u32[]{:S(2)}, u32[]{:S(2)}) collective-permute-start(f32[3,129,72]{2,0,1:T(4,128)S(1)} %get-tuple-element.14), channel_id=1, source_target_pairs={{0,1},{1,2},{2,3},{3,4},{4,5},{5,6},{6,7},{7,8},{8,9},{9,10},{10,1... | collective-permute-start | bytes 334376 | tf_op jit(solution)/shard_map/ppermute | solution.py:21
  23.9 0.2 broadcast_in_dim.71
  24.1 0.2 broadcast_in_dim.73
  24.3 3.4 %collective-permute-done.2 = f32[3,129,72]{2,0,1:T(4,128)S(1)} collective-permute-done((f32[3,129,72]{2,0,1:T(4,128)S(1)}, f32[3,129,72]{2,0,1:T(4,128)S(1)}, u32[]{:S(2)}, u32[]{:S(2)}) %collective-permute-start.2) | collective-permute-done | bytes 111488 | tf_op jit(solution)/shard_map/ppermute | solution.py:21
  27.7 1.8 %collective-permute-done.3 = f32[3,129,72]{2,0,1:T(4,128)S(1)} collective-permute-done((f32[3,129,72]{2,0,1:T(4,128)S(1)}, f32[3,129,72]{2,0,1:T(4,128)S(1)}, u32[]{:S(2)}, u32[]{:S(2)}) %collective-permute-start.3) | collective-permute-done | bytes 111488 | tf_op jit(solution)/shard_map/ppermute | solution.py:21
  29.4 5.7 %fusion.2.source_cols_ref.perm_cols_ref.head_cols_ref = f32[129,72,128]{2,1,0:T(8,128)} fusion(f32[3,129,72]{2,0,1:T(4,128)S(1)} %collective-permute-done.3, f32[3,129,72]{2,0,1:T(4,128)S(1)} %collective-permute-done.2, f32[8]{0:T(128)S(1)} %pad.8.clone, s32[8]{0:T(128)S(1)} %compare_select_fusion.4, pred[8]{0:T(512)(128)(4,1)S(1)} %compare_or_fusion), kind=kOutput, calls=%fused_computation.6 | convolution fusion | flops 114281600 | bytes 4978440 | tf_op jit(solution)/shard_map/kmr,kl->mrl/dot_general | solution.py:232
  35.2 21.6 %shard_map.103 = (bf16[64,64,128]{2,1,0:T(8,128)(2,1)}, f32[64,64,128]{2,1,0:T(8,128)}) custom-call(f32[72,256]{1,0:T(8,128)} %and_convert_fusion.mask_ref, f32[64,128]{1,0:T(8,128)} %source_ref.1, f32[129,8,128]{2,1,0:T(8,128)} %copy-done, f32[129,72,128]{2,1,0:T(8,128)} %fusion.2.source_cols_ref.perm_cols_ref.head_cols_ref, f32[64,64,128]{2,1,0:T(8,128)} %perm_ref.1, ...), custom_call_target="tpu_custom_call" | custom-call | flops 94371840 | bytes 7340032 | tf_op jit(solution)/shard_map/pallas_call | solution.py:79
  56.8 3.8 %copy.26 = f32[64,64,128]{0,2,1:T(8,128)} copy(f32[64,64,128]{2,1,0:T(8,128)} %get-tuple-element.6) | data formatting | bytes 4194304 | tf_op jit(solution)/shard_map/reshape | solution.py:240
  60.6 5.0 %gather_fusion = f32[1024,64]{1,0:T(8,128)S(1)} fusion(f32[64,8192]{0,1:T(8,128)} %bitcast.53, s32[1024]{0:T(1024)S(1)} %broadcast_clamp_fusion), kind=kCustom, calls=%fused_computation | custom fusion | bytes 528384 | tf_op jit(solution)/shard_map/jit(_take)/gather | solution.py:240
  65.6 0.2 copy.23
  65.9 0.3 copy.24
  66.2 24.2 %all_to_all.12 = f32[128,1,512]{2,1,0:T(1,128)S(1)} all-to-all(f32[128,1,512]{2,1,0:T(1,128)S(1)} %copy.24), channel_id=1, replica_groups=mesh['row'=8,'col'=16] {'row','col'}, dimensions={0} | all-to-all | bytes 524288 | tf_op jit(solution)/shard_map/all_to_all | solution.py:110
  90.4 0.2 reduce_sum.18
  90.6 0.8 broadcast_in_dim.76
  91.4 4.3 %all-to-all-start.1 = ((f32[128,1,512]{2,1,0:T(1,128)}), f32[128,1,512]{2,1,0:T(1,128)S(1)}, u32[]{:S(2)}, u32[]{:S(2)}) async-start(f32[128,1,512]{2,1,0:T(1,128)} %broadcast_in_dim.76), calls=%async_computation.1 | async-start | bytes 524288 | tf_op jit(solution)/shard_map/all_to_all | solution.py:112
  95.8 0.4 div.58
  96.2 10.7 %all-to-all-done.1 = f32[128,1,512]{2,1,0:T(1,128)S(1)} async-done(((f32[128,1,512]{2,1,0:T(1,128)}), f32[128,1,512]{2,1,0:T(1,128)S(1)}, u32[]{:S(2)}, u32[]{:S(2)}) %all-to-all-start.1) | async-done | bytes 262176 | tf_op jit(solution)/shard_map/all_to_all | solution.py:112
  106.9 0.6 reduce.7
  107.5 0.1 reshape.242
  107.8 0.4 sub.36
  108.2 1.6 %fusion.51 = (f32[128,512]{1,0:T(8,128)S(1)}, f32[128,512]{1,0:T(8,128)S(1)}) fusion(f32[128,1,512]{2,1,0:T(1,128)S(1)} %all-to-all-done.1, f32[128,1,512]{2,1,0:T(1,128)S(1)} %sub.36, f32[128,1,512]{2,1,0:T(1,128)S(1)} %div.58), kind=kLoop, calls=%fused_computation.82 | loop fusion | flops 196608 | bytes 1310720 | tf_op jit(solution)/shard_map/div | solution.py:164
  109.8 0.1 div.60
  109.9 0.1 div.61
  110.0 0.4 fusion.54
  110.5 5.8 %cholesky.17 = f32[64,64]{1,0:T(8,128)S(1)} custom-call(f32[64,64]{1,0:T(8,128)S(1)} %fusion.26), custom_call_target="Cholesky" | custom-call | tf_op jit(solution)/shard_map/jit(cholesky)/cholesky | solution.py:171
  116.4 0.6 compare_reduce_fusion
  117.0 0.7 fusion.20
  117.7 4.9 %custom-call.8 = f32[1,64,64]{1,2,0:T(8,128)S(1)} custom-call(f32[1,64,64]{2,1,0:T(8,128)S(1)} %fusion.20), custom_call_target="InvertDiagBlocksLowerTriangular" | custom-call | tf_op jit(solution)/shard_map/triangular_solve | solution.py:173
  122.6 0.4 fusion.8
  123.0 0.2 fusion.23
  123.3 0.9 fusion.21.mix_t_ref
  124.1 7.4 %shard_map.104 = f32[4096,128]{1,0:T(8,128)} custom-call(f32[64,64]{1,0:T(8,128)} %fusion.21.mix_t_ref, f32[4096,128]{1,0:T(8,128)} %bitcast.52), custom_call_target="tpu_custom_call" | custom-call | flops 67108864 | bytes 4194304 | tf_op jit(solution)/shard_map/pallas_call | solution.py:151
  (50 shorter events, 1.0 us)
Async XLA Ops:
  0.6 14.1 %copy-start.1 = (bf16[64,64,128]{2,1,0:T(8,128)(2,1)S(1)}, bf16[64,64,128]{2,1,0:T(8,128)(2,1)}, u32[]{:S(2)}) copy-start(bf16[64,64,128]{2,1,0:T(8,128)(2,1)} %head_ref.1) | copy-start | bytes 3145732
  3.6 13.3 %collective-permute-start = (f32[3,129,128]{2,0,1:T(4,128)S(1)}, f32[3,129,128]{2,0,1:T(4,128)S(1)}, u32[]{:S(2)}, u32[]{:S(2)}) collective-permute-start(f32[3,129,128]{2,0,1:T(4,128)S(1)} %maximum_bitcast_fusion), channel_id=1, source_target_pairs={{16,0},{32,16},{48,32},{64,48},{80,64},{96,80},{112,96},{17,1},{33... | collective-permute-start | bytes 594440 | tf_op jit(solution)/shard_map/ppermute | solution.py:21
  6.9 8.8 %copy-start.3 = (f32[64,128]{1,0:T(8,128)S(1)}, f32[64,128]{1,0:T(8,128)}, u32[]{:S(2)}) copy-start(f32[64,128]{1,0:T(8,128)} %source_ref.1) | copy-start | bytes 98308
  6.9 9.0 %copy-start.4 = (s32[4,256]{1,0:T(4,128)S(1)}, s32[4,256]{1,0:T(4,128)}, u32[]{:S(2)}) copy-start(s32[4,256]{1,0:T(4,128)} %param.11) | copy-start | bytes 12292
  6.9 9.1 %copy-start.8 = (s32[4]{0:T(128)S(1)}, s32[4]{0:T(128)}, u32[]{:S(2)}) copy-start(s32[4]{0:T(128)} %param.12) | copy-start | bytes 52
  7.0 9.9 %collective-permute-start.1 = (f32[3,129,128]{2,0,1:T(4,128)S(1)}, f32[3,129,128]{2,0,1:T(4,128)S(1)}, u32[]{:S(2)}, u32[]{:S(2)}) collective-permute-start(f32[3,129,128]{2,0,1:T(4,128)S(1)} %maximum_bitcast_fusion.1), channel_id=1, source_target_pairs={{0,16},{16,32},{32,48},{48,64},{64,80},{80,96},{96,112},{1,17},{17... | collective-permute-start | bytes 594440 | tf_op jit(solution)/shard_map/ppermute | solution.py:21
  17.1 6.9 %copy-start = (f32[129,8,128]{2,1,0:T(8,128)}, f32[129,8,128]{2,1,0:T(8,128)S(1)}, u32[]{:S(2)}) copy-start(f32[129,8,128]{2,1,0:T(8,128)S(1)} %pad_maximum_fusion.source_rows_ref.perm_rows_ref.head_rows_ref) | copy-start | bytes 1585156
  18.4 9.3 %collective-permute-start.2 = (f32[3,129,72]{2,0,1:T(4,128)S(1)}, f32[3,129,72]{2,0,1:T(4,128)S(1)}, u32[]{:S(2)}, u32[]{:S(2)}) collective-permute-start(f32[3,129,72]{2,0,1:T(4,128)S(1)} %get-tuple-element.13), channel_id=1, source_target_pairs={{1,0},{2,1},{3,2},{4,3},{5,4},{6,5},{7,6},{8,7},{9,8},{10,9},{11,1... | collective-permute-start | bytes 334376 | tf_op jit(solution)/shard_map/ppermute | solution.py:21
  19.7 9.8 %collective-permute-start.3 = (f32[3,129,72]{2,0,1:T(4,128)S(1)}, f32[3,129,72]{2,0,1:T(4,128)S(1)}, u32[]{:S(2)}, u32[]{:S(2)}) collective-permute-start(f32[3,129,72]{2,0,1:T(4,128)S(1)} %get-tuple-element.14), channel_id=1, source_target_pairs={{0,1},{1,2},{2,3},{3,4},{4,5},{5,6},{6,7},{7,8},{8,9},{9,10},{10,1... | collective-permute-start | bytes 334376 | tf_op jit(solution)/shard_map/ppermute | solution.py:21
  65.6 30.1 %copy-start.5 = (f32[1024]{0:T(1024)S(1)}, f32[1024]{0:T(1024)}, u32[]{:S(2)}) copy-start(f32[1024]{0:T(1024)} %param.14) | copy-start | bytes 12292
  91.4 15.5 %all-to-all-start.1 = ((f32[128,1,512]{2,1,0:T(1,128)}), f32[128,1,512]{2,1,0:T(1,128)S(1)}, u32[]{:S(2)}, u32[]{:S(2)}) async-start(f32[128,1,512]{2,1,0:T(1,128)} %broadcast_in_dim.76), calls=%async_computation.1 | async-start | bytes 524288 | tf_op jit(solution)/shard_map/all_to_all | solution.py:112
  107.6 15.0 %copy-start.2 = (f32[64,1024]{1,0:T(8,128)}, f32[64,1024]{1,0:T(8,128)S(1)}, u32[]{:S(2)}) copy-start(f32[64,1024]{1,0:T(8,128)S(1)} %reshape.242) | copy-start | bytes 786436
  107.6 15.0 %copy-start.6 = (f32[64,1024]{1,0:T(8,128)S(1)}, f32[64,1024]{1,0:T(8,128)}, u32[]{:S(2)}) copy-start(f32[64,1024]{1,0:T(8,128)} %param.15) | copy-start | bytes 786436
  107.6 15.0 %copy-start.7 = (f32[1024]{0:T(1024)S(1)}, f32[1024]{0:T(1024)}, u32[]{:S(2)}) copy-start(f32[1024]{0:T(1024)} %param.13) | copy-start | bytes 12292

commit v13 on v11

--- a/solution.py
+++ b/solution.py
@@ -129,17 +129,15 @@
     return centre_press + time_step * (flux_total + source)
 
 
-def update_kernel(mix_t_ref, perm_ref, out_ref):
+def update_kernel(mix_t_ref, perm_ref, anomaly_ref, out_ref):
     members = mix_t_ref.shape[0]
     rows = perm_ref.shape[0] // members
     mix_t = mix_t_ref[...]
-    spread = math.sqrt(members - 1)
 
     def body(r, carry):
-        values = perm_ref[pl.ds(r, members, stride=rows)]
-        anomalies = (values - jnp.mean(values, axis=0, keepdims=True)) / spread
-        shift = jnp.dot(mix_t, anomalies, precision=lax.Precision.HIGHEST, preferred_element_type=jnp.float32)
-        out_ref[pl.ds(r, members, stride=rows)] = values + shift
+        window = pl.ds(r, members, stride=rows)
+        shift = jnp.dot(mix_t, anomaly_ref[window], precision=lax.Precision.HIGHEST, preferred_element_type=jnp.float32)
+        out_ref[window] = perm_ref[window] + shift
         return carry
 
     lax.fori_loop(0, rows, body, 0, unroll=8)
@@ -147,14 +145,15 @@
 
 def run_update(perm, mixing):
     members, rows, cols = perm.shape
+    anomalies = (perm - jnp.mean(perm, axis=0, keepdims=True)) / math.sqrt(members - 1)
     flat = perm.reshape(members * rows, cols)
     out = pl.pallas_call(
         update_kernel,
         out_shape=jax.ShapeDtypeStruct(flat.shape, jnp.float32),
         cost_estimate=pl.CostEstimate(
-            flops=2 * members * members * rows * cols, transcendentals=0, bytes_accessed=8 * members * rows * cols
+            flops=2 * members * members * rows * cols, transcendentals=0, bytes_accessed=12 * members * rows * cols
         ),
-    )(mixing.T, flat)
+    )(mixing.T, flat, anomalies.reshape(flat.shape))
     return out.reshape(perm.shape)
 
 

time: 132 us -> 134 us (1.015)
  blocking collectives: 24.2 us -> 0 us
  starting transfers between devices: 16.4 us -> 29.7 us
  waiting for transfers between devices: 15.9 us -> 25.2 us
  other arithmetic: 17 us -> 18.7 us
    all_to_all x1 -> x0, blocking collectives: 24.2 us -> none  [broadcast_from_owners(): own_chunk = lax.all_to_all(chunks, axes, 0, 0, tiled=True).sum(axis=0)]
    all_to_all x0 -> x1, starting transfers between devices: none -> 13.3 us  [broadcast_from_owners(): own_chunk = lax.all_to_all(chunks, axes, 0, 0, tiled=True).sum(axis=0)]
    all_to_all x0 -> x1, waiting for transfers between devices: none -> 10.4 us  [broadcast_from_owners(): own_chunk = lax.all_to_all(chunks, axes, 0, 0, tiled=True).sum(axis=0)]
    div x0 -> x2, other arithmetic: none -> 1.59 us  [the longest x1 1.59 us: run_update(): (perm - jnp.mean(perm, axis=0, keepdims=True)) / math.sqrt(members - 1)]
  transfers between devices with their start and end apart: 5 -> 6, of which waited for: 3 -> 4; matrix products, arithmetic and copies ran while one was open for 6% -> 7% of each run, Pallas kernels for 0% -> 0%
where the time goes in v13:
time: 134 us; the launch traced here: 133 us
  Pallas kernels  30 us (22%)
  starting transfers between devices  29.7 us (22%)
  waiting for transfers between devices  25.2 us (19%)
  other arithmetic  18.7 us (14%)
  local copies, waits for them, and re-layouts  15.2 us (11%)
  matrix products  13.4 us (10%)
    pallas_call x1, Pallas kernels, run_stencil(): pl.pallas_call(stencil_kernel, grid=(blocks,), in_specs=[full2(mask.shape...  21.6 us
    all_to_all x1, starting transfers between devices, broadcast_from_owners(): own_chunk = lax.all_to_all(chunks, axes, 0, 0, tiled=True).sum(axis=0)  13.3 us
    ppermute x4, starting transfers between devices, send(): return lax.ppermute(piece, axis, pairs)  12.1 us
    all_to_all x1, waiting for transfers between devices, broadcast_from_owners(): own_chunk = lax.all_to_all(chunks, axes, 0, 0, tiled=True).sum(axis=0)  10.4 us
    all_to_all x1, waiting for transfers between devices, broadcast_from_owners(): return lax.all_to_all(spread, axes, 0, 0, tiled=True).reshape(value.shape)  9.62 us
    pallas_call x1, Pallas kernels, run_update(): pl.pallas_call(update_kernel, out_shape=jax.ShapeDtypeStruct(flat.shape,...  8.36 us
    another operation x3, other arithmetic, blending_weights(): factor = jnp.linalg.cholesky(system)  6.52 us
    dot_general x1, matrix products, per_device(): halo_cols = jnp.einsum('kmr,kl->mrl', received, selector, precision=highest)  5.72 us
  transfers between devices with their start and end apart: 6, of which 4 were waited for; matrix products, arithmetic and copies ran while one was open for 7% of the time, Pallas kernels for 0%

profile of v13, /device:TPU:1, one launch (start us, length us, event | category | flops | bytes accessed | tf_op | source)
XLA Modules:
  0.0 133.4 jit_solution(15284063026719321332)
XLA Ops:
  0.6 1.1 slice_convert_fusion.1
  1.7 1.1 fusion.52
  2.8 0.7 slice_bitcast_fusion.1
  3.6 3.3 %collective-permute-start = (f32[3,129,128]{2,0,1:T(4,128)S(1)}, f32[3,129,128]{2,0,1:T(4,128)S(1)}, u32[]{:S(2)}, u32[]{:S(2)}) collective-permute-start(f32[3,129,128]{2,0,1:T(4,128)S(1)} %maximum_bitcast_fusion), channel_id=1, source_target_pairs={{16,0},{32,16},{48,32},{64,48},{80,64},{96,80},{112,96},{17,1},{33... | collective-permute-start | bytes 594440 | tf_op jit(solution)/shard_map/ppermute | solution.py:21
  7.0 3.6 %collective-permute-start.1 = (f32[3,129,128]{2,0,1:T(4,128)S(1)}, f32[3,129,128]{2,0,1:T(4,128)S(1)}, u32[]{:S(2)}, u32[]{:S(2)}) collective-permute-start(f32[3,129,128]{2,0,1:T(4,128)S(1)} %maximum_bitcast_fusion.1), channel_id=1, source_target_pairs={{0,16},{16,32},{32,48},{48,64},{64,80},{80,96},{96,112},{1,17},{17... | collective-permute-start | bytes 594440 | tf_op jit(solution)/shard_map/ppermute | solution.py:21
  10.6 4.1 %fusion.32 = f32[8,64,64]{2,0,1:T(8,128)S(1)} fusion(f32[64,64,128]{2,1,0:T(8,128)} %perm_ref.1, s32[8]{0:T(128)S(1)} %compare_select_fusion.4, pred[8]{0:T(512)(128)(4,1)S(1)} %compare_or_fusion), kind=kOutput, calls=%fused_computation.57 | convolution fusion | flops 50333696 | bytes 2228264 | tf_op jit(solution)/shard_map/dot_general | solution.py:217
  14.7 0.9 fusion.35
  15.7 0.2 convolution_bitcast_fusion
  16.2 0.7 and_convert_fusion.mask_ref
  16.9 0.1 pad_maximum_fusion.source_rows_ref.perm_rows_ref.head_rows_ref
  17.1 0.6 fusion
  17.7 0.4 copy.21
  18.1 0.2 pad_maximum_fusion.1
  18.4 1.3 collective-permute-start.2
  19.7 4.0 %collective-permute-start.3 = (f32[3,129,72]{2,0,1:T(4,128)S(1)}, f32[3,129,72]{2,0,1:T(4,128)S(1)}, u32[]{:S(2)}, u32[]{:S(2)}) collective-permute-start(f32[3,129,72]{2,0,1:T(4,128)S(1)} %get-tuple-element.14), channel_id=1, source_target_pairs={{0,1},{1,2},{2,3},{3,4},{4,5},{5,6},{6,7},{7,8},{8,9},{9,10},{10,1... | collective-permute-start | bytes 334376 | tf_op jit(solution)/shard_map/ppermute | solution.py:21
  23.9 0.2 broadcast_in_dim.72
  24.1 0.2 broadcast_in_dim.74
  24.3 3.4 %collective-permute-done.2 = f32[3,129,72]{2,0,1:T(4,128)S(1)} collective-permute-done((f32[3,129,72]{2,0,1:T(4,128)S(1)}, f32[3,129,72]{2,0,1:T(4,128)S(1)}, u32[]{:S(2)}, u32[]{:S(2)}) %collective-permute-start.2) | collective-permute-done | bytes 111488 | tf_op jit(solution)/shard_map/ppermute | solution.py:21
  27.7 1.8 %collective-permute-done.3 = f32[3,129,72]{2,0,1:T(4,128)S(1)} collective-permute-done((f32[3,129,72]{2,0,1:T(4,128)S(1)}, f32[3,129,72]{2,0,1:T(4,128)S(1)}, u32[]{:S(2)}, u32[]{:S(2)}) %collective-permute-start.3) | collective-permute-done | bytes 111488 | tf_op jit(solution)/shard_map/ppermute | solution.py:21
  29.4 5.7 %fusion.2.source_cols_ref.perm_cols_ref.head_cols_ref = f32[129,72,128]{2,1,0:T(8,128)} fusion(f32[3,129,72]{2,0,1:T(4,128)S(1)} %collective-permute-done.3, f32[3,129,72]{2,0,1:T(4,128)S(1)} %collective-permute-done.2, f32[8]{0:T(128)S(1)} %pad.8.clone, s32[8]{0:T(128)S(1)} %compare_select_fusion.4, pred[8]{0:T(512)(128)(4,1)S(1)} %compare_or_fusion), kind=kOutput, calls=%fused_computation.7 | convolution fusion | flops 114281600 | bytes 4978440 | tf_op jit(solution)/shard_map/kmr,kl->mrl/dot_general | solution.py:231
  35.2 21.6 %shard_map.103 = (bf16[64,64,128]{2,1,0:T(8,128)(2,1)}, f32[64,64,128]{2,1,0:T(8,128)}) custom-call(f32[72,256]{1,0:T(8,128)} %and_convert_fusion.mask_ref, f32[64,128]{1,0:T(8,128)} %source_ref.1, f32[129,8,128]{2,1,0:T(8,128)} %copy-done.1, f32[129,72,128]{2,1,0:T(8,128)} %fusion.2.source_cols_ref.perm_cols_ref.head_cols_ref, f32[64,64,128]{2,1,0:T(8,128)} %perm_ref.1, ...), custom_call_target="tpu_custom_call" | custom-call | flops 94371840 | bytes 7340032 | tf_op jit(solution)/shard_map/pallas_call | solution.py:79
  56.8 3.8 %copy.26 = f32[64,64,128]{0,2,1:T(8,128)} copy(f32[64,64,128]{2,1,0:T(8,128)} %get-tuple-element.6) | data formatting | bytes 4194304 | tf_op jit(solution)/shard_map/reshape | solution.py:239
  60.6 5.0 %gather_fusion = f32[1024,64]{1,0:T(8,128)S(1)} fusion(f32[64,8192]{0,1:T(8,128)} %bitcast.54, s32[1024]{0:T(1024)S(1)} %broadcast_clamp_fusion), kind=kCustom, calls=%fused_computation | custom fusion | bytes 528384 | tf_op jit(solution)/shard_map/jit(_take)/gather | solution.py:239
  65.6 0.2 copy.23
  65.9 1.0 copy.24
  66.9 13.3 %all-to-all-start = ((f32[128,1,512]{2,1,0:T(1,128)}), f32[128,1,512]{2,1,0:T(1,128)S(1)}, u32[]{:S(2)}, u32[]{:S(2)}) async-start(f32[128,1,512]{2,1,0:T(1,128)} %copy.24), calls=%async_computation | async-start | bytes 524288 | tf_op jit(solution)/shard_map/all_to_all | solution.py:110
  80.2 0.1 reduce_sum.29
  80.4 0.4 div.70
  80.8 10.4 %all-to-all-done = f32[128,1,512]{2,1,0:T(1,128)S(1)} async-done(((f32[128,1,512]{2,1,0:T(1,128)}), f32[128,1,512]{2,1,0:T(1,128)S(1)}, u32[]{:S(2)}, u32[]{:S(2)}) %all-to-all-start) | async-done | bytes 262176 | tf_op jit(solution)/shard_map/all_to_all | solution.py:110
  91.3 0.2 reduce_sum.27
  91.5 0.8 broadcast_in_dim.77
  92.3 4.3 %all-to-all-start.1 = ((f32[128,1,512]{2,1,0:T(1,128)}), f32[128,1,512]{2,1,0:T(1,128)S(1)}, u32[]{:S(2)}, u32[]{:S(2)}) async-start(f32[128,1,512]{2,1,0:T(1,128)} %broadcast_in_dim.77), calls=%async_computation.1 | async-start | bytes 524288 | tf_op jit(solution)/shard_map/all_to_all | solution.py:112
  96.6 1.6 %subtract_multiply_fusion = f32[64,64,128]{2,1,0:T(8,128)} fusion(f32[64,64,128]{2,1,0:T(8,128)S(1)} %copy-done, f32[64,128]{1,0:T(8,128)S(1)} %broadcast_multiply_fusion), kind=kLoop, calls=%fused_computation.1 | loop fusion | flops 1048576 | bytes 4227072 | tf_op jit(solution)/shard_map/div | solution.py:148
  98.2 9.6 %all-to-all-done.1 = f32[128,1,512]{2,1,0:T(1,128)S(1)} async-done(((f32[128,1,512]{2,1,0:T(1,128)}), f32[128,1,512]{2,1,0:T(1,128)S(1)}, u32[]{:S(2)}, u32[]{:S(2)}) %all-to-all-start.1) | async-done | bytes 262176 | tf_op jit(solution)/shard_map/all_to_all | solution.py:112
  107.8 0.6 reduce.7
  108.4 0.1 reshape.249
  108.7 0.4 sub.44
  109.1 1.6 %fusion.51 = (f32[128,512]{1,0:T(8,128)S(1)}, f32[128,512]{1,0:T(8,128)S(1)}) fusion(f32[128,1,512]{2,1,0:T(1,128)S(1)} %all-to-all-done.1, f32[128,1,512]{2,1,0:T(1,128)S(1)} %sub.44, f32[128,1,512]{2,1,0:T(1,128)S(1)} %div.70), kind=kLoop, calls=%fused_computation.84 | loop fusion | flops 196608 | bytes 1310720 | tf_op jit(solution)/shard_map/div | solution.py:163
  110.7 0.1 div.72
  110.9 0.4 fusion.54
  111.4 5.8 %cholesky.17 = f32[64,64]{1,0:T(8,128)S(1)} custom-call(f32[64,64]{1,0:T(8,128)S(1)} %fusion.26), custom_call_target="Cholesky" | custom-call | tf_op jit(solution)/shard_map/jit(cholesky)/cholesky | solution.py:170
  117.3 0.6 compare_reduce_fusion
  117.9 0.7 fusion.20
  118.6 4.9 %custom-call.8 = f32[1,64,64]{1,2,0:T(8,128)S(1)} custom-call(f32[1,64,64]{2,1,0:T(8,128)S(1)} %fusion.20), custom_call_target="InvertDiagBlocksLowerTriangular" | custom-call | tf_op jit(solution)/shard_map/triangular_solve | solution.py:172
  123.5 0.4 fusion.8
  123.9 0.2 fusion.23
  124.2 0.9 fusion.21.mix_t_ref
  125.0 8.4 %shard_map.104 = f32[4096,128]{1,0:T(8,128)} custom-call(f32[64,64]{1,0:T(8,128)} %fusion.21.mix_t_ref, f32[4096,128]{1,0:T(8,128)} %bitcast.53, f32[4096,128]{1,0:T(8,128)} %bitcast.55), custom_call_target="tpu_custom_call" | custom-call | flops 67108864 | bytes 6291456 | tf_op jit(solution)/shard_map/pallas_call | solution.py:150
  (56 shorter events, 1.3 us)
Async XLA Ops:
  0.6 14.1 %copy-start.2 = (bf16[64,64,128]{2,1,0:T(8,128)(2,1)S(1)}, bf16[64,64,128]{2,1,0:T(8,128)(2,1)}, u32[]{:S(2)}) copy-start(bf16[64,64,128]{2,1,0:T(8,128)(2,1)} %head_ref.1) | copy-start | bytes 3145732
  3.6 13.3 %collective-permute-start = (f32[3,129,128]{2,0,1:T(4,128)S(1)}, f32[3,129,128]{2,0,1:T(4,128)S(1)}, u32[]{:S(2)}, u32[]{:S(2)}) collective-permute-start(f32[3,129,128]{2,0,1:T(4,128)S(1)} %maximum_bitcast_fusion), channel_id=1, source_target_pairs={{16,0},{32,16},{48,32},{64,48},{80,64},{96,80},{112,96},{17,1},{33... | collective-permute-start | bytes 594440 | tf_op jit(solution)/shard_map/ppermute | solution.py:21
  6.9 8.8 %copy-start.4 = (f32[64,128]{1,0:T(8,128)S(1)}, f32[64,128]{1,0:T(8,128)}, u32[]{:S(2)}) copy-start(f32[64,128]{1,0:T(8,128)} %source_ref.1) | copy-start | bytes 98308
  6.9 9.0 %copy-start.5 = (s32[4,256]{1,0:T(4,128)S(1)}, s32[4,256]{1,0:T(4,128)}, u32[]{:S(2)}) copy-start(s32[4,256]{1,0:T(4,128)} %param.11) | copy-start | bytes 12292
  6.9 9.1 %copy-start.9 = (s32[4]{0:T(128)S(1)}, s32[4]{0:T(128)}, u32[]{:S(2)}) copy-start(s32[4]{0:T(128)} %param.12) | copy-start | bytes 52
  7.0 9.9 %collective-permute-start.1 = (f32[3,129,128]{2,0,1:T(4,128)S(1)}, f32[3,129,128]{2,0,1:T(4,128)S(1)}, u32[]{:S(2)}, u32[]{:S(2)}) collective-permute-start(f32[3,129,128]{2,0,1:T(4,128)S(1)} %maximum_bitcast_fusion.1), channel_id=1, source_target_pairs={{0,16},{16,32},{32,48},{48,64},{64,80},{80,96},{96,112},{1,17},{17... | collective-permute-start | bytes 594440 | tf_op jit(solution)/shard_map/ppermute | solution.py:21
  17.1 6.9 %copy-start.1 = (f32[129,8,128]{2,1,0:T(8,128)}, f32[129,8,128]{2,1,0:T(8,128)S(1)}, u32[]{:S(2)}) copy-start(f32[129,8,128]{2,1,0:T(8,128)S(1)} %pad_maximum_fusion.source_rows_ref.perm_rows_ref.head_rows_ref) | copy-start | bytes 1585156
  18.4 9.3 %collective-permute-start.2 = (f32[3,129,72]{2,0,1:T(4,128)S(1)}, f32[3,129,72]{2,0,1:T(4,128)S(1)}, u32[]{:S(2)}, u32[]{:S(2)}) collective-permute-start(f32[3,129,72]{2,0,1:T(4,128)S(1)} %get-tuple-element.13), channel_id=1, source_target_pairs={{1,0},{2,1},{3,2},{4,3},{5,4},{6,5},{7,6},{8,7},{9,8},{10,9},{11,1... | collective-permute-start | bytes 334376 | tf_op jit(solution)/shard_map/ppermute | solution.py:21
  19.7 9.8 %collective-permute-start.3 = (f32[3,129,72]{2,0,1:T(4,128)S(1)}, f32[3,129,72]{2,0,1:T(4,128)S(1)}, u32[]{:S(2)}, u32[]{:S(2)}) collective-permute-start(f32[3,129,72]{2,0,1:T(4,128)S(1)} %get-tuple-element.14), channel_id=1, source_target_pairs={{0,1},{1,2},{2,3},{3,4},{4,5},{5,6},{6,7},{7,8},{8,9},{9,10},{10,1... | collective-permute-start | bytes 334376 | tf_op jit(solution)/shard_map/ppermute | solution.py:21
  65.6 14.6 %copy-start.6 = (f32[1024]{0:T(1024)S(1)}, f32[1024]{0:T(1024)}, u32[]{:S(2)}) copy-start(f32[1024]{0:T(1024)} %param.14) | copy-start | bytes 12292
  65.6 14.6 %copy-start = (f32[64,64,128]{2,1,0:T(8,128)S(1)}, f32[64,64,128]{2,1,0:T(8,128)}, u32[]{:S(2)}) copy-start(f32[64,64,128]{2,1,0:T(8,128)} %perm_ref.1) | copy-start | bytes 6291460
  66.9 24.4 %all-to-all-start = ((f32[128,1,512]{2,1,0:T(1,128)}), f32[128,1,512]{2,1,0:T(1,128)S(1)}, u32[]{:S(2)}, u32[]{:S(2)}) async-start(f32[128,1,512]{2,1,0:T(1,128)} %copy.24), calls=%async_computation | async-start | bytes 524288 | tf_op jit(solution)/shard_map/all_to_all | solution.py:110
  92.3 15.5 %all-to-all-start.1 = ((f32[128,1,512]{2,1,0:T(1,128)}), f32[128,1,512]{2,1,0:T(1,128)S(1)}, u32[]{:S(2)}, u32[]{:S(2)}) async-start(f32[128,1,512]{2,1,0:T(1,128)} %broadcast_in_dim.77), calls=%async_computation.1 | async-start | bytes 524288 | tf_op jit(solution)/shard_map/all_to_all | solution.py:112
  108.5 15.0 %copy-start.3 = (f32[64,1024]{1,0:T(8,128)}, f32[64,1024]{1,0:T(8,128)S(1)}, u32[]{:S(2)}) copy-start(f32[64,1024]{1,0:T(8,128)S(1)} %reshape.249) | copy-start | bytes 786436
  108.5 15.0 %copy-start.7 = (f32[64,1024]{1,0:T(8,128)S(1)}, f32[64,1024]{1,0:T(8,128)}, u32[]{:S(2)}) copy-start(f32[64,1024]{1,0:T(8,128)} %param.15) | copy-start | bytes 786436
  108.6 15.0 %copy-start.8 = (f32[1024]{0:T(1024)S(1)}, f32[1024]{0:T(1024)}, u32[]{:S(2)}) copy-start(f32[1024]{0:T(1024)} %param.13) | copy-start | bytes 12292

commit v14 on v11

--- a/solution.py
+++ b/solution.py
@@ -234,7 +234,7 @@
         "col", col_count, width, ext_cols
     )[None, :]
     pressure_low, hydraulic_head = run_stencil(
-        inside.astype(f32), recharge, halo_rows, halo_cols, logarithmic_conductivity, starting_head, 8
+        inside.astype(f32), recharge, halo_rows, halo_cols, logarithmic_conductivity, starting_head, 4
     )
     group_total, well_count = well_cells.shape
     local_data = jnp.take(hydraulic_head.reshape(member_count, row_count * col_count), well_cells.reshape(-1), axis=1)

time: 132 us -> 133 us (level)
  no operation moved by 1% of the time
where the time goes in v14:
time: 133 us
  Pallas kernels  30 us (23%)
  blocking collectives  24.2 us (18%)
  other arithmetic  17 us (13%)
  starting transfers between devices  16.4 us (12%)
  waiting for transfers between devices  15.9 us (12%)
  local copies, waits for them, and re-layouts  14.5 us (11%)
  matrix products  13.4 us (10%)
    all_to_all x1, blocking collectives, broadcast_from_owners(): own_chunk = lax.all_to_all(chunks, axes, 0, 0, tiled=True).sum(axis=0)  24.2 us
    pallas_call x1, Pallas kernels, run_stencil(): pl.pallas_call(stencil_kernel, grid=(blocks,), in_specs=[full2(mask.shape...  22.3 us
    ppermute x4, starting transfers between devices, send(): return lax.ppermute(piece, axis, pairs)  12.1 us
    all_to_all x1, waiting for transfers between devices, broadcast_from_owners(): return lax.all_to_all(spread, axes, 0, 0, tiled=True).reshape(value.shape)  10.7 us
    pallas_call x1, Pallas kernels, run_update(): pl.pallas_call(update_kernel, out_shape=jax.ShapeDtypeStruct(flat.shape,...  7.73 us
    another operation x3, other arithmetic, blending_weights(): factor = jnp.linalg.cholesky(system)  6.52 us
    dot_general x1, matrix products, per_device(): halo_cols = jnp.einsum('kmr,kl->mrl', received, selector, precision=highest)  5.72 us
    another operation x2, other arithmetic, blending_weights(): lax.linalg.triangular_solve(factor, half_solved, left_side=True, lower=Tr...  5.55 us
  transfers between devices with their start and end apart: 5, of which 3 were waited for; matrix products, arithmetic and copies ran while one was open for 6% of the time, Pallas kernels for 0%

profile of v14, /device:TPU:1, one launch (start us, length us, event | category | flops | bytes accessed | tf_op | source)
XLA Modules:
  0.0 132.5 jit_solution(12512480367296135829)
XLA Ops:
  0.6 1.1 slice_convert_fusion.1
  1.7 1.1 fusion.52
  2.8 0.7 slice_bitcast_fusion.1
  3.6 3.3 %collective-permute-start = (f32[3,129,128]{2,0,1:T(4,128)S(1)}, f32[3,129,128]{2,0,1:T(4,128)S(1)}, u32[]{:S(2)}, u32[]{:S(2)}) collective-permute-start(f32[3,129,128]{2,0,1:T(4,128)S(1)} %maximum_bitcast_fusion), channel_id=1, source_target_pairs={{16,0},{32,16},{48,32},{64,48},{80,64},{96,80},{112,96},{17,1},{33... | collective-permute-start | bytes 594440 | tf_op jit(solution)/shard_map/ppermute | solution.py:21
  7.0 3.6 %collective-permute-start.1 = (f32[3,129,128]{2,0,1:T(4,128)S(1)}, f32[3,129,128]{2,0,1:T(4,128)S(1)}, u32[]{:S(2)}, u32[]{:S(2)}) collective-permute-start(f32[3,129,128]{2,0,1:T(4,128)S(1)} %maximum_bitcast_fusion.1), channel_id=1, source_target_pairs={{0,16},{16,32},{32,48},{48,64},{64,80},{80,96},{96,112},{1,17},{17... | collective-permute-start | bytes 594440 | tf_op jit(solution)/shard_map/ppermute | solution.py:21
  10.6 4.1 %fusion.32 = f32[8,64,64]{2,0,1:T(8,128)S(1)} fusion(f32[64,64,128]{2,1,0:T(8,128)} %perm_ref.1, s32[8]{0:T(128)S(1)} %compare_select_fusion.4, pred[8]{0:T(512)(128)(4,1)S(1)} %compare_or_fusion), kind=kOutput, calls=%fused_computation.55 | convolution fusion | flops 50333696 | bytes 2228264 | tf_op jit(solution)/shard_map/dot_general | solution.py:218
  14.7 0.9 fusion.35
  15.7 0.2 convolution_bitcast_fusion
  16.0 0.1 broadcast_in_dim.67
  16.2 0.7 and_convert_fusion.mask_ref
  16.9 0.1 pad_maximum_fusion.source_rows_ref.perm_rows_ref.head_rows_ref
  17.1 0.6 fusion
  17.7 0.4 copy.21
  18.1 0.2 pad_maximum_fusion.1
  18.3 0.1 fusion.53
  18.4 1.3 collective-permute-start.2
  19.7 4.0 %collective-permute-start.3 = (f32[3,129,72]{2,0,1:T(4,128)S(1)}, f32[3,129,72]{2,0,1:T(4,128)S(1)}, u32[]{:S(2)}, u32[]{:S(2)}) collective-permute-start(f32[3,129,72]{2,0,1:T(4,128)S(1)} %get-tuple-element.14), channel_id=1, source_target_pairs={{0,1},{1,2},{2,3},{3,4},{4,5},{5,6},{6,7},{7,8},{8,9},{9,10},{10,1... | collective-permute-start | bytes 334376 | tf_op jit(solution)/shard_map/ppermute | solution.py:21
  23.9 0.2 broadcast_in_dim.71
  24.1 0.2 broadcast_in_dim.73
  24.3 3.4 %collective-permute-done.2 = f32[3,129,72]{2,0,1:T(4,128)S(1)} collective-permute-done((f32[3,129,72]{2,0,1:T(4,128)S(1)}, f32[3,129,72]{2,0,1:T(4,128)S(1)}, u32[]{:S(2)}, u32[]{:S(2)}) %collective-permute-start.2) | collective-permute-done | bytes 111488 | tf_op jit(solution)/shard_map/ppermute | solution.py:21
  27.7 1.8 %collective-permute-done.3 = f32[3,129,72]{2,0,1:T(4,128)S(1)} collective-permute-done((f32[3,129,72]{2,0,1:T(4,128)S(1)}, f32[3,129,72]{2,0,1:T(4,128)S(1)}, u32[]{:S(2)}, u32[]{:S(2)}) %collective-permute-start.3) | collective-permute-done | bytes 111488 | tf_op jit(solution)/shard_map/ppermute | solution.py:21
  29.4 5.7 %fusion.2.source_cols_ref.perm_cols_ref.head_cols_ref = f32[129,72,128]{2,1,0:T(8,128)} fusion(f32[3,129,72]{2,0,1:T(4,128)S(1)} %collective-permute-done.3, f32[3,129,72]{2,0,1:T(4,128)S(1)} %collective-permute-done.2, f32[8]{0:T(128)S(1)} %pad.8.clone, s32[8]{0:T(128)S(1)} %compare_select_fusion.4, pred[8]{0:T(512)(128)(4,1)S(1)} %compare_or_fusion), kind=kOutput, calls=%fused_computation.6 | convolution fusion | flops 114281600 | bytes 4978440 | tf_op jit(solution)/shard_map/kmr,kl->mrl/dot_general | solution.py:232
  35.2 22.3 %shard_map.103 = (bf16[64,64,128]{2,1,0:T(8,128)(2,1)}, f32[64,64,128]{2,1,0:T(8,128)}) custom-call(f32[72,256]{1,0:T(8,128)} %and_convert_fusion.mask_ref, f32[64,128]{1,0:T(8,128)} %source_ref.1, f32[129,8,128]{2,1,0:T(8,128)} %copy-done, f32[129,72,128]{2,1,0:T(8,128)} %fusion.2.source_cols_ref.perm_cols_ref.head_cols_ref, f32[64,64,128]{2,1,0:T(8,128)} %perm_ref.1, ...), custom_call_target="tpu_custom_call" | custom-call | flops 94371840 | bytes 7340032 | tf_op jit(solution)/shard_map/pallas_call | solution.py:79
  57.4 3.8 %copy.26 = f32[64,64,128]{0,2,1:T(8,128)} copy(f32[64,64,128]{2,1,0:T(8,128)} %get-tuple-element.6) | data formatting | bytes 4194304 | tf_op jit(solution)/shard_map/reshape | solution.py:240
  61.3 5.0 %gather_fusion = f32[1024,64]{1,0:T(8,128)S(1)} fusion(f32[64,8192]{0,1:T(8,128)} %bitcast.53, s32[1024]{0:T(1024)S(1)} %broadcast_clamp_fusion), kind=kCustom, calls=%fused_computation | custom fusion | bytes 528384 | tf_op jit(solution)/shard_map/jit(_take)/gather | solution.py:240
  66.3 0.2 copy.23
  66.6 0.3 copy.24
  66.8 24.2 %all_to_all.12 = f32[128,1,512]{2,1,0:T(1,128)S(1)} all-to-all(f32[128,1,512]{2,1,0:T(1,128)S(1)} %copy.24), channel_id=1, replica_groups=mesh['row'=8,'col'=16] {'row','col'}, dimensions={0} | all-to-all | bytes 524288 | tf_op jit(solution)/shard_map/all_to_all | solution.py:110
  91.1 0.2 reduce_sum.18
  91.3 0.8 broadcast_in_dim.76
  92.1 4.3 %all-to-all-start.1 = ((f32[128,1,512]{2,1,0:T(1,128)}), f32[128,1,512]{2,1,0:T(1,128)S(1)}, u32[]{:S(2)}, u32[]{:S(2)}) async-start(f32[128,1,512]{2,1,0:T(1,128)} %broadcast_in_dim.76), calls=%async_computation.1 | async-start | bytes 524288 | tf_op jit(solution)/shard_map/all_to_all | solution.py:112
  96.5 0.4 div.58
  96.9 10.7 %all-to-all-done.1 = f32[128,1,512]{2,1,0:T(1,128)S(1)} async-done(((f32[128,1,512]{2,1,0:T(1,128)}), f32[128,1,512]{2,1,0:T(1,128)S(1)}, u32[]{:S(2)}, u32[]{:S(2)}) %all-to-all-start.1) | async-done | bytes 262176 | tf_op jit(solution)/shard_map/all_to_all | solution.py:112
  107.6 0.6 reduce.7
  108.2 0.1 reshape.242
  108.5 0.4 sub.36
  108.9 1.6 %fusion.51 = (f32[128,512]{1,0:T(8,128)S(1)}, f32[128,512]{1,0:T(8,128)S(1)}) fusion(f32[128,1,512]{2,1,0:T(1,128)S(1)} %all-to-all-done.1, f32[128,1,512]{2,1,0:T(1,128)S(1)} %sub.36, f32[128,1,512]{2,1,0:T(1,128)S(1)} %div.58), kind=kLoop, calls=%fused_computation.82 | loop fusion | flops 196608 | bytes 1310720 | tf_op jit(solution)/shard_map/div | solution.py:164
  110.5 0.1 div.60
  110.6 0.1 div.61
  110.7 0.4 fusion.54
  111.2 5.8 %cholesky.17 = f32[64,64]{1,0:T(8,128)S(1)} custom-call(f32[64,64]{1,0:T(8,128)S(1)} %fusion.26), custom_call_target="Cholesky" | custom-call | tf_op jit(solution)/shard_map/jit(cholesky)/cholesky | solution.py:171
  117.0 0.6 compare_reduce_fusion
  117.7 0.7 fusion.20
  118.4 4.9 %custom-call.8 = f32[1,64,64]{1,2,0:T(8,128)S(1)} custom-call(f32[1,64,64]{2,1,0:T(8,128)S(1)} %fusion.20), custom_call_target="InvertDiagBlocksLowerTriangular" | custom-call | tf_op jit(solution)/shard_map/triangular_solve | solution.py:173
  123.3 0.4 fusion.8
  123.7 0.2 fusion.23
  123.9 0.9 fusion.21.mix_t_ref
  124.8 7.7 %shard_map.104 = f32[4096,128]{1,0:T(8,128)} custom-call(f32[64,64]{1,0:T(8,128)} %fusion.21.mix_t_ref, f32[4096,128]{1,0:T(8,128)} %bitcast.52), custom_call_target="tpu_custom_call" | custom-call | flops 67108864 | bytes 4194304 | tf_op jit(solution)/shard_map/pallas_call | solution.py:151
  (50 shorter events, 1.0 us)
Async XLA Ops:
  0.6 14.1 %copy-start.1 = (bf16[64,64,128]{2,1,0:T(8,128)(2,1)S(1)}, bf16[64,64,128]{2,1,0:T(8,128)(2,1)}, u32[]{:S(2)}) copy-start(bf16[64,64,128]{2,1,0:T(8,128)(2,1)} %head_ref.1) | copy-start | bytes 3145732
  3.6 13.3 %collective-permute-start = (f32[3,129,128]{2,0,1:T(4,128)S(1)}, f32[3,129,128]{2,0,1:T(4,128)S(1)}, u32[]{:S(2)}, u32[]{:S(2)}) collective-permute-start(f32[3,129,128]{2,0,1:T(4,128)S(1)} %maximum_bitcast_fusion), channel_id=1, source_target_pairs={{16,0},{32,16},{48,32},{64,48},{80,64},{96,80},{112,96},{17,1},{33... | collective-permute-start | bytes 594440 | tf_op jit(solution)/shard_map/ppermute | solution.py:21
  6.9 8.8 %copy-start.3 = (f32[64,128]{1,0:T(8,128)S(1)}, f32[64,128]{1,0:T(8,128)}, u32[]{:S(2)}) copy-start(f32[64,128]{1,0:T(8,128)} %source_ref.1) | copy-start | bytes 98308
  6.9 9.0 %copy-start.4 = (s32[4,256]{1,0:T(4,128)S(1)}, s32[4,256]{1,0:T(4,128)}, u32[]{:S(2)}) copy-start(s32[4,256]{1,0:T(4,128)} %param.11) | copy-start | bytes 12292
  6.9 9.1 %copy-start.8 = (s32[4]{0:T(128)S(1)}, s32[4]{0:T(128)}, u32[]{:S(2)}) copy-start(s32[4]{0:T(128)} %param.12) | copy-start | bytes 52
  7.0 9.9 %collective-permute-start.1 = (f32[3,129,128]{2,0,1:T(4,128)S(1)}, f32[3,129,128]{2,0,1:T(4,128)S(1)}, u32[]{:S(2)}, u32[]{:S(2)}) collective-permute-start(f32[3,129,128]{2,0,1:T(4,128)S(1)} %maximum_bitcast_fusion.1), channel_id=1, source_target_pairs={{0,16},{16,32},{32,48},{48,64},{64,80},{80,96},{96,112},{1,17},{17... | collective-permute-start | bytes 594440 | tf_op jit(solution)/shard_map/ppermute | solution.py:21
  17.1 6.9 %copy-start = (f32[129,8,128]{2,1,0:T(8,128)}, f32[129,8,128]{2,1,0:T(8,128)S(1)}, u32[]{:S(2)}) copy-start(f32[129,8,128]{2,1,0:T(8,128)S(1)} %pad_maximum_fusion.source_rows_ref.perm_rows_ref.head_rows_ref) | copy-start | bytes 1585156
  18.4 9.3 %collective-permute-start.2 = (f32[3,129,72]{2,0,1:T(4,128)S(1)}, f32[3,129,72]{2,0,1:T(4,128)S(1)}, u32[]{:S(2)}, u32[]{:S(2)}) collective-permute-start(f32[3,129,72]{2,0,1:T(4,128)S(1)} %get-tuple-element.13), channel_id=1, source_target_pairs={{1,0},{2,1},{3,2},{4,3},{5,4},{6,5},{7,6},{8,7},{9,8},{10,9},{11,1... | collective-permute-start | bytes 334376 | tf_op jit(solution)/shard_map/ppermute | solution.py:21
  19.7 9.8 %collective-permute-start.3 = (f32[3,129,72]{2,0,1:T(4,128)S(1)}, f32[3,129,72]{2,0,1:T(4,128)S(1)}, u32[]{:S(2)}, u32[]{:S(2)}) collective-permute-start(f32[3,129,72]{2,0,1:T(4,128)S(1)} %get-tuple-element.14), channel_id=1, source_target_pairs={{0,1},{1,2},{2,3},{3,4},{4,5},{5,6},{6,7},{7,8},{8,9},{9,10},{10,1... | collective-permute-start | bytes 334376 | tf_op jit(solution)/shard_map/ppermute | solution.py:21
  66.3 30.1 %copy-start.5 = (f32[1024]{0:T(1024)S(1)}, f32[1024]{0:T(1024)}, u32[]{:S(2)}) copy-start(f32[1024]{0:T(1024)} %param.14) | copy-start | bytes 12292
  92.1 15.5 %all-to-all-start.1 = ((f32[128,1,512]{2,1,0:T(1,128)}), f32[128,1,512]{2,1,0:T(1,128)S(1)}, u32[]{:S(2)}, u32[]{:S(2)}) async-start(f32[128,1,512]{2,1,0:T(1,128)} %broadcast_in_dim.76), calls=%async_computation.1 | async-start | bytes 524288 | tf_op jit(solution)/shard_map/all_to_all | solution.py:112
  108.3 15.0 %copy-start.2 = (f32[64,1024]{1,0:T(8,128)}, f32[64,1024]{1,0:T(8,128)S(1)}, u32[]{:S(2)}) copy-start(f32[64,1024]{1,0:T(8,128)S(1)} %reshape.242) | copy-start | bytes 786436
  108.3 15.0 %copy-start.6 = (f32[64,1024]{1,0:T(8,128)S(1)}, f32[64,1024]{1,0:T(8,128)}, u32[]{:S(2)}) copy-start(f32[64,1024]{1,0:T(8,128)} %param.15) | copy-start | bytes 786436
  108.3 15.0 %copy-start.7 = (f32[1024]{0:T(1024)S(1)}, f32[1024]{0:T(1024)}, u32[]{:S(2)}) copy-start(f32[1024]{0:T(1024)} %param.13) | copy-start | bytes 12292

commit v15 on v11

--- a/solution.py
+++ b/solution.py
@@ -237,7 +237,7 @@
         inside.astype(f32), recharge, halo_rows, halo_cols, logarithmic_conductivity, starting_head, 8
     )
     group_total, well_count = well_cells.shape
-    local_data = jnp.take(hydraulic_head.reshape(member_count, row_count * col_count), well_cells.reshape(-1), axis=1)
+    local_data = jnp.take(hydraulic_head.reshape(member_count, row_count * col_count), well_cells.reshape(-1), axis=1, mode="clip")
     me = lax.axis_index("row") * lax.axis_size("col") + lax.axis_index("col")
     mine = jnp.repeat(well_owner == me, well_count)
     local_data = jnp.where(mine[None, :], local_data, 0.0)

time: 132 us -> 132 us (level)
  transfers between devices with their start and end apart: 5 -> 5, of which waited for: 3 -> 3; matrix products, arithmetic and copies ran while one was open for 6% -> 5% of each run, Pallas kernels for 0% -> 0%
where the time goes in v15:
time: 132 us
  Pallas kernels  29.3 us (22%)
  blocking collectives  24.2 us (18%)
  other arithmetic  16.9 us (13%)
  starting transfers between devices  16.4 us (12%)
  waiting for transfers between devices  16.1 us (12%)
  local copies, waits for them, and re-layouts  14.3 us (11%)
  matrix products  13.4 us (10%)
    all_to_all x1, blocking collectives, broadcast_from_owners(): own_chunk = lax.all_to_all(chunks, axes, 0, 0, tiled=True).sum(axis=0)  24.2 us
    pallas_call x1, Pallas kernels, run_stencil(): pl.pallas_call(stencil_kernel, grid=(blocks,), in_specs=[full2(mask.shape...  21.6 us
    ppermute x4, starting transfers between devices, send(): return lax.ppermute(piece, axis, pairs)  12.1 us
    all_to_all x1, waiting for transfers between devices, broadcast_from_owners(): return lax.all_to_all(spread, axes, 0, 0, tiled=True).reshape(value.shape)  10.7 us
    pallas_call x1, Pallas kernels, run_update(): pl.pallas_call(update_kernel, out_shape=jax.ShapeDtypeStruct(flat.shape,...  7.73 us
    another operation x3, other arithmetic, blending_weights(): factor = jnp.linalg.cholesky(system)  6.52 us
    dot_general x1, matrix products, per_device(): halo_cols = jnp.einsum('kmr,kl->mrl', received, selector, precision=highest)  5.72 us
    another operation x2, other arithmetic, blending_weights(): lax.linalg.triangular_solve(factor, half_solved, left_side=True, lower=Tr...  5.55 us
  transfers between devices with their start and end apart: 5, of which 3 were waited for; matrix products, arithmetic and copies ran while one was open for 5% of the time, Pallas kernels for 0%

profile of v15, /device:TPU:1, one launch (start us, length us, event | category | flops | bytes accessed | tf_op | source)
XLA Modules:
  0.0 131.8 jit_solution(5514634761922411768)
XLA Ops:
  0.6 1.1 slice_convert_fusion.1
  1.7 1.1 fusion.52
  2.8 0.7 slice_bitcast_fusion.1
  3.6 3.3 %collective-permute-start = (f32[3,129,128]{2,0,1:T(4,128)S(1)}, f32[3,129,128]{2,0,1:T(4,128)S(1)}, u32[]{:S(2)}, u32[]{:S(2)}) collective-permute-start(f32[3,129,128]{2,0,1:T(4,128)S(1)} %maximum_bitcast_fusion), channel_id=1, source_target_pairs={{16,0},{32,16},{48,32},{64,48},{80,64},{96,80},{112,96},{17,1},{33... | collective-permute-start | bytes 594440 | tf_op jit(solution)/shard_map/ppermute | solution.py:21
  7.0 3.6 %collective-permute-start.1 = (f32[3,129,128]{2,0,1:T(4,128)S(1)}, f32[3,129,128]{2,0,1:T(4,128)S(1)}, u32[]{:S(2)}, u32[]{:S(2)}) collective-permute-start(f32[3,129,128]{2,0,1:T(4,128)S(1)} %maximum_bitcast_fusion.1), channel_id=1, source_target_pairs={{0,16},{16,32},{32,48},{48,64},{64,80},{80,96},{96,112},{1,17},{17... | collective-permute-start | bytes 594440 | tf_op jit(solution)/shard_map/ppermute | solution.py:21
  10.6 4.1 %fusion.32 = f32[8,64,64]{2,0,1:T(8,128)S(1)} fusion(f32[64,64,128]{2,1,0:T(8,128)} %perm_ref.1, s32[8]{0:T(128)S(1)} %compare_select_fusion.2, pred[8]{0:T(512)(128)(4,1)S(1)} %compare_or_fusion), kind=kOutput, calls=%fused_computation.52 | convolution fusion | flops 50333696 | bytes 2228264 | tf_op jit(solution)/shard_map/dot_general | solution.py:218
  14.7 0.9 fusion.35
  15.7 0.2 convolution_bitcast_fusion
  16.0 0.1 broadcast_in_dim.59
  16.1 0.1 pad.8.clone
  16.2 0.7 and_convert_fusion.mask_ref
  16.9 0.1 pad_maximum_fusion.source_rows_ref.perm_rows_ref.head_rows_ref
  17.0 0.6 fusion
  17.6 0.4 copy.21
  18.0 0.2 pad_maximum_fusion.1
  18.2 0.1 fusion.53
  18.3 1.3 collective-permute-start.2
  19.6 4.0 %collective-permute-start.3 = (f32[3,129,72]{2,0,1:T(4,128)S(1)}, f32[3,129,72]{2,0,1:T(4,128)S(1)}, u32[]{:S(2)}, u32[]{:S(2)}) collective-permute-start(f32[3,129,72]{2,0,1:T(4,128)S(1)} %get-tuple-element.14), channel_id=1, source_target_pairs={{0,1},{1,2},{2,3},{3,4},{4,5},{5,6},{6,7},{7,8},{8,9},{9,10},{10,1... | collective-permute-start | bytes 334376 | tf_op jit(solution)/shard_map/ppermute | solution.py:21
  23.8 0.2 broadcast_in_dim.63
  24.0 3.7 %collective-permute-done.2 = f32[3,129,72]{2,0,1:T(4,128)S(1)} collective-permute-done((f32[3,129,72]{2,0,1:T(4,128)S(1)}, f32[3,129,72]{2,0,1:T(4,128)S(1)}, u32[]{:S(2)}, u32[]{:S(2)}) %collective-permute-start.2) | collective-permute-done | bytes 111488 | tf_op jit(solution)/shard_map/ppermute | solution.py:21
  27.6 1.8 %collective-permute-done.3 = f32[3,129,72]{2,0,1:T(4,128)S(1)} collective-permute-done((f32[3,129,72]{2,0,1:T(4,128)S(1)}, f32[3,129,72]{2,0,1:T(4,128)S(1)}, u32[]{:S(2)}, u32[]{:S(2)}) %collective-permute-start.3) | collective-permute-done | bytes 111488 | tf_op jit(solution)/shard_map/ppermute | solution.py:21
  29.4 5.7 %fusion.2.source_cols_ref.perm_cols_ref.head_cols_ref = f32[129,72,128]{2,1,0:T(8,128)} fusion(f32[3,129,72]{2,0,1:T(4,128)S(1)} %collective-permute-done.3, f32[3,129,72]{2,0,1:T(4,128)S(1)} %collective-permute-done.2, f32[8]{0:T(128)S(1)} %pad.8.clone, s32[8]{0:T(128)S(1)} %compare_select_fusion.2, pred[8]{0:T(512)(128)(4,1)S(1)} %compare_or_fusion), kind=kOutput, calls=%fused_computation.6 | convolution fusion | flops 114281600 | bytes 4978440 | tf_op jit(solution)/shard_map/kmr,kl->mrl/dot_general | solution.py:232
  35.1 21.6 %shard_map.103 = (bf16[64,64,128]{2,1,0:T(8,128)(2,1)}, f32[64,64,128]{2,1,0:T(8,128)}) custom-call(f32[72,256]{1,0:T(8,128)} %and_convert_fusion.mask_ref, f32[64,128]{1,0:T(8,128)} %source_ref.1, f32[129,8,128]{2,1,0:T(8,128)} %copy-done, f32[129,72,128]{2,1,0:T(8,128)} %fusion.2.source_cols_ref.perm_cols_ref.head_cols_ref, f32[64,64,128]{2,1,0:T(8,128)} %perm_ref.1, ...), custom_call_target="tpu_custom_call" | custom-call | flops 94371840 | bytes 7340032 | tf_op jit(solution)/shard_map/pallas_call | solution.py:79
  56.7 3.8 %copy.26 = f32[64,64,128]{0,2,1:T(8,128)} copy(f32[64,64,128]{2,1,0:T(8,128)} %get-tuple-element.6) | data formatting | bytes 4194304 | tf_op jit(solution)/shard_map/reshape | solution.py:240
  60.5 5.0 %gather_fusion = f32[1024,64]{1,0:T(8,128)S(1)} fusion(f32[64,8192]{0,1:T(8,128)} %bitcast.50, s32[1024]{0:T(1024)S(1)} %broadcast_clamp_fusion), kind=kCustom, calls=%fused_computation | custom fusion | bytes 528384 | tf_op jit(solution)/shard_map/jit(_take)/gather | solution.py:240
  65.5 0.2 copy.23
  65.8 0.3 copy.24
  66.1 24.2 %all_to_all.12 = f32[128,1,512]{2,1,0:T(1,128)S(1)} all-to-all(f32[128,1,512]{2,1,0:T(1,128)S(1)} %copy.24), channel_id=1, replica_groups=mesh['row'=8,'col'=16] {'row','col'}, dimensions={0} | all-to-all | bytes 524288 | tf_op jit(solution)/shard_map/all_to_all | solution.py:110
  90.3 0.2 reduce_sum.18
  90.5 0.8 broadcast_in_dim.66
  91.3 4.3 %all-to-all-start.1 = ((f32[128,1,512]{2,1,0:T(1,128)}), f32[128,1,512]{2,1,0:T(1,128)S(1)}, u32[]{:S(2)}, u32[]{:S(2)}) async-start(f32[128,1,512]{2,1,0:T(1,128)} %broadcast_in_dim.66), calls=%async_computation.1 | async-start | bytes 524288 | tf_op jit(solution)/shard_map/all_to_all | solution.py:112
  95.7 0.4 div.58
  96.1 10.7 %all-to-all-done.1 = f32[128,1,512]{2,1,0:T(1,128)S(1)} async-done(((f32[128,1,512]{2,1,0:T(1,128)}), f32[128,1,512]{2,1,0:T(1,128)S(1)}, u32[]{:S(2)}, u32[]{:S(2)}) %all-to-all-start.1) | async-done | bytes 262176 | tf_op jit(solution)/shard_map/all_to_all | solution.py:112
  106.8 0.6 reduce.7
  107.4 0.1 reshape.190
  107.7 0.4 sub.36
  108.1 1.6 %fusion.51 = (f32[128,512]{1,0:T(8,128)S(1)}, f32[128,512]{1,0:T(8,128)S(1)}) fusion(f32[128,1,512]{2,1,0:T(1,128)S(1)} %all-to-all-done.1, f32[128,1,512]{2,1,0:T(1,128)S(1)} %sub.36, f32[128,1,512]{2,1,0:T(1,128)S(1)} %div.58), kind=kLoop, calls=%fused_computation.79 | loop fusion | flops 196608 | bytes 1310720 | tf_op jit(solution)/shard_map/div | solution.py:164
  109.7 0.1 div.60
  109.8 0.1 div.61
  109.9 0.4 fusion.54
  110.4 5.8 %cholesky.17 = f32[64,64]{1,0:T(8,128)S(1)} custom-call(f32[64,64]{1,0:T(8,128)S(1)} %fusion.26), custom_call_target="Cholesky" | custom-call | tf_op jit(solution)/shard_map/jit(cholesky)/cholesky | solution.py:171
  116.3 0.6 compare_reduce_fusion
  116.9 0.7 fusion.20
  117.6 4.9 %custom-call.8 = f32[1,64,64]{1,2,0:T(8,128)S(1)} custom-call(f32[1,64,64]{2,1,0:T(8,128)S(1)} %fusion.20), custom_call_target="InvertDiagBlocksLowerTriangular" | custom-call | tf_op jit(solution)/shard_map/triangular_solve | solution.py:173
  122.5 0.4 fusion.8
  122.9 0.2 fusion.23
  123.2 0.9 fusion.21.mix_t_ref
  124.0 7.7 %shard_map.104 = f32[4096,128]{1,0:T(8,128)} custom-call(f32[64,64]{1,0:T(8,128)} %fusion.21.mix_t_ref, f32[4096,128]{1,0:T(8,128)} %bitcast.49), custom_call_target="tpu_custom_call" | custom-call | flops 67108864 | bytes 4194304 | tf_op jit(solution)/shard_map/pallas_call | solution.py:151
  (45 shorter events, 0.8 us)
Async XLA Ops:
  0.6 14.1 %copy-start.1 = (bf16[64,64,128]{2,1,0:T(8,128)(2,1)S(1)}, bf16[64,64,128]{2,1,0:T(8,128)(2,1)}, u32[]{:S(2)}) copy-start(bf16[64,64,128]{2,1,0:T(8,128)(2,1)} %head_ref.1) | copy-start | bytes 3145732
  3.6 13.3 %collective-permute-start = (f32[3,129,128]{2,0,1:T(4,128)S(1)}, f32[3,129,128]{2,0,1:T(4,128)S(1)}, u32[]{:S(2)}, u32[]{:S(2)}) collective-permute-start(f32[3,129,128]{2,0,1:T(4,128)S(1)} %maximum_bitcast_fusion), channel_id=1, source_target_pairs={{16,0},{32,16},{48,32},{64,48},{80,64},{96,80},{112,96},{17,1},{33... | collective-permute-start | bytes 594440 | tf_op jit(solution)/shard_map/ppermute | solution.py:21
  6.9 8.8 %copy-start.3 = (f32[64,128]{1,0:T(8,128)S(1)}, f32[64,128]{1,0:T(8,128)}, u32[]{:S(2)}) copy-start(f32[64,128]{1,0:T(8,128)} %source_ref.1) | copy-start | bytes 98308
  6.9 9.0 %copy-start.5 = (s32[4,256]{1,0:T(4,128)S(1)}, s32[4,256]{1,0:T(4,128)}, u32[]{:S(2)}) copy-start(s32[4,256]{1,0:T(4,128)} %param.11) | copy-start | bytes 12292
  6.9 9.0 %copy-start.8 = (s32[4]{0:T(128)S(1)}, s32[4]{0:T(128)}, u32[]{:S(2)}) copy-start(s32[4]{0:T(128)} %param.12) | copy-start | bytes 52
  7.0 9.9 %collective-permute-start.1 = (f32[3,129,128]{2,0,1:T(4,128)S(1)}, f32[3,129,128]{2,0,1:T(4,128)S(1)}, u32[]{:S(2)}, u32[]{:S(2)}) collective-permute-start(f32[3,129,128]{2,0,1:T(4,128)S(1)} %maximum_bitcast_fusion.1), channel_id=1, source_target_pairs={{0,16},{16,32},{32,48},{48,64},{64,80},{80,96},{96,112},{1,17},{17... | collective-permute-start | bytes 594440 | tf_op jit(solution)/shard_map/ppermute | solution.py:21
  17.0 6.9 %copy-start = (f32[129,8,128]{2,1,0:T(8,128)}, f32[129,8,128]{2,1,0:T(8,128)S(1)}, u32[]{:S(2)}) copy-start(f32[129,8,128]{2,1,0:T(8,128)S(1)} %pad_maximum_fusion.source_rows_ref.perm_rows_ref.head_rows_ref) | copy-start | bytes 1585156
  18.3 9.3 %collective-permute-start.2 = (f32[3,129,72]{2,0,1:T(4,128)S(1)}, f32[3,129,72]{2,0,1:T(4,128)S(1)}, u32[]{:S(2)}, u32[]{:S(2)}) collective-permute-start(f32[3,129,72]{2,0,1:T(4,128)S(1)} %get-tuple-element.13), channel_id=1, source_target_pairs={{1,0},{2,1},{3,2},{4,3},{5,4},{6,5},{7,6},{8,7},{9,8},{10,9},{11,1... | collective-permute-start | bytes 334376 | tf_op jit(solution)/shard_map/ppermute | solution.py:21
  19.6 9.8 %collective-permute-start.3 = (f32[3,129,72]{2,0,1:T(4,128)S(1)}, f32[3,129,72]{2,0,1:T(4,128)S(1)}, u32[]{:S(2)}, u32[]{:S(2)}) collective-permute-start(f32[3,129,72]{2,0,1:T(4,128)S(1)} %get-tuple-element.14), channel_id=1, source_target_pairs={{0,1},{1,2},{2,3},{3,4},{4,5},{5,6},{6,7},{7,8},{8,9},{9,10},{10,1... | collective-permute-start | bytes 334376 | tf_op jit(solution)/shard_map/ppermute | solution.py:21
  65.5 30.1 %copy-start.4 = (f32[1024]{0:T(1024)S(1)}, f32[1024]{0:T(1024)}, u32[]{:S(2)}) copy-start(f32[1024]{0:T(1024)} %param.14) | copy-start | bytes 12292
  91.3 15.5 %all-to-all-start.1 = ((f32[128,1,512]{2,1,0:T(1,128)}), f32[128,1,512]{2,1,0:T(1,128)S(1)}, u32[]{:S(2)}, u32[]{:S(2)}) async-start(f32[128,1,512]{2,1,0:T(1,128)} %broadcast_in_dim.66), calls=%async_computation.1 | async-start | bytes 524288 | tf_op jit(solution)/shard_map/all_to_all | solution.py:112
  107.5 15.0 %copy-start.2 = (f32[64,1024]{1,0:T(8,128)}, f32[64,1024]{1,0:T(8,128)S(1)}, u32[]{:S(2)}) copy-start(f32[64,1024]{1,0:T(8,128)S(1)} %reshape.190) | copy-start | bytes 786436
  107.5 15.0 %copy-start.6 = (f32[64,1024]{1,0:T(8,128)S(1)}, f32[64,1024]{1,0:T(8,128)}, u32[]{:S(2)}) copy-start(f32[64,1024]{1,0:T(8,128)} %param.15) | copy-start | bytes 786436
  107.6 15.0 %copy-start.7 = (f32[1024]{0:T(1024)S(1)}, f32[1024]{0:T(1024)}, u32[]{:S(2)}) copy-start(f32[1024]{0:T(1024)} %param.13) | copy-start | bytes 12292
